TPU v7x, 256 devices: a whole 4x4x8 slice. The times are simulated.
256 devices in a mesh: adapter: 32 (over z, y), tensor: 8 (over x, core).
Axes of the slice: x: 4, y: 4, z: 8, core: 2. Of those that a mesh axis runs over, the one named last changes fastest.
Arguments:
- hidden: bfloat16 [3072, 2, 8192], P('adapter'), may hold values from -6 to 6
- input_norm_gain: bfloat16 [8192], replicated, may hold values from 0.25 to 1.75
- key_value_weight: bfloat16 [8192, 2, 1024], P(None, None, 'tensor'), may hold values from -0.0625 to 0.0625
- adapter_down_weight: bfloat16 [128, 8192, 128], P('adapter', 'tensor'), may hold values from -0.0625 to 0.0625
- adapter_up_weight: bfloat16 [128, 2, 64, 1024], P('adapter', None, None, 'tensor'), may hold values from -0.375 to 0.375
- request_adapter: int32 [3072], P('adapter'), may hold values from 0 to 127, as said below
- queries: bfloat16 [3072, 2, 8192], P('adapter', None, 'tensor'), may hold values from -100 to 100
- cached_key_rows: bfloat16 [3072, 64, 1024], P('adapter', None, 'tensor'), may hold values from -5 to 5
- cached_value_rows: bfloat16 [3072, 64, 1024], P('adapter', None, 'tensor'), may hold values from -6 to 6
- cached_length: int32 [3072], P('adapter'), may hold values from 2 to 64, as said below
Outputs:
- new_keys: bfloat16 [3072, 2, 1024], P('adapter', None, 'tensor')
- new_values: bfloat16 [3072, 2, 1024], P('adapter', None, 'tensor')
- attended: bfloat16 [3072, 2, 8192], P('adapter', None, 'tensor')
Inputs may be any that keep to these rules, and one draw needn't show every extreme that they name: `request_adapter`: adapter a is held by adapter index a // 4. Of the requests on one adapter index at most 6 name adapters held by one adapter index, and in every draw one adapter index is named by exactly 6 requests of every adapter index. `cached_length`: some request has exactly 64 cached tokens.
All inputs are finite; a program needn't handle non-finite values.
Results may differ from a plain program's by a relative error of at most 0.0055.
Values may be sent and summed in bfloat16 or wider, within the bound.
No kernel may reach another device: no remote copies, remote signals or barrier semaphores. Data moves between devices by JAX's collectives and lax.ppermute only.
A program may use at most 128 MiB of HBM per device.

v0:
```python
import jax
import jax.numpy as jnp
from jax import lax
from jax.sharding import PartitionSpec as P

HEAD_DIM = 128


epsilon = 1e-05
rope_base = 500000.0


def rotate_keys(key_vecs, positions):
    head_size = key_vecs.shape[-1]
    half_size = head_size // 2
    inverse = rope_base ** (-(jnp.arange(half_size, dtype=jnp.float32) * 2.0 / head_size))
    angles = positions[..., None] * inverse
    cosine = jnp.cos(angles)
    sine_part = jnp.sin(angles)
    first_half = key_vecs[..., :half_size]
    second = key_vecs[..., half_size:]
    return jnp.concatenate(
        [first_half * cosine - second * sine_part, second * cosine + first_half * sine_part],
        axis=-1,
    )


def normalize(hidden, input_norm_gain):
    values = hidden.astype(jnp.float32)
    meansq = jnp.mean(values * values, axis=-1, keepdims=True)
    return (values * lax.rsqrt(meansq + epsilon) * input_norm_gain.astype(jnp.float32)).astype(
        jnp.bfloat16
    )


def down_weight_rows(input_rows, adapter_down_weight, adapter_selector):
    projected_output = jnp.einsum(
        "euz,nzs->euns", input_rows, adapter_down_weight, preferred_element_type=jnp.float32
    )
    return jnp.sum(projected_output * adapter_selector[..., None], axis=2)


def up_weight_rows(rank_hidden, adapter_up_weight, adapter_selector):
    rank_width = adapter_up_weight.shape[2]
    masked_scores = rank_hidden[:, :, None, :] * adapter_selector[..., None]
    key_part = jnp.einsum(
        "gled,edb->glb",
        masked_scores[..., :rank_width],
        adapter_up_weight[:, 0],
        preferred_element_type=jnp.float32,
    )
    value_part = jnp.einsum(
        "gled,edb->glb",
        masked_scores[..., rank_width:],
        adapter_up_weight[:, 1],
        preferred_element_type=jnp.float32,
    )
    return jnp.stack([key_part, value_part], axis=2)


def attend(
    queries, cached_key_rows, cached_value_rows, cached_length, new_keys, new_values, head_size
):
    row_total, token_total, query_width = queries.shape
    context = cached_key_rows.shape[1]
    kv_local = cached_key_rows.shape[2] // head_size
    group_size = query_width // (kv_local * head_size)
    score_scale = float(head_size) ** (-0.5)
    query_vecs = queries.reshape(row_total, token_total, kv_local, group_size, head_size)
    cache_vecs = cached_key_rows.reshape(row_total, context, kv_local, head_size)
    fresh_vecs = new_keys.reshape(row_total, token_total, kv_local, head_size)
    cache_scores = (
        jnp.einsum("rthgd,rjhd->rthgj", query_vecs, cache_vecs, preferred_element_type=jnp.float32)
        * score_scale
    )
    slot_live = jnp.arange(context, dtype=jnp.int32)[None, :] < cached_length[:, None]
    cache_scores = jnp.where(slot_live[:, None, None, None, :], cache_scores, -1e30)
    fresh_scores = (
        jnp.einsum("rthgd,rshd->rthgs", query_vecs, fresh_vecs, preferred_element_type=jnp.float32)
        * score_scale
    )
    causal = (
        jnp.arange(token_total, dtype=jnp.int32)[:, None]
        >= jnp.arange(token_total, dtype=jnp.int32)[None, :]
    )
    fresh_scores = jnp.where(causal[None, :, None, None, :], fresh_scores, -1e30)
    top_score = jnp.maximum(jnp.max(cache_scores, axis=-1), jnp.max(fresh_scores, axis=-1))[
        ..., None
    ]
    cache_weights = jnp.exp(cache_scores - top_score)
    fresh_weights = jnp.exp(fresh_scores - top_score)
    total_weight = jnp.sum(cache_weights, axis=-1, keepdims=True) + jnp.sum(
        fresh_weights, axis=-1, keepdims=True
    )
    cache_probs = (cache_weights / total_weight).astype(jnp.bfloat16)
    fresh_probs = (fresh_weights / total_weight).astype(jnp.bfloat16)
    cache_vals = cached_value_rows.reshape(row_total, context, kv_local, head_size)
    fresh_vals = new_values.reshape(row_total, token_total, kv_local, head_size)
    mixed_out = jnp.einsum(
        "rthgj,rjhd->rthgd", cache_probs, cache_vals, preferred_element_type=jnp.float32
    )
    mixed_out = mixed_out + jnp.einsum(
        "rthgs,rshd->rthgd", fresh_probs, fresh_vals, preferred_element_type=jnp.float32
    )
    return mixed_out.reshape(row_total, token_total, query_width).astype(jnp.bfloat16)


def body(
    hidden,
    input_norm_gain,
    key_value_weight,
    adapter_down_weight,
    adapter_up_weight,
    request_adapter,
    queries,
    cached_key_rows,
    cached_value_rows,
    cached_length,
):
    row_count, token_count, model_width = hidden.shape
    feature_total = adapter_down_weight.shape[1]
    adapter_number = adapter_down_weight.shape[0]
    column_count = key_value_weight.shape[2]
    normed_input = normalize(hidden, input_norm_gain)
    base_proj = jnp.dot(
        normed_input.reshape(row_count * token_count, model_width),
        key_value_weight.reshape(model_width, 2 * column_count),
        preferred_element_type=jnp.float32,
    )
    base_proj = base_proj.reshape(row_count, token_count, 2, column_count)
    feature_start = lax.axis_index("tensor") * feature_total
    own_features = lax.dynamic_slice_in_dim(normed_input, feature_start, feature_total, 2)
    adapter_slots = jnp.arange(adapter_number, dtype=jnp.int32)
    every_row, all_ids = (
        lax.all_gather(own_features, "adapter", axis=0, tiled=True),
        lax.all_gather(request_adapter, "adapter", axis=0, tiled=True),
    )
    local_ids = all_ids - lax.axis_index("adapter") * adapter_number
    owned = (local_ids[:, None] == adapter_slots[None, :]).astype(jnp.float32)
    adapter_selector = jnp.broadcast_to(
        owned[:, None, :], (all_ids.shape[0], token_count, adapter_number)
    )
    partial_rank_sum = down_weight_rows(every_row, adapter_down_weight, adapter_selector)
    rank_hidden = lax.psum(partial_rank_sum, "tensor").astype(jnp.bfloat16)
    rank_selector = adapter_selector.astype(jnp.bfloat16)
    adapter_update = lax.psum_scatter(
        up_weight_rows(rank_hidden, adapter_up_weight, rank_selector),
        "adapter",
        scatter_dimension=0,
        tiled=True,
    )
    projected_output = base_proj + adapter_update
    positions = (cached_length[:, None] + jnp.arange(token_count, dtype=jnp.int32)[None, :]).astype(
        jnp.float32
    )
    kv_local = column_count // HEAD_DIM
    key_vecs = rotate_keys(
        projected_output[:, :, 0].reshape(row_count, token_count, kv_local, HEAD_DIM),
        positions[:, :, None],
    )
    new_keys = key_vecs.reshape(row_count, token_count, column_count).astype(jnp.bfloat16)
    new_values = projected_output[:, :, 1].astype(jnp.bfloat16)
    attended = attend(
        queries, cached_key_rows, cached_value_rows, cached_length, new_keys, new_values, HEAD_DIM
    )
    return (new_keys, new_values, attended)


def solution(mesh):
    in_specs = (
        P("adapter", None, None),
        P(),
        P(None, None, "tensor"),
        P("adapter", "tensor", None),
        P("adapter", None, None, "tensor"),
        P("adapter"),
        P("adapter", None, "tensor"),
        P("adapter", None, "tensor"),
        P("adapter", None, "tensor"),
        P("adapter"),
    )
    out_specs = (
        P("adapter", None, "tensor"),
        P("adapter", None, "tensor"),
        P("adapter", None, "tensor"),
    )
    return jax.shard_map(body, mesh=mesh, in_specs=in_specs, out_specs=out_specs, check_vma=False)
```

profile of v0, /device:TPU:6, one launch (start us, length us, event | category | flops | bytes accessed | tf_op | source)
XLA Modules:
  0.0 460.4 jit_solution(8272533959495657048)
XLA Ops:
  7.2 0.0 copy-start
  7.2 0.0 all-gather.2.cloned.1.call-start
  7.2 0.8 convert_element_type.62
  8.1 5.2 %fusion.4 = f32[96,2]{0,1:T(2,128)S(1)} fusion(bf16[96,2,8192]{2,1,0:T(2,128)(2,1)} %param.10), kind=kLoop, calls=%fused_computation.5 | loop fusion | flops 4718400 | bytes 3146496 | tf_op jit(solution)/shard_map/reduce_sum | solution.py:30
  13.3 0.0 copy-start.5
  13.3 6.4 %fusion.6 = bf16[96,2,8192]{2,0,1:T(8,128)(2,1)} fusion(f32[8192]{0:T(1024)S(1)} %convert_element_type.62, f32[96,2]{0,1:T(2,128)S(1)} %add_rsqrt_fusion, bf16[96,2,8192]{2,1,0:T(2,128)(2,1)} %param.10), kind=kLoop, calls=%fused_computation.7 | loop fusion | flops 6291456 | bytes 6324992 | tf_op jit(solution)/shard_map/convert_element_type | solution.py:31
  19.8 1.8 constant_dynamic-slice_fusion.1
  21.5 0.0 all-gather.2.cloned.1.call-update
  21.5 0.0 all-reduce.5.cloned.1.call-start
  21.6 0.6 fusion.70
  22.9 0.3 dynamic-update-slice
  23.2 148.3 %all-reduce = s32[3072]{0:T(1024)S(1)} all-reduce(s32[3072]{0:T(1024)S(1)} %dynamic-update-slice), channel_id=1, replica_groups=mesh['adapter'=32,'tensor'=8] {'adapter'}, use_global_device_ids=true, to_apply=%add | all-reduce | flops 3072 | bytes 24576
  171.5 0.0 all-gather.2.cloned.1.call-done
  171.6 11.6 %multiply_reduce_fusion = f32[3072,2,128]{2,0,1:T(8,128)} fusion(bf16[3072,2,1024]{2,0,1:T(8,128)(2,1)} %all-gather.2.cloned.1.call-done, f32[3072,4]{0,1:T(4,128)S(1)} %get-tuple-element.17, bf16[4,1024,128]{2,1,0:T(8,128)(2,1)S(1)} %copy-done.5), kind=kOutput, calls=%fused_computation.2 | convolution fusion | flops 6447955968 | bytes 16826368 | tf_op jit(solution)/shard_map/euz,nzs->euns/dot_general | solution.py:37
  183.1 51.6 %all-reduce.6 = bf16[3072,2,128]{2,0,1:T(8,128)(2,1)} all-reduce(f32[3072,2,128]{2,0,1:T(8,128)} %multiply_reduce_fusion), channel_id=1, replica_groups=mesh['adapter'=32,'tensor'=8] {'tensor'}, use_global_device_ids=true, to_apply=%region_2.0 | all-reduce | flops 786432 | bytes 4718592 | tf_op jit(solution)/shard_map/psum | solution.py:144
  234.7 1.7 copy.58
  236.5 0.5 broadcast_multiply_fusion
  236.9 0.4 copy-done.2
  237.4 1.0 convolution_bitcast_fusion
  238.4 1.0 convolution_bitcast_fusion.1
  239.4 0.5 pad_maximum_fusion
  239.9 17.8 %copy.61 = f32[3072,2,2,128]{3,2,1,0:T(2,128)} copy(f32[3072,2,2,128]{3,0,1,2:T(8,128)S(1)} %pad_maximum_fusion) | data formatting | bytes 12582912 | tf_op jit(solution)/shard_map/stack | solution.py:58
  257.8 0.0 all-reduce.5.cloned.1.call-update
  257.8 4.7 %copy.91 = bf16[1024,8,2,128]{3,1,2,0:T(8,128)(2,1)} copy(bf16[1024,8,2,128]{3,2,1,0:T(2,128)(2,1)} %bitcast.160) | data formatting | bytes 8388608
  262.5 6.6 %copy.57 = bf16[256,8192]{1,0:T(8,128)(2,1)} copy(bf16[256,8192]{0,1:T(8,128)(2,1)} %bitcast.159) | data formatting | bytes 8388608 | tf_op jit(solution)/shard_map/dot_general | solution.py:125
  269.1 0.3 reshape.193
  270.1 0.1 iota_compare_fusion
  270.1 2.5 fusion.71
  272.6 167.5 %all-reduce.5.cloned.1.call-done = f32[3072,2,2,128]{3,2,1,0:T(2,128)} async-done(((f32[3072,2,2,128]{3,2,1,0:T(2,128)}), f32[3072,2,2,128]{3,2,1,0:T(2,128)}) %all-reduce.5.cloned.1.call-update) | async-done | bytes 6291472
  440.1 0.9 constant_dynamic-slice_fusion
  441.0 0.1 copy.63
  441.2 4.4 fusion.39
  445.6 0.3 fusion.80
  445.9 0.3 fusion.57
  446.3 0.3 fusion.79
  446.6 0.3 fusion.78
  447.0 0.7 copy.70
  447.7 0.7 copy.71
  448.4 0.1 copy.80
  448.6 0.1 copy.78
  448.7 1.9 fusion.72
  450.6 0.1 max.9
  450.6 0.6 fusion.45
  451.3 0.4 fusion.48
  451.6 0.1 add.62
  451.7 0.4 fusion.49
  452.1 0.6 fusion.36
  452.8 0.8 convert_element_type.76
  (21 shorter events, 0.1 us)
Async XLA Ops:
  7.2 444.9 %copy-start = (bf16[96,64,128]{2,1,0:T(8,128)(2,1)S(1)}, bf16[96,64,128]{2,1,0:T(8,128)(2,1)}, u32[]{:S(2)}) copy-start(bf16[96,64,128]{2,1,0:T(8,128)(2,1)} %param.18) | copy-start | bytes 4718596
  7.2 164.4 %all-gather.2.cloned.1.call-start = ((), (), s32[]{:S(2)}) async-start(), calls=%async_computation | async-start | bytes 12976128 | tf_op jit(solution)/shard_map/all_gather | solution.py:135
  13.3 8.3 %copy-start.3 = (u32[256]{0:T(256)S(1)}, u32[256]{0:T(256)}, u32[]{:S(2)}) copy-start(u32[256]{0:T(256)} %constant.42) | copy-start | bytes 3076
  13.3 9.6 %copy-start.6 = (s32[96]{0:T(128)S(1)}, s32[96]{0:T(128)}, u32[]{:S(2)}) copy-start(s32[96]{0:T(128)} %param.15) | copy-start | bytes 1156
  13.3 158.2 %copy-start.5 = (bf16[4,1024,128]{2,1,0:T(8,128)(2,1)S(1)}, bf16[4,1024,128]{2,1,0:T(8,128)(2,1)}, u32[]{:S(2)}) copy-start(bf16[4,1024,128]{2,1,0:T(8,128)(2,1)} %param.13) | copy-start | bytes 3145732
  21.5 418.5 %all-reduce.5.cloned.1.call-start = ((), (), s32[]{:S(2)}) async-start(), calls=%async_computation.1 | async-start | bytes 12582912
  236.5 0.9 copy-start.2
  262.4 6.7 %copy-start.1 = (bf16[96,2,1024]{2,1,0:T(2,128)(2,1)S(1)}, bf16[96,2,1024]{2,1,0:T(2,128)(2,1)}, u32[]{:S(2)}) copy-start(bf16[96,2,1024]{2,1,0:T(2,128)(2,1)} %param.16) | copy-start | bytes 1179652
  262.5 7.6 %copy-start.4 = (s32[96]{0:T(128)S(1)}, s32[96]{0:T(128)}, u32[]{:S(2)}) copy-start(s32[96]{0:T(128)} %param.19) | copy-start | bytes 1156
Sparse Core Ops, SparseCore 0:
  21.7 122.9 all-gather.1
  257.9 182.1 all-reduce.4
where the time goes:
time: 461 us; the launch traced here: 460 us
  blocking collectives  200 us (43%)
  waiting for transfers between devices  168 us (36%)
  local copies, waits for them, and re-layouts  37.8 us (8%)
  matrix products  23.5 us (5%)
  other arithmetic  16 us (3%)
  between operations  15.6 us (3%)
    unnamed x3, waiting for transfers between devices  168 us
    unnamed x1, blocking collectives  148 us
    psum x1, blocking collectives, body(): rank_hidden = lax.psum(partial_rank_sum, 'tensor').astype(jnp.bfloat16)  51.6 us
    another operation x1, local copies, waits for them, and re-layouts, up_weight_rows(): return jnp.stack([key_part, value_part], axis=2)  17.8 us
    dot_general x1, matrix products, down_weight_rows(): jnp.einsum('euz,nzs->euns', input_rows, adapter_down_weight, preferred_el...  11.6 us
  transfers between devices with their start and end apart: 2, of which 1 were waited for; matrix products, arithmetic and copies ran while one was open for 3% of the time, Pallas kernels for 0%

commit v1 on v0

--- a/solution.py
+++ b/solution.py
@@ -4,6 +4,7 @@
 from jax.sharding import PartitionSpec as P
 
 HEAD_DIM = 128
+SLOT_CAPACITY = 6
 
 
 epsilon = 1e-05
@@ -31,31 +32,6 @@
     return (values * lax.rsqrt(meansq + epsilon) * input_norm_gain.astype(jnp.float32)).astype(
         jnp.bfloat16
     )
-
-
-def down_weight_rows(input_rows, adapter_down_weight, adapter_selector):
-    projected_output = jnp.einsum(
-        "euz,nzs->euns", input_rows, adapter_down_weight, preferred_element_type=jnp.float32
-    )
-    return jnp.sum(projected_output * adapter_selector[..., None], axis=2)
-
-
-def up_weight_rows(rank_hidden, adapter_up_weight, adapter_selector):
-    rank_width = adapter_up_weight.shape[2]
-    masked_scores = rank_hidden[:, :, None, :] * adapter_selector[..., None]
-    key_part = jnp.einsum(
-        "gled,edb->glb",
-        masked_scores[..., :rank_width],
-        adapter_up_weight[:, 0],
-        preferred_element_type=jnp.float32,
-    )
-    value_part = jnp.einsum(
-        "gled,edb->glb",
-        masked_scores[..., rank_width:],
-        adapter_up_weight[:, 1],
-        preferred_element_type=jnp.float32,
-    )
-    return jnp.stack([key_part, value_part], axis=2)
 
 
 def attend(
@@ -120,7 +96,13 @@
     row_count, token_count, model_width = hidden.shape
     feature_total = adapter_down_weight.shape[1]
     adapter_number = adapter_down_weight.shape[0]
+    rank_total = adapter_down_weight.shape[2]
+    rank_width = adapter_up_weight.shape[2]
     column_count = key_value_weight.shape[2]
+    owner_count = lax.axis_size("adapter")
+    cap = SLOT_CAPACITY
+    slot_total = owner_count * cap
+
     normed_input = normalize(hidden, input_norm_gain)
     base_proj = jnp.dot(
         normed_input.reshape(row_count * token_count, model_width),
@@ -128,27 +110,70 @@
         preferred_element_type=jnp.float32,
     )
     base_proj = base_proj.reshape(row_count, token_count, 2, column_count)
+
+    owner_of = request_adapter // adapter_number
+    local_adapter = request_adapter - owner_of * adapter_number
+    row_ids = jnp.arange(row_count, dtype=jnp.int32)
+    same_owner = owner_of[:, None] == owner_of[None, :]
+    earlier = row_ids[None, :] < row_ids[:, None]
+    rank_in_owner = jnp.sum((same_owner & earlier).astype(jnp.int32), axis=1)
+    slot_of = owner_of * cap + rank_in_owner
+    pick = (slot_of[None, :] == jnp.arange(slot_total, dtype=jnp.int32)[:, None]).astype(
+        jnp.bfloat16
+    )
+
     feature_start = lax.axis_index("tensor") * feature_total
     own_features = lax.dynamic_slice_in_dim(normed_input, feature_start, feature_total, 2)
-    adapter_slots = jnp.arange(adapter_number, dtype=jnp.int32)
-    every_row, all_ids = (
-        lax.all_gather(own_features, "adapter", axis=0, tiled=True),
-        lax.all_gather(request_adapter, "adapter", axis=0, tiled=True),
-    )
-    local_ids = all_ids - lax.axis_index("adapter") * adapter_number
-    owned = (local_ids[:, None] == adapter_slots[None, :]).astype(jnp.float32)
-    adapter_selector = jnp.broadcast_to(
-        owned[:, None, :], (all_ids.shape[0], token_count, adapter_number)
-    )
-    partial_rank_sum = down_weight_rows(every_row, adapter_down_weight, adapter_selector)
-    rank_hidden = lax.psum(partial_rank_sum, "tensor").astype(jnp.bfloat16)
-    rank_selector = adapter_selector.astype(jnp.bfloat16)
-    adapter_update = lax.psum_scatter(
-        up_weight_rows(rank_hidden, adapter_up_weight, rank_selector),
-        "adapter",
-        scatter_dimension=0,
-        tiled=True,
-    )
+    packed = jnp.dot(
+        pick,
+        own_features.reshape(row_count, token_count * feature_total),
+        preferred_element_type=jnp.float32,
+    ).astype(jnp.bfloat16)
+    packed = packed.reshape(owner_count, cap * token_count, feature_total)
+    slot_adapter = jnp.dot(
+        pick, local_adapter.astype(jnp.bfloat16), preferred_element_type=jnp.float32
+    ).astype(jnp.bfloat16)
+    id_row = jnp.zeros((owner_count, 1, feature_total), jnp.bfloat16)
+    id_row = lax.dynamic_update_slice(
+        id_row, slot_adapter.reshape(owner_count, 1, cap), (0, 0, 0)
+    )
+    send = jnp.concatenate([packed, id_row], axis=1)
+    recv = lax.all_to_all(send, "adapter", 0, 0, tiled=True)
+
+    got_rows = recv[:, : cap * token_count].reshape(slot_total, token_count, feature_total)
+    got_adapter = recv[:, cap * token_count, :cap].reshape(slot_total).astype(jnp.int32)
+    selector = (
+        got_adapter[:, None] == jnp.arange(adapter_number, dtype=jnp.int32)[None, :]
+    ).astype(jnp.float32)
+
+    down_all = jnp.einsum(
+        "euz,nzs->euns", got_rows, adapter_down_weight, preferred_element_type=jnp.float32
+    )
+    partial_rank = jnp.sum(down_all * selector[:, None, :, None], axis=2)
+    rank_hidden = lax.psum(partial_rank, "tensor").astype(jnp.bfloat16)
+
+    rank_selector = selector.astype(jnp.bfloat16)
+    masked = rank_hidden[:, :, None, :] * rank_selector[:, None, :, None]
+    key_part = jnp.einsum(
+        "gled,edb->glb",
+        masked[..., :rank_width],
+        adapter_up_weight[:, 0],
+        preferred_element_type=jnp.float32,
+    )
+    value_part = jnp.einsum(
+        "gled,edb->glb",
+        masked[..., rank_width:],
+        adapter_up_weight[:, 1],
+        preferred_element_type=jnp.float32,
+    )
+    delta_slots = jnp.stack([key_part, value_part], axis=2)
+    delta_send = delta_slots.reshape(owner_count, cap * token_count * 2, column_count)
+    delta_recv = lax.all_to_all(delta_send, "adapter", 0, 0, tiled=True)
+    delta_rows = delta_recv.reshape(slot_total, token_count * 2 * column_count)
+    adapter_update = jnp.take(delta_rows, slot_of, axis=0).reshape(
+        row_count, token_count, 2, column_count
+    )
+
     projected_output = base_proj + adapter_update
     positions = (cached_length[:, None] + jnp.arange(token_count, dtype=jnp.int32)[None, :]).astype(
         jnp.float32

time: 461 us -> 130 us (0.28)
  the two profiles are of different devices: /device:TPU:6 before, /device:TPU:8 now
where the time goes in v1:
time: 130 us; the launch traced here: 129 us
  waiting for transfers between devices  28 us (22%)
  blocking collectives  25.8 us (20%)
  other arithmetic  21 us (16%)
  local copies, waits for them, and re-layouts  19.4 us (15%)
  starting transfers between devices  18.1 us (14%)
  matrix products  16.1 us (12%)
    all_to_all x1, waiting for transfers between devices, body(): recv = lax.all_to_all(send, 'adapter', 0, 0, tiled=True)  28 us
    psum x1, blocking collectives, body(): rank_hidden = lax.psum(partial_rank, 'tensor').astype(jnp.bfloat16)  25.8 us
    all_to_all x1, starting transfers between devices, body(): recv = lax.all_to_all(send, 'adapter', 0, 0, tiled=True)  11.7 us
    convert_element_type x1, other arithmetic, normalize(): (values * lax.rsqrt(meansq + epsilon) * input_norm_gain.astype(jnp.float3...  9.86 us
    dot_general x1, matrix products, body(): jnp.dot(normed_input.reshape(row_count * token_count, model_width), key_v...  7.31 us
    dot_general x1, local copies, waits for them, and re-layouts, body(): jnp.dot(normed_input.reshape(row_count * token_count, model_width), key_v...  6.42 us
    all_to_all x1, starting transfers between devices, body(): delta_recv = lax.all_to_all(delta_send, 'adapter', 0, 0, tiled=True)  6.35 us
    unnamed x20, local copies, waits for them, and re-layouts  6.29 us
  transfers between devices with their start and end apart: 2, of which 1 were waited for; matrix products, arithmetic and copies ran while one was open for 12% of the time, Pallas kernels for 0%

profile of v1, /device:TPU:8, one launch (start us, length us, event | category | flops | bytes accessed | tf_op | source)
XLA Modules:
  0.0 129.5 jit_solution(16451189336925691821)
XLA Ops:
  0.7 0.8 convert_element_type.91
  1.5 5.2 %fusion = f32[96,2]{1,0:T(8,128)S(1)} fusion(bf16[96,2,8192]{2,1,0:T(2,128)(2,1)} %param.10), kind=kLoop, calls=%fused_computation.3 | loop fusion | flops 4718400 | bytes 3146496 | tf_op jit(solution)/shard_map/reduce_sum | solution.py:31
  6.8 0.2 convert_reduce_fusion
  6.9 0.5 compare_and_fusion
  7.5 0.1 fusion.53
  7.6 0.1 reshape.289
  7.8 9.9 %fusion.2 = bf16[96,2,8192]{2,1,0:T(2,128)(2,1)} fusion(bf16[96,2,8192]{2,1,0:T(2,128)(2,1)} %param.10, f32[8192]{0:T(1024)S(1)} %convert_element_type.91, f32[96,2]{1,0:T(8,128)S(1)} %add_rsqrt_fusion), kind=kLoop, calls=%fused_computation.5 | loop fusion | flops 6291456 | bytes 6324992 | tf_op jit(solution)/shard_map/convert_element_type | solution.py:32
  17.6 1.3 constant_dynamic-slice_fusion
  18.9 0.1 copy.136
  19.0 0.4 convolution_convert_fusion
  19.4 0.4 reshape.257
  19.7 1.2 fusion.41
  20.9 11.7 %all-to-all-start = ((bf16[32,13,1024]{2,1,0:T(8,128)(2,1)}), bf16[32,13,1024]{2,1,0:T(8,128)(2,1)S(1)}, u32[]{:S(2)}, u32[]{:S(2)}) async-start(bf16[32,13,1024]{2,1,0:T(8,128)(2,1)} %fusion.41), calls=%async_computation | async-start | bytes 2097152 | tf_op jit(solution)/shard_map/all_to_all | solution.py:141
  32.7 28.0 %all-to-all-done = bf16[32,13,1024]{2,1,0:T(8,128)(2,1)S(1)} async-done(((bf16[32,13,1024]{2,1,0:T(8,128)(2,1)}), bf16[32,13,1024]{2,1,0:T(8,128)(2,1)S(1)}, u32[]{:S(2)}, u32[]{:S(2)}) %all-to-all-start) | async-done | bytes 852000 | tf_op jit(solution)/shard_map/all_to_all | solution.py:141
  60.7 0.1 fusion.73
  60.7 0.1 reshape.265
  60.9 0.6 reshape.259
  61.5 1.8 %fusion.26 = f32[192,2,128]{2,0,1:T(8,128)S(1)} fusion(bf16[4,1024,128]{2,1,0:T(8,128)(2,1)} %param.13, bf16[192,2,1024,1]{2,1,0,3:T(2,128)(2,1)S(1)} %bitcast.166, f32[192,4]{0,1:T(4,128)S(1)} %get-tuple-element.25), kind=kOutput, calls=%fused_computation.23 | convolution fusion | flops 402997248 | bytes 2034688 | tf_op jit(solution)/shard_map/euz,nzs->euns/dot_general | solution.py:149
  63.3 25.8 %all-reduce.2 = bf16[192,2,128]{2,0,1:T(8,128)(2,1)S(1)} all-reduce(f32[192,2,128]{2,0,1:T(8,128)S(1)} %fusion.26), channel_id=1, replica_groups=mesh['adapter'=32,'tensor'=8] {'tensor'}, use_global_device_ids=true, to_apply=%region_3.4 | all-reduce | flops 49152 | bytes 294912 | tf_op jit(solution)/shard_map/psum | solution.py:153
  89.1 0.1 copy.104
  89.3 0.2 convolution_bitcast_fusion
  89.5 0.2 convolution_bitcast_fusion.1
  89.8 1.1 copy.107
  90.9 6.4 %all-to-all-start.1 = ((f32[32,24,128]{2,1,0:T(8,128)}), f32[32,24,128]{2,1,0:T(8,128)S(1)}, u32[]{:S(2)}, u32[]{:S(2)}) async-start(f32[32,24,128]{2,1,0:T(8,128)} %bitcast.19), calls=%async_computation.1 | async-start | bytes 786432 | tf_op jit(solution)/shard_map/all_to_all | solution.py:171
  97.2 0.5 iota_compare_fusion.7
  97.8 4.7 %copy.147 = bf16[1024,8,2,128]{3,1,2,0:T(8,128)(2,1)} copy(bf16[1024,8,2,128]{3,2,1,0:T(2,128)(2,1)} %bitcast.162) | data formatting | bytes 8388608
  102.5 6.4 %copy.100 = bf16[256,8192]{1,0:T(8,128)(2,1)} copy(bf16[256,8192]{0,1:T(8,128)(2,1)} %bitcast.160) | data formatting | bytes 8388608 | tf_op jit(solution)/shard_map/dot_general | solution.py:107
  108.9 0.3 reshape.262
  109.2 0.1 iota_compare_fusion.4
  109.3 3.1 %fusion.80 = (f32[96,2,8]{2,1,0:T(2,128)}, f32[96,2,1,8,64]{4,3,1,0,2:T(8,128)S(1)}) fusion(bf16[96,2,8,128]{3,2,1,0:T(8,128)(2,1)S(1)} %reshape.262, bf16[96,64,128]{2,1,0:T(8,128)(2,1)} %param.17, pred[96,64]{1,0:T(8,128)(4,1)S(1)} %iota_compare_fusion.4), kind=kOutput, calls=%fused_computation.103 | convolution fusion | flops 25459200 | bytes 2371584 | tf_op jit(solution)/shard_map/rthgd,rjhd->rthgj/dot_general | solution.py:49
  112.5 0.7 gather_fusion
  113.2 0.1 gather.7
  113.3 0.8 copy.108
  114.1 7.3 %fusion.36 = f32[96,2,2,128]{0,3,1,2:T(8,128)S(1)} fusion(bf16[2,128,8192,1]{2,1,3,0:T(8,128)(2,1)} %bitcast.163, bf16[96,2,8192]{2,1,0:T(2,128)(2,1)} %fusion.2, f32[96,2,2,128]{0,3,1,2:T(8,128)} %copy.108, pred[96]{0:T(512)(128)(4,1)S(1)} %copy-done.6), kind=kOutput, calls=%fused_computation.27 | convolution fusion | flops 805404672 | bytes 7733344 | tf_op jit(solution)/shard_map/dot_general | solution.py:107
  121.5 0.3 fusion.90
  121.8 0.3 fusion.59
  122.1 0.3 fusion.89
  122.5 0.3 fusion.88
  122.8 0.7 copy.116
  123.6 0.7 copy.117
  124.3 0.1 copy.126
  124.4 0.1 copy.124
  124.6 1.9 %fusion.81 = (f32[96,2,8]{2,1,0:T(2,128)S(1)}, f32[96,2,1,8,2]{3,4,1,0,2:T(2,128)S(1)}) fusion(bf16[96,2,128,1]{2,1,3,0:T(2,128)(2,1)S(1)} %copy.124, bf16[96,2,8,128]{3,2,1,0:T(8,128)(2,1)S(1)} %reshape.262, pred[2,2]{1,0:T(4,128)(4,1)S(1)} %copy-done.7), kind=kOutput, calls=%fused_computation.104 | convolution fusion | flops 794112 | bytes 460804 | tf_op jit(solution)/shard_map/rthgd,rshd->rthgs/dot_general | solution.py:55
  126.5 0.6 fusion.44
  127.1 0.4 fusion.49
  127.6 0.4 fusion.50
  128.0 0.6 fusion.33
  128.6 0.8 convert_element_type.111
  (33 shorter events, 0.4 us)
Async XLA Ops:
  0.6 127.4 %copy-start = (bf16[96,64,128]{2,1,0:T(8,128)(2,1)S(1)}, bf16[96,64,128]{2,1,0:T(8,128)(2,1)}, u32[]{:S(2)}) copy-start(bf16[96,64,128]{2,1,0:T(8,128)(2,1)} %param.18) | copy-start | bytes 4718596
  0.6 6.1 %copy-start.5 = (s32[96]{0:T(128)S(1)}, s32[96]{0:T(128)}, u32[]{:S(2)}) copy-start(s32[96]{0:T(128)} %param.15) | copy-start | bytes 1156
  20.9 39.8 %all-to-all-start = ((bf16[32,13,1024]{2,1,0:T(8,128)(2,1)}), bf16[32,13,1024]{2,1,0:T(8,128)(2,1)S(1)}, u32[]{:S(2)}, u32[]{:S(2)}) async-start(bf16[32,13,1024]{2,1,0:T(8,128)(2,1)} %fusion.41), calls=%async_computation | async-start | bytes 2097152 | tf_op jit(solution)/shard_map/all_to_all | solution.py:141
  32.6 56.7 %copy-start.3 = (bf16[4,2,64,128]{3,2,1,0:T(8,128)(2,1)S(1)}, bf16[4,2,64,128]{3,2,1,0:T(8,128)(2,1)}, u32[]{:S(2)}) copy-start(bf16[4,2,64,128]{3,2,1,0:T(8,128)(2,1)} %param.14) | copy-start | bytes 393220
  90.9 21.5 %all-to-all-start.1 = ((f32[32,24,128]{2,1,0:T(8,128)}), f32[32,24,128]{2,1,0:T(8,128)S(1)}, u32[]{:S(2)}, u32[]{:S(2)}) async-start(f32[32,24,128]{2,1,0:T(8,128)} %bitcast.19), calls=%async_computation.1 | async-start | bytes 786432 | tf_op jit(solution)/shard_map/all_to_all | solution.py:171
  102.5 6.4 %copy-start.2 = (bf16[96,2,1024]{2,1,0:T(2,128)(2,1)S(1)}, bf16[96,2,1024]{2,1,0:T(2,128)(2,1)}, u32[]{:S(2)}) copy-start(bf16[96,2,1024]{2,1,0:T(2,128)(2,1)} %param.16) | copy-start | bytes 1179652
  102.5 6.7 %copy-start.4 = (s32[96]{0:T(128)S(1)}, s32[96]{0:T(128)}, u32[]{:S(2)}) copy-start(s32[96]{0:T(128)} %param.19) | copy-start | bytes 1156
  109.2 5.0 %copy-start.6 = (pred[96]{0:T(512)(128)(4,1)S(1)}, pred[96]{0:T(512)(128)(4,1)}, u32[]{:S(2)}) copy-start(pred[96]{0:T(512)(128)(4,1)} %get-tuple-element.21) | copy-start | bytes 292
  114.1 10.4 %copy-start.7 = (pred[2,2]{1,0:T(4,128)(4,1)S(1)}, pred[2,2]{1,0:T(4,128)(4,1)}, u32[]{:S(2)}) copy-start(pred[2,2]{1,0:T(4,128)(4,1)} %iota_compare_fusion.7) | copy-start | bytes 16
  114.1 12.3 %copy-start.1 = (f32[96,2,8]{2,1,0:T(2,128)S(1)}, f32[96,2,8]{2,1,0:T(2,128)}, u32[]{:S(2)}) copy-start(f32[96,2,8]{2,1,0:T(2,128)} %get-tuple-element.27) | copy-start | bytes 18436

commit v2 on v1

--- a/solution.py
+++ b/solution.py
@@ -103,13 +103,16 @@
     cap = SLOT_CAPACITY
     slot_total = owner_count * cap
 
-    normed_input = normalize(hidden, input_norm_gain)
+    values = hidden.astype(jnp.float32)
+    meansq = jnp.mean(values * values, axis=-1, keepdims=True)
+    row_scale = lax.rsqrt(meansq + epsilon)
+    normed_input = (values * row_scale * input_norm_gain.astype(jnp.float32)).astype(jnp.bfloat16)
     base_proj = jnp.dot(
         normed_input.reshape(row_count * token_count, model_width),
         key_value_weight.reshape(model_width, 2 * column_count),
         preferred_element_type=jnp.float32,
     )
-    base_proj = base_proj.reshape(row_count, token_count, 2, column_count)
+    base_proj = lax.optimization_barrier(base_proj.reshape(row_count, token_count, 2, column_count))
 
     owner_of = request_adapter // adapter_number
     local_adapter = request_adapter - owner_of * adapter_number
@@ -123,7 +126,11 @@
     )
 
     feature_start = lax.axis_index("tensor") * feature_total
-    own_features = lax.dynamic_slice_in_dim(normed_input, feature_start, feature_total, 2)
+    hidden_shard = lax.dynamic_slice_in_dim(hidden, feature_start, feature_total, 2)
+    gain_shard = lax.dynamic_slice_in_dim(input_norm_gain, feature_start, feature_total, 0)
+    own_features = (
+        hidden_shard.astype(jnp.float32) * row_scale * gain_shard.astype(jnp.float32)
+    ).astype(jnp.bfloat16)
     packed = jnp.dot(
         pick,
         own_features.reshape(row_count, token_count * feature_total),

time: 130 us -> 115 us (0.88)
  the two profiles are of different devices: /device:TPU:8 before, /device:TPU:6 now
where the time goes in v2:
time: 115 us; the launch traced here: 114 us
  blocking collectives  23.2 us (20%)
  other arithmetic  22.9 us (20%)
  starting transfers between devices  21 us (18%)
  matrix products  17.3 us (15%)
  local copies, waits for them, and re-layouts  16.1 us (14%)
  waiting for transfers between devices  12.6 us (11%)
    psum x1, blocking collectives, body(): rank_hidden = lax.psum(partial_rank, 'tensor').astype(jnp.bfloat16)  23.2 us
    all_to_all x1, starting transfers between devices, body(): recv = lax.all_to_all(send, 'adapter', 0, 0, tiled=True)  11.7 us
    all_to_all x1, waiting for transfers between devices, body(): delta_recv = lax.all_to_all(delta_send, 'adapter', 0, 0, tiled=True)  11.4 us
    convert_element_type x1, other arithmetic, body(): (values * row_scale * input_norm_gain.astype(jnp.float32)).astype(jnp.bfl...  9.97 us
    all_to_all x1, starting transfers between devices, body(): delta_recv = lax.all_to_all(delta_send, 'adapter', 0, 0, tiled=True)  9.32 us
    dot_general x1, matrix products, body(): jnp.dot(normed_input.reshape(row_count * token_count, model_width), key_v...  7.75 us
    dot_general x1, local copies, waits for them, and re-layouts, body(): jnp.dot(normed_input.reshape(row_count * token_count, model_width), key_v...  6.37 us
    reduce_sum x1, other arithmetic, body(): meansq = jnp.mean(values * values, axis=-1, keepdims=True)  5.33 us
  transfers between devices with their start and end apart: 2, of which 2 were waited for; matrix products, arithmetic and copies ran while one was open for 28% of the time, Pallas kernels for 0%

profile of v2, /device:TPU:6, one launch (start us, length us, event | category | flops | bytes accessed | tf_op | source)
XLA Modules:
  0.0 114.0 jit_solution(14848379622276625619)
XLA Ops:
  0.7 5.3 %fusion = f32[96,2]{1,0:T(8,128)S(1)} fusion(bf16[96,2,8192]{2,1,0:T(2,128)(2,1)} %param.10), kind=kLoop, calls=%fused_computation.3 | loop fusion | flops 4718400 | bytes 3146496 | tf_op jit(solution)/shard_map/reduce_sum | solution.py:107
  6.0 0.2 convert_reduce_fusion
  6.2 0.5 compare_and_fusion
  6.8 0.1 fusion.50
  6.9 0.1 reshape.290
  7.1 1.5 %multiply_convert_fusion = bf16[96,2,1024]{2,1,0:T(2,128)(2,1)S(1)} fusion(f32[1024]{0:T(1024)S(1)} %dynamic-slice_convert_fusion, f32[96,2]{1,0:T(8,128)S(1)} %add_rsqrt_fusion, bf16[96,2,8192]{2,1,0:T(2,128)(2,1)} %param.10, s32[]{:T(128)S(6)} %select_n.31), kind=kLoop, calls=%fused_computation.37 | loop fusion | flops 786432 | bytes 791300 | tf_op jit(solution)/shard_map/convert_element_type | solution.py:133
  8.7 0.4 convolution_convert_fusion
  9.0 0.4 reshape.258
  9.4 1.1 %fusion.38 = bf16[32,13,1024]{2,1,0:T(8,128)(2,1)} fusion(bf16[32,1,6]{2,1,0:T(2,128)(2,1)S(1)} %reshape.290, bf16[32,12,1024]{2,1,0:T(8,128)(2,1)S(1)} %reshape.258), kind=kLoop, calls=%fused_computation.32 | loop fusion | flops 2555904 | bytes 1638784 | tf_op jit(solution)/shard_map/concatenate | solution.py:147
  10.5 11.7 %all-to-all-start = ((bf16[32,13,1024]{2,1,0:T(8,128)(2,1)}), bf16[32,13,1024]{2,1,0:T(8,128)(2,1)S(1)}, u32[]{:S(2)}, u32[]{:S(2)}) async-start(bf16[32,13,1024]{2,1,0:T(8,128)(2,1)} %fusion.38), calls=%async_computation | async-start | bytes 2097152 | tf_op jit(solution)/shard_map/all_to_all | solution.py:148
  22.2 10.0 %fusion.3 = bf16[96,2,8192,1]{2,1,0,3:T(2,128)(2,1)} fusion(bf16[96,2,8192]{2,1,0:T(2,128)(2,1)} %param.10, f32[8192]{0:T(1024)S(1)} %convert_element_type.100, f32[96,2]{1,0:T(8,128)S(1)} %add_rsqrt_fusion), kind=kLoop, calls=%fused_computation.7 | loop fusion | flops 6291456 | bytes 6324992 | tf_op jit(solution)/shard_map/convert_element_type | solution.py:109
  32.2 2.5 %copy.122 = bf16[1024,8,2,128]{3,1,2,0:T(8,128)(2,1)} copy(bf16[1024,8,2,128]{3,2,1,0:T(2,128)(2,1)S(1)} %bitcast.157) | data formatting | bytes 8388608
  34.7 6.4 %copy.79 = bf16[256,8192]{1,0:T(8,128)(2,1)} copy(bf16[256,8192]{0,1:T(8,128)(2,1)} %bitcast.155) | data formatting | bytes 8388608 | tf_op jit(solution)/shard_map/dot_general | solution.py:110
  41.1 7.7 %fusion.4 = f32[96,2,2,128]{3,0,2,1:T(8,128)} fusion(bf16[2,128,8192,1]{2,1,0,3:T(8,128)(2,1)} %bitcast.158, bf16[96,2,8192,1]{2,1,0,3:T(2,128)(2,1)} %fusion.3), kind=kOutput, calls=%fused_computation.8 | convolution fusion | flops 805306368 | bytes 7536640 | tf_op jit(solution)/shard_map/dot_general | solution.py:110
  48.9 1.2 %all-to-all-done = bf16[32,13,1024]{2,1,0:T(8,128)(2,1)S(1)} async-done(((bf16[32,13,1024]{2,1,0:T(8,128)(2,1)}), bf16[32,13,1024]{2,1,0:T(8,128)(2,1)S(1)}, u32[]{:S(2)}, u32[]{:S(2)}) %all-to-all-start) | async-done | bytes 852000 | tf_op jit(solution)/shard_map/all_to_all | solution.py:148
  50.1 0.1 reshape.266
  50.3 0.6 reshape.260
  50.9 1.8 %fusion.26 = f32[192,2,128]{2,0,1:T(8,128)S(1)} fusion(bf16[4,1024,128]{2,1,0:T(8,128)(2,1)} %param.13, bf16[192,2,1024,1]{2,1,0,3:T(2,128)(2,1)S(1)} %bitcast.161, f32[192,4]{0,1:T(4,128)S(1)} %get-tuple-element.22), kind=kOutput, calls=%fused_computation.23 | convolution fusion | flops 402997248 | bytes 2034688 | tf_op jit(solution)/shard_map/euz,nzs->euns/dot_general | solution.py:156
  52.8 23.2 %all-reduce.2 = bf16[192,2,128]{2,0,1:T(8,128)(2,1)S(1)} all-reduce(f32[192,2,128]{2,0,1:T(8,128)S(1)} %fusion.26), channel_id=1, replica_groups=mesh['adapter'=32,'tensor'=8] {'tensor'}, use_global_device_ids=true, to_apply=%region_3.4 | all-reduce | flops 49152 | bytes 294912 | tf_op jit(solution)/shard_map/psum | solution.py:160
  76.0 0.1 copy.83
  76.1 0.2 convolution_bitcast_fusion
  76.4 0.2 convolution_bitcast_fusion.1
  76.7 1.1 copy.86
  77.7 9.3 %all-to-all-start.1 = ((f32[32,24,128]{2,1,0:T(8,128)}), f32[32,24,128]{2,1,0:T(8,128)S(1)}, u32[]{:S(2)}, u32[]{:S(2)}) async-start(f32[32,24,128]{2,1,0:T(8,128)} %bitcast.18), calls=%async_computation.1 | async-start | bytes 786432 | tf_op jit(solution)/shard_map/all_to_all | solution.py:178
  87.1 0.5 iota_compare_fusion.7
  87.6 0.8 copy.88
  88.4 0.3 reshape.263
  88.7 0.1 iota_compare_fusion.4
  88.8 3.1 %fusion.77 = (f32[96,2,8]{2,1,0:T(2,128)}, f32[96,2,1,8,64]{4,3,1,0,2:T(8,128)S(1)}) fusion(bf16[96,2,8,128]{3,2,1,0:T(8,128)(2,1)S(1)} %reshape.263, bf16[96,64,128]{2,1,0:T(8,128)(2,1)} %param.17, pred[96,64]{1,0:T(8,128)(4,1)S(1)} %iota_compare_fusion.4), kind=kOutput, calls=%fused_computation.104 | convolution fusion | flops 25459200 | bytes 2371584 | tf_op jit(solution)/shard_map/rthgd,rjhd->rthgj/dot_general | solution.py:49
  91.9 11.4 %all-to-all-done.1 = f32[32,24,128]{2,1,0:T(8,128)S(1)} async-done(((f32[32,24,128]{2,1,0:T(8,128)}), f32[32,24,128]{2,1,0:T(8,128)S(1)}, u32[]{:S(2)}, u32[]{:S(2)}) %all-to-all-start.1) | async-done | bytes 393248 | tf_op jit(solution)/shard_map/all_to_all | solution.py:178
  103.4 0.7 gather_fusion
  104.1 0.1 gather.7
  104.2 0.1 copy.87
  104.4 1.0 select_add_fusion
  105.4 0.3 fusion.87
  105.7 0.3 fusion.56
  106.0 0.3 fusion.86
  106.4 0.3 fusion.85
  106.7 0.7 copy.95
  107.4 0.7 copy.96
  108.2 0.1 copy.104
  108.3 0.1 copy.102
  108.4 2.5 %fusion.78 = (f32[96,2,8]{2,1,0:T(2,128)S(1)}, f32[96,2,1,8,2]{3,4,1,0,2:T(2,128)S(1)}) fusion(bf16[96,2,128,1]{2,1,3,0:T(2,128)(2,1)S(1)} %copy.102, bf16[96,2,8,128]{3,2,1,0:T(8,128)(2,1)S(1)} %reshape.263, pred[2,2]{1,0:T(4,128)(4,1)} %iota_compare_fusion.7), kind=kOutput, calls=%fused_computation.105 | convolution fusion | flops 794112 | bytes 460804 | tf_op jit(solution)/shard_map/rthgd,rshd->rthgs/dot_general | solution.py:55
  111.0 0.6 fusion.41
  111.7 0.4 fusion.46
  112.1 0.4 fusion.47
  112.5 0.6 fusion.33
  113.2 0.8 convert_element_type.123
  (40 shorter events, 0.6 us)
Async XLA Ops:
  0.6 111.9 %copy-start = (bf16[96,64,128]{2,1,0:T(8,128)(2,1)S(1)}, bf16[96,64,128]{2,1,0:T(8,128)(2,1)}, u32[]{:S(2)}) copy-start(bf16[96,64,128]{2,1,0:T(8,128)(2,1)} %param.18) | copy-start | bytes 4718596
  0.6 5.4 %copy-start.9 = (s32[96]{0:T(128)S(1)}, s32[96]{0:T(128)}, u32[]{:S(2)}) copy-start(s32[96]{0:T(128)} %param.15) | copy-start | bytes 1156
  0.7 6.4 %copy-start.6 = (bf16[8192]{0:T(1024)(128)(2,1)S(1)}, bf16[8192]{0:T(1024)(128)(2,1)}, u32[]{:S(2)}) copy-start(bf16[8192]{0:T(1024)(128)(2,1)} %param.11) | copy-start | bytes 49156
  10.5 39.5 %all-to-all-start = ((bf16[32,13,1024]{2,1,0:T(8,128)(2,1)}), bf16[32,13,1024]{2,1,0:T(8,128)(2,1)S(1)}, u32[]{:S(2)}, u32[]{:S(2)}) async-start(bf16[32,13,1024]{2,1,0:T(8,128)(2,1)} %fusion.38), calls=%async_computation | async-start | bytes 2097152 | tf_op jit(solution)/shard_map/all_to_all | solution.py:148
  22.2 10.0 %copy-start.1 = (bf16[8192,2,128]{2,1,0:T(2,128)(2,1)S(1)}, bf16[8192,2,128]{2,1,0:T(2,128)(2,1)}, u32[]{:S(2)}) copy-start(bf16[8192,2,128]{2,1,0:T(2,128)(2,1)} %param.12) | copy-start | bytes 12582916
  48.9 27.3 %copy-start.5 = (bf16[4,2,64,128]{3,2,1,0:T(8,128)(2,1)S(1)}, bf16[4,2,64,128]{3,2,1,0:T(8,128)(2,1)}, u32[]{:S(2)}) copy-start(bf16[4,2,64,128]{3,2,1,0:T(8,128)(2,1)} %param.14) | copy-start | bytes 393220
  50.9 36.7 %copy-start.4 = (f32[96,2,2,128]{3,0,2,1:T(8,128)S(1)}, f32[96,2,2,128]{3,0,2,1:T(8,128)}, u32[]{:S(2)}) copy-start(f32[96,2,2,128]{3,0,2,1:T(8,128)} %fusion.4) | copy-start | bytes 589828
  52.8 35.7 %copy-start.3 = (bf16[96,2,1024]{2,1,0:T(2,128)(2,1)S(1)}, bf16[96,2,1024]{2,1,0:T(2,128)(2,1)}, u32[]{:S(2)}) copy-start(bf16[96,2,1024]{2,1,0:T(2,128)(2,1)} %param.16) | copy-start | bytes 1179652
  52.8 35.9 %copy-start.8 = (s32[96]{0:T(128)S(1)}, s32[96]{0:T(128)}, u32[]{:S(2)}) copy-start(s32[96]{0:T(128)} %param.19) | copy-start | bytes 1156
  77.7 25.6 %all-to-all-start.1 = ((f32[32,24,128]{2,1,0:T(8,128)}), f32[32,24,128]{2,1,0:T(8,128)S(1)}, u32[]{:S(2)}, u32[]{:S(2)}) async-start(f32[32,24,128]{2,1,0:T(8,128)} %bitcast.18), calls=%async_computation.1 | async-start | bytes 786432 | tf_op jit(solution)/shard_map/all_to_all | solution.py:178
  88.7 15.7 %copy-start.7 = (pred[96]{0:T(512)(128)(4,1)S(1)}, pred[96]{0:T(512)(128)(4,1)}, u32[]{:S(2)}) copy-start(pred[96]{0:T(512)(128)(4,1)} %get-tuple-element.18) | copy-start | bytes 292
  104.1 6.9 %copy-start.2 = (f32[96,2,8]{2,1,0:T(2,128)S(1)}, f32[96,2,8]{2,1,0:T(2,128)}, u32[]{:S(2)}) copy-start(f32[96,2,8]{2,1,0:T(2,128)} %get-tuple-element.24) | copy-start | bytes 18436

commit v3 on v2

--- a/solution.py
+++ b/solution.py
@@ -157,7 +157,8 @@
         "euz,nzs->euns", got_rows, adapter_down_weight, preferred_element_type=jnp.float32
     )
     partial_rank = jnp.sum(down_all * selector[:, None, :, None], axis=2)
-    rank_hidden = lax.psum(partial_rank, "tensor").astype(jnp.bfloat16)
+    every_partial = lax.all_gather(partial_rank, "tensor", axis=0, tiled=False)
+    rank_hidden = jnp.sum(every_partial, axis=0).astype(jnp.bfloat16)
 
     rank_selector = selector.astype(jnp.bfloat16)
     masked = rank_hidden[:, :, None, :] * rank_selector[:, None, :, None]

time: 115 us -> 130 us (1.13)
  waiting for transfers between devices: 12.6 us -> 39.8 us
  blocking collectives: 23.2 us -> 0 us
  between operations: 1.07 us -> 14.5 us
  matrix products: 17.3 us -> 13.4 us
  local copies, waits for them, and re-layouts: 16.1 us -> 19.1 us
  other arithmetic: 22.9 us -> 20.7 us
    all_to_all x1, waiting for transfers between devices: 1.21 us -> 28 us  [body(): recv = lax.all_to_all(send, 'adapter', 0, 0, tiled=True)]
    psum x1 -> x0, blocking collectives: 23.2 us -> none  [body(): rank_hidden = lax.psum(partial_rank, 'tensor').astype(jnp.bfloat16)]
    dot_general x1, matrix products: 7.75 us -> 3.91 us  [body(): jnp.dot(normed_input.reshape(row_count * token_count, model_width), key_v...]
    convert_element_type x1, other arithmetic: 9.97 us -> 6.3 us  [body(): (values * row_scale * input_norm_gain.astype(jnp.float32)).astype(jnp.bfl...]
    unnamed x24 -> x20, local copies, waits for them, and re-layouts: 4.12 us -> 6.25 us
    reduce_sum x0 -> x1, other arithmetic: none -> 2.02 us  [body(): rank_hidden = jnp.sum(every_partial, axis=0).astype(jnp.bfloat16)]
  transfers between devices with their start and end apart: 2 -> 3, of which waited for: 2 -> 3; matrix products, arithmetic and copies ran while one was open for 28% -> 20% of each run, Pallas kernels for 0% -> 0%
where the time goes in v3:
time: 130 us; the launch traced here: 129 us
  waiting for transfers between devices  39.8 us (31%)
  starting transfers between devices  21.6 us (17%)
  other arithmetic  20.7 us (16%)
  local copies, waits for them, and re-layouts  19.1 us (15%)
  between operations  14.5 us (11%)
  matrix products  13.4 us (10%)
    all_to_all x1, waiting for transfers between devices, body(): recv = lax.all_to_all(send, 'adapter', 0, 0, tiled=True)  28 us
    all_to_all x1, starting transfers between devices, body(): recv = lax.all_to_all(send, 'adapter', 0, 0, tiled=True)  11.5 us
    all_to_all x1, waiting for transfers between devices, body(): delta_recv = lax.all_to_all(delta_send, 'adapter', 0, 0, tiled=True)  10.7 us
    all_to_all x1, starting transfers between devices, body(): delta_recv = lax.all_to_all(delta_send, 'adapter', 0, 0, tiled=True)  10.1 us
    dot_general x1, local copies, waits for them, and re-layouts, body(): jnp.dot(normed_input.reshape(row_count * token_count, model_width), key_v...  6.4 us
    convert_element_type x1, other arithmetic, body(): (values * row_scale * input_norm_gain.astype(jnp.float32)).astype(jnp.bfl...  6.3 us
    unnamed x20, local copies, waits for them, and re-layouts  6.25 us
    reduce_sum x1, other arithmetic, body(): meansq = jnp.mean(values * values, axis=-1, keepdims=True)  5.33 us
  transfers between devices with their start and end apart: 3, of which 3 were waited for; matrix products, arithmetic and copies ran while one was open for 20% of the time, Pallas kernels for 0%

profile of v3, /device:TPU:6, one launch (start us, length us, event | category | flops | bytes accessed | tf_op | source)
XLA Modules:
  0.0 129.0 jit_solution(7158921476039924621)
XLA Ops:
  7.2 5.3 %fusion = f32[96,2]{1,0:T(8,128)S(1)} fusion(bf16[96,2,8192]{2,1,0:T(2,128)(2,1)} %param.10), kind=kLoop, calls=%fused_computation.3 | loop fusion | flops 4718400 | bytes 3146496 | tf_op jit(solution)/shard_map/reduce_sum | solution.py:107
  12.6 0.2 convert_reduce_fusion
  12.8 0.1 fusion.50
  12.9 0.1 reshape.293
  13.1 1.5 %multiply_convert_fusion = bf16[96,2,1024]{2,1,0:T(2,128)(2,1)S(1)} fusion(f32[1024]{0:T(1024)S(1)} %dynamic-slice_convert_fusion, f32[96,2]{1,0:T(8,128)S(1)} %add_rsqrt_fusion, bf16[96,2,8192]{2,1,0:T(2,128)(2,1)} %param.10, s32[]{:T(128)S(6)} %select_n.31), kind=kLoop, calls=%fused_computation.37 | loop fusion | flops 786432 | bytes 791300 | tf_op jit(solution)/shard_map/convert_element_type | solution.py:133
  14.7 0.4 convolution_convert_fusion
  15.0 0.4 reshape.260
  15.4 1.2 fusion.38
  16.6 11.5 %all-to-all-start = ((bf16[32,13,1024]{2,1,0:T(8,128)(2,1)}), bf16[32,13,1024]{2,1,0:T(8,128)(2,1)S(1)}, u32[]{:S(2)}, u32[]{:S(2)}) async-start(bf16[32,13,1024]{2,1,0:T(8,128)(2,1)} %fusion.38), calls=%async_computation | async-start | bytes 2097152 | tf_op jit(solution)/shard_map/all_to_all | solution.py:148
  28.1 28.0 %all-to-all-done = bf16[32,13,1024]{2,1,0:T(8,128)(2,1)S(1)} async-done(((bf16[32,13,1024]{2,1,0:T(8,128)(2,1)}), bf16[32,13,1024]{2,1,0:T(8,128)(2,1)S(1)}, u32[]{:S(2)}, u32[]{:S(2)}) %all-to-all-start) | async-done | bytes 852000 | tf_op jit(solution)/shard_map/all_to_all | solution.py:148
  56.2 0.1 reshape.268
  56.3 0.6 reshape.262
  56.9 1.8 %fusion.26 = f32[192,2,128]{2,0,1:T(8,128)S(1)} fusion(bf16[4,1024,128]{2,1,0:T(8,128)(2,1)} %param.13, bf16[192,2,1024,1]{2,1,0,3:T(2,128)(2,1)S(1)} %bitcast.163, f32[192,4]{0,1:T(4,128)S(1)} %get-tuple-element.25), kind=kOutput, calls=%fused_computation.23 | convolution fusion | flops 402997248 | bytes 2034688 | tf_op jit(solution)/shard_map/euz,nzs->euns/dot_general | solution.py:156
  58.7 0.8 copy.103
  59.6 4.7 %copy.143 = bf16[1024,8,2,128]{3,1,2,0:T(8,128)(2,1)} copy(bf16[1024,8,2,128]{3,2,1,0:T(2,128)(2,1)} %bitcast.158) | data formatting | bytes 8388608
  64.3 6.4 %copy.99 = bf16[256,8192]{1,0:T(8,128)(2,1)} copy(bf16[256,8192]{0,1:T(8,128)(2,1)} %bitcast.156) | data formatting | bytes 8388608 | tf_op jit(solution)/shard_map/dot_general | solution.py:110
  70.7 6.3 %fusion.3 = bf16[96,2,8192,1]{2,1,0,3:T(2,128)(2,1)S(1)} fusion(bf16[96,2,8192]{2,1,0:T(2,128)(2,1)} %param.10, f32[8192]{0:T(1024)S(1)} %convert_element_type.104, f32[96,2]{1,0:T(8,128)S(1)} %add_rsqrt_fusion), kind=kLoop, calls=%fused_computation.7 | loop fusion | flops 6291456 | bytes 6324992 | tf_op jit(solution)/shard_map/convert_element_type | solution.py:109
  77.0 3.9 %fusion.4 = f32[96,2,2,128]{3,0,2,1:T(8,128)S(1)} fusion(bf16[2,128,8192,1]{2,1,0,3:T(8,128)(2,1)S(1)} %bitcast.159, bf16[96,2,8192,1]{2,1,0,3:T(2,128)(2,1)S(1)} %fusion.3), kind=kOutput, calls=%fused_computation.8 | convolution fusion | flops 805306368 | bytes 7536640 | tf_op jit(solution)/shard_map/dot_general | solution.py:110
  80.9 1.1 all-gather.3.cloned.1.call-done
  82.0 2.0 %reduce_sum.57 = bf16[192,2,128]{2,1,0:T(2,128)(2,1)S(1)} reduce(f32[8,192,2,128]{3,2,1,0:T(2,128)} %bitcast.160, f32[]{:T(128)} %constant.18.clone.1), dimensions={0}, to_apply=%region_3.4 | reduce | flops 344064 | bytes 1671172 | tf_op jit(solution)/shard_map/reduce_sum | solution.py:161
  84.1 0.1 copy.104
  84.3 0.2 convolution_bitcast_fusion
  84.5 0.3 convolution_bitcast_fusion.1
  84.8 1.1 copy.107
  85.8 10.1 %all-to-all-start.1 = ((f32[32,24,128]{2,1,0:T(8,128)}), f32[32,24,128]{2,1,0:T(8,128)S(1)}, u32[]{:S(2)}, u32[]{:S(2)}) async-start(f32[32,24,128]{2,1,0:T(8,128)} %bitcast.19), calls=%async_computation.1 | async-start | bytes 786432 | tf_op jit(solution)/shard_map/all_to_all | solution.py:179
  95.9 0.5 iota_compare_fusion.7
  96.5 0.8 copy.109
  97.3 0.3 reshape.265
  97.6 3.1 %fusion.77 = (f32[96,2,8]{2,1,0:T(2,128)}, f32[96,2,1,8,64]{4,3,1,0,2:T(8,128)S(1)}) fusion(bf16[96,2,8,128]{3,2,1,0:T(8,128)(2,1)S(1)} %reshape.265, bf16[96,64,128]{2,1,0:T(8,128)(2,1)} %param.17, pred[96,64]{1,0:T(8,128)(4,1)S(1)} %iota_compare_fusion.4), kind=kOutput, calls=%fused_computation.104 | convolution fusion | flops 25459200 | bytes 2371584 | tf_op jit(solution)/shard_map/rthgd,rjhd->rthgj/dot_general | solution.py:49
  100.8 10.7 %all-to-all-done.1 = f32[32,24,128]{2,1,0:T(8,128)S(1)} async-done(((f32[32,24,128]{2,1,0:T(8,128)}), f32[32,24,128]{2,1,0:T(8,128)S(1)}, u32[]{:S(2)}, u32[]{:S(2)}) %all-to-all-start.1) | async-done | bytes 393248 | tf_op jit(solution)/shard_map/all_to_all | solution.py:179
  111.5 0.7 gather_fusion
  112.2 0.1 gather.7
  112.4 0.1 copy.108
  112.5 1.0 select_add_fusion
  113.5 0.3 fusion.87
  113.8 0.3 fusion.56
  114.2 0.3 fusion.86
  114.5 0.3 fusion.85
  114.8 0.7 copy.116
  115.6 0.7 copy.117
  116.3 0.1 copy.125
  116.5 0.1 copy.123
  116.6 2.5 %fusion.78 = (f32[96,2,8]{2,1,0:T(2,128)S(1)}, f32[96,2,1,8,2]{3,4,1,0,2:T(2,128)S(1)}) fusion(bf16[96,2,128,1]{2,1,3,0:T(2,128)(2,1)S(1)} %copy.123, bf16[96,2,8,128]{3,2,1,0:T(8,128)(2,1)S(1)} %reshape.265, pred[2,2]{1,0:T(4,128)(4,1)} %iota_compare_fusion.7), kind=kOutput, calls=%fused_computation.105 | convolution fusion | flops 794112 | bytes 460804 | tf_op jit(solution)/shard_map/rthgd,rshd->rthgs/dot_general | solution.py:55
  119.2 0.6 fusion.41
  119.8 0.4 fusion.46
  120.2 0.4 fusion.47
  120.7 0.6 fusion.33
  121.3 0.8 convert_element_type.127
  (40 shorter events, 0.7 us)
Async XLA Ops:
  7.2 113.5 %copy-start = (bf16[96,64,128]{2,1,0:T(8,128)(2,1)S(1)}, bf16[96,64,128]{2,1,0:T(8,128)(2,1)}, u32[]{:S(2)}) copy-start(bf16[96,64,128]{2,1,0:T(8,128)(2,1)} %param.18) | copy-start | bytes 4718596
  7.2 5.4 %copy-start.7 = (s32[96]{0:T(128)S(1)}, s32[96]{0:T(128)}, u32[]{:S(2)}) copy-start(s32[96]{0:T(128)} %param.15) | copy-start | bytes 1156
  7.2 5.9 %copy-start.5 = (bf16[8192]{0:T(1024)(128)(2,1)S(1)}, bf16[8192]{0:T(1024)(128)(2,1)}, u32[]{:S(2)}) copy-start(bf16[8192]{0:T(1024)(128)(2,1)} %param.11) | copy-start | bytes 49156
  16.6 39.5 %all-to-all-start = ((bf16[32,13,1024]{2,1,0:T(8,128)(2,1)}), bf16[32,13,1024]{2,1,0:T(8,128)(2,1)S(1)}, u32[]{:S(2)}, u32[]{:S(2)}) async-start(bf16[32,13,1024]{2,1,0:T(8,128)(2,1)} %fusion.38), calls=%async_computation | async-start | bytes 2097152 | tf_op jit(solution)/shard_map/all_to_all | solution.py:148
  28.1 54.0 %all-gather.3.cloned.1.call-start = ((), (), s32[]{:S(2)}) async-start(), calls=%async_computation.2 | async-start | bytes 1769472 | tf_op jit(solution)/shard_map/all_gather | solution.py:160
  70.7 6.3 %copy-start.1 = (bf16[256,8192]{1,0:T(8,128)(2,1)S(1)}, bf16[256,8192]{1,0:T(8,128)(2,1)}, u32[]{:S(2)}) copy-start(bf16[256,8192]{1,0:T(8,128)(2,1)} %copy.99) | copy-start | bytes 12582916
  77.0 7.2 %copy-start.4 = (bf16[4,2,64,128]{3,2,1,0:T(8,128)(2,1)S(1)}, bf16[4,2,64,128]{3,2,1,0:T(8,128)(2,1)}, u32[]{:S(2)}) copy-start(bf16[4,2,64,128]{3,2,1,0:T(8,128)(2,1)} %param.14) | copy-start | bytes 393220
  82.0 15.3 %copy-start.3 = (bf16[96,2,1024]{2,1,0:T(2,128)(2,1)S(1)}, bf16[96,2,1024]{2,1,0:T(2,128)(2,1)}, u32[]{:S(2)}) copy-start(bf16[96,2,1024]{2,1,0:T(2,128)(2,1)} %param.16) | copy-start | bytes 1179652
  84.1 13.5 %copy-start.6 = (s32[96]{0:T(128)S(1)}, s32[96]{0:T(128)}, u32[]{:S(2)}) copy-start(s32[96]{0:T(128)} %param.19) | copy-start | bytes 1156
  85.8 25.6 %all-to-all-start.1 = ((f32[32,24,128]{2,1,0:T(8,128)}), f32[32,24,128]{2,1,0:T(8,128)S(1)}, u32[]{:S(2)}, u32[]{:S(2)}) async-start(f32[32,24,128]{2,1,0:T(8,128)} %bitcast.19), calls=%async_computation.1 | async-start | bytes 786432 | tf_op jit(solution)/shard_map/all_to_all | solution.py:179
  112.2 6.9 %copy-start.2 = (f32[96,2,8]{2,1,0:T(2,128)S(1)}, f32[96,2,8]{2,1,0:T(2,128)}, u32[]{:S(2)}) copy-start(f32[96,2,8]{2,1,0:T(2,128)} %get-tuple-element.27) | copy-start | bytes 18436
Sparse Core Ops, SparseCore 0:
  59.7 22.2 all-gather.2

commit v4 on v2

--- a/solution.py
+++ b/solution.py
@@ -175,8 +175,8 @@
     )
     delta_slots = jnp.stack([key_part, value_part], axis=2)
     delta_send = delta_slots.reshape(owner_count, cap * token_count * 2, column_count)
-    delta_recv = lax.all_to_all(delta_send, "adapter", 0, 0, tiled=True)
-    delta_rows = delta_recv.reshape(slot_total, token_count * 2 * column_count)
+    delta_recv = lax.all_to_all(delta_send.astype(jnp.bfloat16), "adapter", 0, 0, tiled=True)
+    delta_rows = delta_recv.reshape(slot_total, token_count * 2 * column_count).astype(jnp.float32)
     adapter_update = jnp.take(delta_rows, slot_of, axis=0).reshape(
         row_count, token_count, 2, column_count
     )

time: 115 us -> 116 us (level)
  local copies, waits for them, and re-layouts: 16.1 us -> 21.2 us
  waiting for transfers between devices: 12.6 us -> 10.5 us
  other arithmetic: 22.9 us -> 20.9 us
    gather x3, local copies, waits for them, and re-layouts: 0.96 us -> 4.14 us  [body(): jnp.take(delta_rows, slot_of, axis=0)]
    all_to_all x1, waiting for transfers between devices: 11.4 us -> 10.2 us  [body(): lax.all_to_all(delta_send.astype(jnp.bfloat16), 'adapter', 0, 0, tiled=True)]
    unnamed x24 -> x16, local copies, waits for them, and re-layouts: 4.12 us -> 4.1 us
  transfers between devices with their start and end apart: 2 -> 2, of which waited for: 2 -> 2; matrix products, arithmetic and copies ran while one was open for 28% -> 26% of each run, Pallas kernels for 0% -> 0%
where the time goes in v4:
time: 116 us; the launch traced here: 115 us
  blocking collectives  23.9 us (21%)
  local copies, waits for them, and re-layouts  21.2 us (18%)
  starting transfers between devices  21.1 us (18%)
  other arithmetic  20.9 us (18%)
  matrix products  16.3 us (14%)
  waiting for transfers between devices  10.5 us (9%)
    psum x1, blocking collectives, body(): rank_hidden = lax.psum(partial_rank, 'tensor').astype(jnp.bfloat16)  23.9 us
    all_to_all x1, starting transfers between devices, body(): recv = lax.all_to_all(send, 'adapter', 0, 0, tiled=True)  11.7 us
    all_to_all x1, waiting for transfers between devices, body(): lax.all_to_all(delta_send.astype(jnp.bfloat16), 'adapter', 0, 0, tiled=True)  10.2 us
    convert_element_type x1, other arithmetic, body(): (values * row_scale * input_norm_gain.astype(jnp.float32)).astype(jnp.bfl...  9.97 us
    all_to_all x1, starting transfers between devices, body(): lax.all_to_all(delta_send.astype(jnp.bfloat16), 'adapter', 0, 0, tiled=True)  9.44 us
    dot_general x1, matrix products, body(): jnp.dot(normed_input.reshape(row_count * token_count, model_width), key_v...  7.07 us
    dot_general x1, local copies, waits for them, and re-layouts, body(): jnp.dot(normed_input.reshape(row_count * token_count, model_width), key_v...  6.37 us
    reduce_sum x1, other arithmetic, body(): meansq = jnp.mean(values * values, axis=-1, keepdims=True)  5.33 us
  transfers between devices with their start and end apart: 2, of which 2 were waited for; matrix products, arithmetic and copies ran while one was open for 26% of the time, Pallas kernels for 0%

profile of v4, /device:TPU:6, one launch (start us, length us, event | category | flops | bytes accessed | tf_op | source)
XLA Modules:
  0.0 115.0 jit_solution(5642547199656187493)
XLA Ops:
  0.7 5.3 %fusion = f32[96,2]{1,0:T(8,128)S(1)} fusion(bf16[96,2,8192]{2,1,0:T(2,128)(2,1)} %param.10), kind=kLoop, calls=%fused_computation.3 | loop fusion | flops 4718400 | bytes 3146496 | tf_op jit(solution)/shard_map/reduce_sum | solution.py:107
  6.0 0.2 convert_reduce_fusion
  6.3 0.1 fusion.54
  6.4 0.1 reshape.288
  6.6 1.5 %multiply_convert_fusion = bf16[96,2,1024]{2,1,0:T(2,128)(2,1)S(1)} fusion(f32[1024]{0:T(1024)S(1)} %dynamic-slice_convert_fusion, f32[96,2]{1,0:T(8,128)S(1)} %add_rsqrt_fusion, bf16[96,2,8192]{2,1,0:T(2,128)(2,1)} %param.10, s32[]{:T(128)S(6)} %select_n.31), kind=kLoop, calls=%fused_computation.41 | loop fusion | flops 786432 | bytes 791300 | tf_op jit(solution)/shard_map/convert_element_type | solution.py:133
  8.1 0.1 copy.116
  8.1 0.4 convolution_convert_fusion
  8.5 0.4 reshape.257
  8.9 1.1 fusion.42
  10.0 11.7 %all-to-all-start = ((bf16[32,13,1024]{2,1,0:T(8,128)(2,1)}), bf16[32,13,1024]{2,1,0:T(8,128)(2,1)S(1)}, u32[]{:S(2)}, u32[]{:S(2)}) async-start(bf16[32,13,1024]{2,1,0:T(8,128)(2,1)} %fusion.42), calls=%async_computation | async-start | bytes 2097152 | tf_op jit(solution)/shard_map/all_to_all | solution.py:148
  21.7 10.0 %fusion.3 = bf16[96,2,8192,1]{2,1,0,3:T(2,128)(2,1)} fusion(bf16[96,2,8192]{2,1,0:T(2,128)(2,1)} %param.10, f32[8192]{0:T(1024)S(1)} %convert_element_type.110, f32[96,2]{1,0:T(8,128)S(1)} %add_rsqrt_fusion), kind=kLoop, calls=%fused_computation.7 | loop fusion | flops 6291456 | bytes 6324992 | tf_op jit(solution)/shard_map/convert_element_type | solution.py:109
  31.7 2.5 %copy.122 = bf16[1024,8,2,128]{3,1,2,0:T(8,128)(2,1)} copy(bf16[1024,8,2,128]{3,2,1,0:T(2,128)(2,1)S(1)} %bitcast.167) | data formatting | bytes 8388608
  34.2 6.4 %copy.79 = bf16[256,8192]{1,0:T(8,128)(2,1)} copy(bf16[256,8192]{0,1:T(8,128)(2,1)} %bitcast.165) | data formatting | bytes 8388608 | tf_op jit(solution)/shard_map/dot_general | solution.py:110
  40.6 7.1 %fusion.4 = f32[96,2,2,128]{3,0,2,1:T(8,128)S(1)} fusion(bf16[2,128,8192,1]{2,1,0,3:T(8,128)(2,1)} %bitcast.168, bf16[96,2,8192,1]{2,1,0,3:T(2,128)(2,1)} %fusion.3), kind=kOutput, calls=%fused_computation.8 | convolution fusion | flops 805306368 | bytes 7536640 | tf_op jit(solution)/shard_map/dot_general | solution.py:110
  47.7 0.1 copy.88
  47.8 1.2 %reshape.260 = bf16[96,2,8,128]{3,2,1,0:T(8,128)(2,1)S(1)} reshape(bf16[96,2,1024]{2,1,0:T(2,128)(2,1)} %param.16) | data formatting | bytes 786432 | tf_op jit(solution)/shard_map/reshape.5
  49.1 0.1 iota_compare_fusion.4
  49.2 0.4 all-to-all-done
  49.6 0.1 fusion.74
  49.6 0.1 reshape.263
  49.8 1.5 %reshape.259 = bf16[192,2,1024]{2,1,0:T(2,128)(2,1)} reshape(bf16[32,12,1024]{2,1,0:T(8,128)(2,1)S(1)} %bitcast.166) | data formatting | bytes 1572864 | tf_op jit(solution)/shard_map/reshape | solution.py:150
  51.3 2.1 %fusion.26 = f32[192,2,128]{2,0,1:T(8,128)S(1)} fusion(bf16[4,1024,128]{2,1,0:T(8,128)(2,1)} %param.13, bf16[192,2,1024,1]{2,1,0,3:T(2,128)(2,1)} %bitcast.171, f32[192,4]{0,1:T(4,128)S(1)} %get-tuple-element.22), kind=kOutput, calls=%fused_computation.23 | convolution fusion | flops 402997248 | bytes 2034688 | tf_op jit(solution)/shard_map/euz,nzs->euns/dot_general | solution.py:156
  53.3 23.9 %all-reduce.2 = bf16[192,2,128]{2,0,1:T(8,128)(2,1)S(1)} all-reduce(f32[192,2,128]{2,0,1:T(8,128)S(1)} %fusion.26), channel_id=1, replica_groups=mesh['adapter'=32,'tensor'=8] {'tensor'}, use_global_device_ids=true, to_apply=%region_3.4 | all-reduce | flops 49152 | bytes 294912 | tf_op jit(solution)/shard_map/psum | solution.py:160
  77.2 0.1 copy.83
  77.4 1.1 fusion.39
  78.5 0.2 fusion.40
  78.8 0.9 copy.86
  79.7 9.4 %all-to-all-start.1 = ((bf16[32,24,128]{2,1,0:T(8,128)(2,1)}), bf16[32,24,128]{2,1,0:T(8,128)(2,1)}, u32[]{:S(2)}, u32[]{:S(2)}) async-start(bf16[32,24,128]{2,1,0:T(8,128)(2,1)} %bitcast.18), calls=%async_computation.1 | async-start | bytes 393216 | tf_op jit(solution)/shard_map/all_to_all | solution.py:178
  89.1 2.5 %fusion.81 = (f32[96,2,8]{2,1,0:T(2,128)S(1)}, f32[96,2,1,8,64]{4,3,1,0,2:T(8,128)S(1)}) fusion(bf16[96,2,8,128]{3,2,1,0:T(8,128)(2,1)S(1)} %reshape.260, bf16[96,64,128]{2,1,0:T(8,128)(2,1)} %param.17, pred[96,64]{1,0:T(8,128)(4,1)S(1)} %iota_compare_fusion.4), kind=kOutput, calls=%fused_computation.108 | convolution fusion | flops 25459200 | bytes 2371584 | tf_op jit(solution)/shard_map/rthgd,rjhd->rthgj/dot_general | solution.py:49
  91.6 10.2 %all-to-all-done.1 = bf16[32,24,128]{2,1,0:T(8,128)(2,1)} async-done(((bf16[32,24,128]{2,1,0:T(8,128)(2,1)}), bf16[32,24,128]{2,1,0:T(8,128)(2,1)}, u32[]{:S(2)}, u32[]{:S(2)}) %all-to-all-start.1) | async-done | bytes 196640 | tf_op jit(solution)/shard_map/all_to_all | solution.py:178
  101.8 1.0 reshape.264
  102.8 1.4 %gather_fusion = f32[96,512]{1,0:T(8,128)} fusion(f32[192,512]{1,0:T(8,128)S(1)} %reshape.264, s32[1024]{0:T(1024)S(1)} %pad_clamp_fusion), kind=kCustom, calls=%fused_computation | custom fusion | bytes 393600 | tf_op jit(solution)/shard_map/jit(_take)/gather | solution.py:180
  104.2 1.7 %gather.7 = f32[96,2,2,128]{3,2,1,0:T(2,128)} reshape(f32[96,512]{1,0:T(8,128)} %gather_fusion) | data formatting | bytes 393216 | tf_op jit(solution)/shard_map/jit(_take)/gather | solution.py:180
  105.9 1.0 copy.87
  107.0 0.3 fusion.91
  107.3 0.3 fusion.60
  107.7 0.3 fusion.90
  108.0 0.3 fusion.89
  108.4 0.7 copy.95
  109.1 0.7 copy.96
  109.8 0.1 copy.104
  110.0 0.1 copy.102
  110.1 1.9 %fusion.82 = (f32[96,2,8]{2,1,0:T(2,128)S(1)}, f32[96,2,1,8,2]{3,4,1,0,2:T(2,128)S(1)}) fusion(bf16[96,2,128,1]{2,1,3,0:T(2,128)(2,1)S(1)} %copy.102, bf16[96,2,8,128]{3,2,1,0:T(8,128)(2,1)S(1)} %reshape.260, pred[2,2]{1,0:T(4,128)(4,1)S(1)} %iota_compare_fusion.7), kind=kOutput, calls=%fused_computation.109 | convolution fusion | flops 794112 | bytes 460804 | tf_op jit(solution)/shard_map/rthgd,rshd->rthgs/dot_general | solution.py:55
  112.0 0.6 fusion.45
  112.7 0.4 fusion.50
  113.1 0.4 fusion.51
  113.5 0.6 fusion.33
  114.1 0.8 convert_element_type.136
  (32 shorter events, 0.4 us)
Async XLA Ops:
  0.6 112.9 %copy-start = (bf16[96,64,128]{2,1,0:T(8,128)(2,1)S(1)}, bf16[96,64,128]{2,1,0:T(8,128)(2,1)}, u32[]{:S(2)}) copy-start(bf16[96,64,128]{2,1,0:T(8,128)(2,1)} %param.18) | copy-start | bytes 4718596
  0.6 5.4 %copy-start.4 = (s32[96]{0:T(128)S(1)}, s32[96]{0:T(128)}, u32[]{:S(2)}) copy-start(s32[96]{0:T(128)} %param.15) | copy-start | bytes 1156
  0.7 5.9 %copy-start.2 = (bf16[8192]{0:T(1024)(128)(2,1)S(1)}, bf16[8192]{0:T(1024)(128)(2,1)}, u32[]{:S(2)}) copy-start(bf16[8192]{0:T(1024)(128)(2,1)} %param.11) | copy-start | bytes 49156
  10.0 39.5 %all-to-all-start = ((bf16[32,13,1024]{2,1,0:T(8,128)(2,1)}), bf16[32,13,1024]{2,1,0:T(8,128)(2,1)S(1)}, u32[]{:S(2)}, u32[]{:S(2)}) async-start(bf16[32,13,1024]{2,1,0:T(8,128)(2,1)} %fusion.42), calls=%async_computation | async-start | bytes 2097152 | tf_op jit(solution)/shard_map/all_to_all | solution.py:148
  21.7 10.0 %copy-start.1 = (bf16[8192,2,128]{2,1,0:T(2,128)(2,1)S(1)}, bf16[8192,2,128]{2,1,0:T(2,128)(2,1)}, u32[]{:S(2)}) copy-start(bf16[8192,2,128]{2,1,0:T(2,128)(2,1)} %param.12) | copy-start | bytes 12582916
  40.6 8.5 %copy-start.3 = (s32[96]{0:T(128)S(1)}, s32[96]{0:T(128)}, u32[]{:S(2)}) copy-start(s32[96]{0:T(128)} %param.19) | copy-start | bytes 1156
  49.8 28.7 %copy-start.5 = (bf16[4,2,64,128]{3,2,1,0:T(8,128)(2,1)S(1)}, bf16[4,2,64,128]{3,2,1,0:T(8,128)(2,1)}, u32[]{:S(2)}) copy-start(bf16[4,2,64,128]{3,2,1,0:T(8,128)(2,1)} %param.14) | copy-start | bytes 393220
  79.7 22.1 %all-to-all-start.1 = ((bf16[32,24,128]{2,1,0:T(8,128)(2,1)}), bf16[32,24,128]{2,1,0:T(8,128)(2,1)}, u32[]{:S(2)}, u32[]{:S(2)}) async-start(bf16[32,24,128]{2,1,0:T(8,128)(2,1)} %bitcast.18), calls=%async_computation.1 | async-start | bytes 393216 | tf_op jit(solution)/shard_map/all_to_all | solution.py:178

commit v5 on v2

--- a/solution.py
+++ b/solution.py
@@ -1,7 +1,7 @@
 import jax
 import jax.numpy as jnp
 from jax import lax
-from jax.sharding import PartitionSpec as P
+from jax.sharding import Mesh, PartitionSpec as P
 
 HEAD_DIM = 128
 SLOT_CAPACITY = 6
@@ -125,7 +125,7 @@
         jnp.bfloat16
     )
 
-    feature_start = lax.axis_index("tensor") * feature_total
+    feature_start = (lax.axis_index("tx") * lax.axis_size("tc") + lax.axis_index("tc")) * feature_total
     hidden_shard = lax.dynamic_slice_in_dim(hidden, feature_start, feature_total, 2)
     gain_shard = lax.dynamic_slice_in_dim(input_norm_gain, feature_start, feature_total, 0)
     own_features = (
@@ -157,7 +157,7 @@
         "euz,nzs->euns", got_rows, adapter_down_weight, preferred_element_type=jnp.float32
     )
     partial_rank = jnp.sum(down_all * selector[:, None, :, None], axis=2)
-    rank_hidden = lax.psum(partial_rank, "tensor").astype(jnp.bfloat16)
+    rank_hidden = lax.psum(lax.psum(partial_rank, "tc"), "tx").astype(jnp.bfloat16)
 
     rank_selector = selector.astype(jnp.bfloat16)
     masked = rank_hidden[:, :, None, :] * rank_selector[:, None, :, None]
@@ -199,21 +199,30 @@
 
 
 def solution(mesh):
+    tensor_devices = mesh.devices.shape[1]
+    core_count = 2 if tensor_devices % 2 == 0 else 1
+    split_mesh = Mesh(
+        mesh.devices.reshape(mesh.devices.shape[0], tensor_devices // core_count, core_count),
+        ("adapter", "tx", "tc"),
+    )
+    tensor = ("tx", "tc")
     in_specs = (
         P("adapter", None, None),
         P(),
-        P(None, None, "tensor"),
-        P("adapter", "tensor", None),
-        P("adapter", None, None, "tensor"),
+        P(None, None, tensor),
+        P("adapter", tensor, None),
+        P("adapter", None, None, tensor),
         P("adapter"),
-        P("adapter", None, "tensor"),
-        P("adapter", None, "tensor"),
-        P("adapter", None, "tensor"),
+        P("adapter", None, tensor),
+        P("adapter", None, tensor),
+        P("adapter", None, tensor),
         P("adapter"),
     )
     out_specs = (
-        P("adapter", None, "tensor"),
-        P("adapter", None, "tensor"),
-        P("adapter", None, "tensor"),
-    )
-    return jax.shard_map(body, mesh=mesh, in_specs=in_specs, out_specs=out_specs, check_vma=False)
+        P("adapter", None, tensor),
+        P("adapter", None, tensor),
+        P("adapter", None, tensor),
+    )
+    return jax.shard_map(
+        body, mesh=split_mesh, in_specs=in_specs, out_specs=out_specs, check_vma=False
+    )

time: 115 us -> 150 us (1.30)
  waiting for transfers between devices: 12.6 us -> 37.6 us
  between operations: 1.07 us -> 14.4 us
  blocking collectives: 23.2 us -> 16.7 us
    psum x0 -> x1, waiting for transfers between devices: none -> 28.8 us  [body(): lax.psum(partial_rank, 'tc')]
    psum x1, blocking collectives: 23.2 us -> 16.7 us  [body(): lax.psum(lax.psum(partial_rank, 'tc'), 'tx').astype(jnp.bfloat16)]
    all_to_all x1, waiting for transfers between devices: 11.4 us -> 8.04 us  [body(): delta_recv = lax.all_to_all(delta_send, 'adapter', 0, 0, tiled=True)]
    unnamed x24 -> x22, local copies, waits for them, and re-layouts: 4.12 us -> 4.11 us
  transfers between devices with their start and end apart: 2 -> 3, of which waited for: 2 -> 3; matrix products, arithmetic and copies ran while one was open for 28% -> 22% of each run, Pallas kernels for 0% -> 0%
where the time goes in v5:
time: 150 us; the launch traced here: 148 us
  waiting for transfers between devices  37.6 us (25%)
  other arithmetic  23.6 us (16%)
  starting transfers between devices  21.6 us (14%)
  matrix products  17.9 us (12%)
  blocking collectives  16.7 us (11%)
  local copies, waits for them, and re-layouts  16.1 us (11%)
  between operations  14.4 us (10%)
    psum x1, waiting for transfers between devices, body(): lax.psum(partial_rank, 'tc')  28.8 us
    psum x1, blocking collectives, body(): lax.psum(lax.psum(partial_rank, 'tc'), 'tx').astype(jnp.bfloat16)  16.7 us
    all_to_all x1, starting transfers between devices, body(): recv = lax.all_to_all(send, 'adapter', 0, 0, tiled=True)  11.5 us
    convert_element_type x1, other arithmetic, body(): (values * row_scale * input_norm_gain.astype(jnp.float32)).astype(jnp.bfl...  9.97 us
    all_to_all x1, starting transfers between devices, body(): delta_recv = lax.all_to_all(delta_send, 'adapter', 0, 0, tiled=True)  9.85 us
    all_to_all x1, waiting for transfers between devices, body(): delta_recv = lax.all_to_all(delta_send, 'adapter', 0, 0, tiled=True)  8.04 us
    dot_general x1, matrix products, body(): jnp.dot(normed_input.reshape(row_count * token_count, model_width), key_v...  7.74 us
    dot_general x1, local copies, waits for them, and re-layouts, body(): jnp.dot(normed_input.reshape(row_count * token_count, model_width), key_v...  6.37 us
  transfers between devices with their start and end apart: 3, of which 3 were waited for; matrix products, arithmetic and copies ran while one was open for 22% of the time, Pallas kernels for 0%

profile of v5, /device:TPU:6, one launch (start us, length us, event | category | flops | bytes accessed | tf_op | source)
XLA Modules:
  0.0 147.8 jit_solution(3331017649046048096)
XLA Ops:
  7.2 5.3 %fusion = f32[96,2]{1,0:T(8,128)S(1)} fusion(bf16[96,2,8192]{2,1,0:T(2,128)(2,1)} %param.10), kind=kLoop, calls=%fused_computation.3 | loop fusion | flops 4718400 | bytes 3146496 | tf_op jit(solution)/shard_map/reduce_sum | solution.py:107
  12.6 0.2 convert_reduce_fusion
  12.8 0.1 fusion.50
  12.9 0.1 reshape.290
  13.1 1.5 multiply_convert_fusion
  14.7 0.4 convolution_convert_fusion
  15.0 0.4 reshape.258
  15.4 1.1 fusion.38
  16.6 11.5 %all-to-all-start = ((bf16[32,13,1024]{2,1,0:T(8,128)(2,1)}), bf16[32,13,1024]{2,1,0:T(8,128)(2,1)S(1)}, u32[]{:S(2)}, u32[]{:S(2)}) async-start(bf16[32,13,1024]{2,1,0:T(8,128)(2,1)} %fusion.38), calls=%async_computation | async-start | bytes 2097152 | tf_op jit(solution)/shard_map/all_to_all | solution.py:148
  28.1 0.2 all-reduce.4.cloned.1.call-start
  28.3 10.0 %fusion.3 = bf16[96,2,8192,1]{2,1,0,3:T(2,128)(2,1)} fusion(bf16[96,2,8192]{2,1,0:T(2,128)(2,1)} %param.10, f32[8192]{0:T(1024)S(1)} %convert_element_type.100, f32[96,2]{1,0:T(8,128)S(1)} %add_rsqrt_fusion), kind=kLoop, calls=%fused_computation.7 | loop fusion | flops 6291456 | bytes 6324992 | tf_op jit(solution)/shard_map/convert_element_type | solution.py:109
  38.3 2.5 %copy.122 = bf16[1024,8,2,128]{3,1,2,0:T(8,128)(2,1)} copy(bf16[1024,8,2,128]{3,2,1,0:T(2,128)(2,1)S(1)} %bitcast.157) | data formatting | bytes 8388608
  40.8 6.4 %copy.79 = bf16[256,8192]{1,0:T(8,128)(2,1)} copy(bf16[256,8192]{0,1:T(8,128)(2,1)} %bitcast.155) | data formatting | bytes 8388608 | tf_op jit(solution)/shard_map/dot_general | solution.py:110
  47.2 0.5 compare_select_fusion
  47.7 7.7 %fusion.4 = f32[96,2,2,128]{3,0,2,1:T(8,128)} fusion(bf16[2,128,8192,1]{2,1,0,3:T(8,128)(2,1)} %bitcast.158, bf16[96,2,8192,1]{2,1,0,3:T(2,128)(2,1)} %fusion.3), kind=kOutput, calls=%fused_computation.8 | convolution fusion | flops 805306368 | bytes 7536640 | tf_op jit(solution)/shard_map/dot_general | solution.py:110
  55.4 0.7 all-to-all-done
  56.3 0.6 reshape.260
  56.9 2.5 %fusion.26 = f32[192,2,128]{2,0,1:T(8,128)} fusion(bf16[4,1024,128]{2,1,0:T(8,128)(2,1)} %param.13, bf16[192,2,1024,1]{2,1,0,3:T(2,128)(2,1)S(1)} %bitcast.161, f32[192,4]{0,1:T(4,128)S(1)} %get-tuple-element.22), kind=kOutput, calls=%fused_computation.23 | convolution fusion | flops 402997248 | bytes 2034688 | tf_op jit(solution)/shard_map/euz,nzs->euns/dot_general | solution.py:156
  59.5 0.7 pad_clamp_fusion
  60.2 28.8 %all-reduce.4.cloned.1.call-done = f32[192,2,128]{2,0,1:T(8,128)} async-done(((f32[192,2,128]{2,0,1:T(8,128)}), f32[192,2,128]{2,0,1:T(8,128)}) %all-reduce.4.cloned.1.call-update) | async-done | bytes 196624 | tf_op jit(solution)/shard_map/psum | solution.py:160
  89.0 16.7 %all-reduce.5 = bf16[192,2,128]{2,0,1:T(8,128)(2,1)S(1)} all-reduce(f32[192,2,128]{2,0,1:T(8,128)} %all-reduce.4.cloned.1.call-done), channel_id=1, replica_groups=mesh['adapter'=32,'tx'=4,'tc'=2] {'tx'}, use_global_device_ids=true, to_apply=%region_4.5 | all-reduce | flops 49152 | bytes 294912 | tf_op jit(solution)/shard_map/psum | solution.py:160
  105.7 0.1 copy.83
  105.9 0.2 convolution_bitcast_fusion
  106.1 0.2 convolution_bitcast_fusion.1
  106.4 1.1 copy.86
  107.5 9.9 %all-to-all-start.1 = ((f32[32,24,128]{2,1,0:T(8,128)}), f32[32,24,128]{2,1,0:T(8,128)S(1)}, u32[]{:S(2)}, u32[]{:S(2)}) async-start(f32[32,24,128]{2,1,0:T(8,128)} %bitcast.18), calls=%async_computation.1 | async-start | bytes 786432 | tf_op jit(solution)/shard_map/all_to_all | solution.py:178
  117.3 0.5 iota_compare_fusion.7
  117.9 0.8 copy.88
  118.7 0.3 reshape.263
  119.1 3.1 %fusion.77 = (f32[96,2,8]{2,1,0:T(2,128)}, f32[96,2,1,8,64]{4,3,1,0,2:T(8,128)S(1)}) fusion(bf16[96,2,8,128]{3,2,1,0:T(8,128)(2,1)S(1)} %reshape.263, bf16[96,64,128]{2,1,0:T(8,128)(2,1)} %param.17, pred[96,64]{1,0:T(8,128)(4,1)S(1)} %iota_compare_fusion.4), kind=kOutput, calls=%fused_computation.104 | convolution fusion | flops 25459200 | bytes 2371584 | tf_op jit(solution)/shard_map/rthgd,rjhd->rthgj/dot_general | solution.py:49
  122.2 8.0 %all-to-all-done.1 = f32[32,24,128]{2,1,0:T(8,128)S(1)} async-done(((f32[32,24,128]{2,1,0:T(8,128)}), f32[32,24,128]{2,1,0:T(8,128)S(1)}, u32[]{:S(2)}, u32[]{:S(2)}) %all-to-all-start.1) | async-done | bytes 393248 | tf_op jit(solution)/shard_map/all_to_all | solution.py:178
  130.3 0.7 gather_fusion
  131.0 0.1 gather.7
  131.1 0.1 copy.87
  131.3 1.0 select_add_fusion
  132.3 0.3 fusion.87
  132.6 0.3 fusion.56
  132.9 0.3 fusion.86
  133.3 0.3 fusion.85
  133.6 0.7 copy.95
  134.4 0.7 copy.96
  135.2 0.1 copy.102
  135.4 2.5 %fusion.78 = (f32[96,2,8]{2,1,0:T(2,128)S(1)}, f32[96,2,1,8,2]{3,4,1,0,2:T(2,128)S(1)}) fusion(bf16[96,2,128,1]{2,1,3,0:T(2,128)(2,1)S(1)} %copy.102, bf16[96,2,8,128]{3,2,1,0:T(8,128)(2,1)S(1)} %reshape.263, pred[2,2]{1,0:T(4,128)(4,1)} %iota_compare_fusion.7), kind=kOutput, calls=%fused_computation.105 | convolution fusion | flops 794112 | bytes 460804 | tf_op jit(solution)/shard_map/rthgd,rshd->rthgs/dot_general | solution.py:55
  138.0 0.6 fusion.41
  138.6 0.4 fusion.46
  139.0 0.4 fusion.47
  139.4 0.6 fusion.33
  140.1 0.8 convert_element_type.123
  (41 shorter events, 0.9 us)
Async XLA Ops:
  7.2 132.3 %copy-start = (bf16[96,64,128]{2,1,0:T(8,128)(2,1)S(1)}, bf16[96,64,128]{2,1,0:T(8,128)(2,1)}, u32[]{:S(2)}) copy-start(bf16[96,64,128]{2,1,0:T(8,128)(2,1)} %param.18) | copy-start | bytes 4718596
  7.2 5.4 %copy-start.8 = (s32[96]{0:T(128)S(1)}, s32[96]{0:T(128)}, u32[]{:S(2)}) copy-start(s32[96]{0:T(128)} %param.15) | copy-start | bytes 1156
  7.2 5.9 %copy-start.6 = (bf16[8192]{0:T(1024)(128)(2,1)S(1)}, bf16[8192]{0:T(1024)(128)(2,1)}, u32[]{:S(2)}) copy-start(bf16[8192]{0:T(1024)(128)(2,1)} %param.11) | copy-start | bytes 49156
  16.6 39.5 %all-to-all-start = ((bf16[32,13,1024]{2,1,0:T(8,128)(2,1)}), bf16[32,13,1024]{2,1,0:T(8,128)(2,1)S(1)}, u32[]{:S(2)}, u32[]{:S(2)}) async-start(bf16[32,13,1024]{2,1,0:T(8,128)(2,1)} %fusion.38), calls=%async_computation | async-start | bytes 2097152 | tf_op jit(solution)/shard_map/all_to_all | solution.py:148
  28.1 61.0 %all-reduce.4.cloned.1.call-start = ((), (), s32[]{:S(2)}) async-start(), calls=%async_computation.2 | async-start | bytes 393216 | tf_op jit(solution)/shard_map/psum | solution.py:160
  28.3 10.0 %copy-start.1 = (bf16[8192,2,128]{2,1,0:T(2,128)(2,1)S(1)}, bf16[8192,2,128]{2,1,0:T(2,128)(2,1)}, u32[]{:S(2)}) copy-start(bf16[8192,2,128]{2,1,0:T(2,128)(2,1)} %param.12) | copy-start | bytes 12582916
  56.3 49.6 %copy-start.5 = (bf16[4,2,64,128]{3,2,1,0:T(8,128)(2,1)S(1)}, bf16[4,2,64,128]{3,2,1,0:T(8,128)(2,1)}, u32[]{:S(2)}) copy-start(bf16[4,2,64,128]{3,2,1,0:T(8,128)(2,1)} %param.14) | copy-start | bytes 393220
  59.4 58.5 %copy-start.4 = (f32[96,2,2,128]{3,0,2,1:T(8,128)S(1)}, f32[96,2,2,128]{3,0,2,1:T(8,128)}, u32[]{:S(2)}) copy-start(f32[96,2,2,128]{3,0,2,1:T(8,128)} %fusion.4) | copy-start | bytes 589828
  59.4 59.3 %copy-start.3 = (bf16[96,2,1024]{2,1,0:T(2,128)(2,1)S(1)}, bf16[96,2,1024]{2,1,0:T(2,128)(2,1)}, u32[]{:S(2)}) copy-start(bf16[96,2,1024]{2,1,0:T(2,128)(2,1)} %param.16) | copy-start | bytes 1179652
  59.4 59.5 %copy-start.7 = (s32[96]{0:T(128)S(1)}, s32[96]{0:T(128)}, u32[]{:S(2)}) copy-start(s32[96]{0:T(128)} %param.19) | copy-start | bytes 1156
  107.5 22.7 %all-to-all-start.1 = ((f32[32,24,128]{2,1,0:T(8,128)}), f32[32,24,128]{2,1,0:T(8,128)S(1)}, u32[]{:S(2)}, u32[]{:S(2)}) async-start(f32[32,24,128]{2,1,0:T(8,128)} %bitcast.18), calls=%async_computation.1 | async-start | bytes 786432 | tf_op jit(solution)/shard_map/all_to_all | solution.py:178
  131.0 6.9 %copy-start.2 = (f32[96,2,8]{2,1,0:T(2,128)S(1)}, f32[96,2,8]{2,1,0:T(2,128)}, u32[]{:S(2)}) copy-start(f32[96,2,8]{2,1,0:T(2,128)} %get-tuple-element.24) | copy-start | bytes 18436
Sparse Core Ops, SparseCore 0:
  59.6 29.3 all-reduce.3

commit v6 on v2

--- a/solution.py
+++ b/solution.py
@@ -28,7 +28,15 @@
 
 def normalize(hidden, input_norm_gain):
     values = hidden.astype(jnp.float32)
-    meansq = jnp.mean(values * values, axis=-1, keepdims=True)
+    square_grid = jnp.einsum("rtd,sud->rtsu", hidden, hidden, preferred_element_type=jnp.float32)
+    row_index = jnp.arange(row_count, dtype=jnp.int32)
+    token_index = jnp.arange(token_count, dtype=jnp.int32)
+    diagonal = (row_index[:, None, None, None] == row_index[None, None, :, None]) & (
+        token_index[None, :, None, None] == token_index[None, None, None, :]
+    )
+    meansq = (
+        jnp.sum(jnp.where(diagonal, square_grid, 0.0), axis=(2, 3))[..., None] / model_width
+    )
     return (values * lax.rsqrt(meansq + epsilon) * input_norm_gain.astype(jnp.float32)).astype(
         jnp.bfloat16
     )
@@ -52,7 +60,11 @@
     slot_live = jnp.arange(context, dtype=jnp.int32)[None, :] < cached_length[:, None]
     cache_scores = jnp.where(slot_live[:, None, None, None, :], cache_scores, -1e30)
     fresh_scores = (
-        jnp.einsum("rthgd,rshd->rthgs", query_vecs, fresh_vecs, preferred_element_type=jnp.float32)
+        jnp.sum(
+            query_vecs.astype(jnp.float32)[:, :, :, :, None, :]
+            * jnp.moveaxis(fresh_vecs.astype(jnp.float32), 1, 2)[:, None, :, None, :, :],
+            axis=-1,
+        )
         * score_scale
     )
     causal = (
@@ -104,7 +116,15 @@
     slot_total = owner_count * cap
 
     values = hidden.astype(jnp.float32)
-    meansq = jnp.mean(values * values, axis=-1, keepdims=True)
+    square_grid = jnp.einsum("rtd,sud->rtsu", hidden, hidden, preferred_element_type=jnp.float32)
+    row_index = jnp.arange(row_count, dtype=jnp.int32)
+    token_index = jnp.arange(token_count, dtype=jnp.int32)
+    diagonal = (row_index[:, None, None, None] == row_index[None, None, :, None]) & (
+        token_index[None, :, None, None] == token_index[None, None, None, :]
+    )
+    meansq = (
+        jnp.sum(jnp.where(diagonal, square_grid, 0.0), axis=(2, 3))[..., None] / model_width
+    )
     row_scale = lax.rsqrt(meansq + epsilon)
     normed_input = (values * row_scale * input_norm_gain.astype(jnp.float32)).astype(jnp.bfloat16)
     base_proj = jnp.dot(

time: 115 us -> 124 us (1.078)
  matrix products: 17.3 us -> 25.1 us
  local copies, waits for them, and re-layouts: 16.1 us -> 21 us
  other arithmetic: 22.9 us -> 18.2 us
    dot_general x1, matrix products: 2.52 us -> 9.55 us  [body(): jnp.einsum('rtd,sud->rtsu', hidden, hidden, preferred_element_type=jnp.fl...]
    reduce_sum x1, other arithmetic: 5.33 us -> 0.64 us  [attend(): jnp.sum(query_vecs.astype(jnp.float32)[:, :, :, :, None, :] * jnp.moveaxi...]
    gather x3, local copies, waits for them, and re-layouts: 0.96 us -> 4.17 us  [body(): jnp.take(delta_rows, slot_of, axis=0)]
  transfers between devices with their start and end apart: 2 -> 2, of which waited for: 2 -> 2; matrix products, arithmetic and copies ran while one was open for 28% -> 25% of each run, Pallas kernels for 0% -> 0%
where the time goes in v6:
time: 124 us; the launch traced here: 123 us
  matrix products  25.1 us (20%)
  blocking collectives  23.7 us (19%)
  starting transfers between devices  21.3 us (17%)
  local copies, waits for them, and re-layouts  21 us (17%)
  other arithmetic  18.2 us (15%)
  waiting for transfers between devices  12.8 us (10%)
    psum x1, blocking collectives, body(): rank_hidden = lax.psum(partial_rank, 'tensor').astype(jnp.bfloat16)  23.7 us
    all_to_all x1, starting transfers between devices, body(): recv = lax.all_to_all(send, 'adapter', 0, 0, tiled=True)  11.7 us
    all_to_all x1, waiting for transfers between devices, body(): delta_recv = lax.all_to_all(delta_send, 'adapter', 0, 0, tiled=True)  11.6 us
    convert_element_type x1, other arithmetic, body(): (values * row_scale * input_norm_gain.astype(jnp.float32)).astype(jnp.bfl...  9.97 us
    all_to_all x1, starting transfers between devices, body(): delta_recv = lax.all_to_all(delta_send, 'adapter', 0, 0, tiled=True)  9.66 us
    dot_general x1, matrix products, body(): jnp.einsum('rtd,sud->rtsu', hidden, hidden, preferred_element_type=jnp.fl...  9.55 us
    dot_general x1, matrix products, body(): jnp.dot(normed_input.reshape(row_count * token_count, model_width), key_v...  7.75 us
    dot_general x1, local copies, waits for them, and re-layouts, body(): jnp.dot(normed_input.reshape(row_count * token_count, model_width), key_v...  6.37 us
  transfers between devices with their start and end apart: 2, of which 2 were waited for; matrix products, arithmetic and copies ran while one was open for 25% of the time, Pallas kernels for 0%

profile of v6, /device:TPU:6, one launch (start us, length us, event | category | flops | bytes accessed | tf_op | source)
XLA Modules:
  0.0 123.2 jit_solution(3269194863437971899)
XLA Ops:
  0.7 9.6 %fusion.42 = f32[96,2]{0,1:T(2,128)S(1)} fusion(bf16[96,2,8192]{2,1,0:T(2,128)(2,1)} %param.10, bf16[96,2,8192,1]{2,1,0,3:T(2,128)(2,1)} %bitcast.154, pred[2,2]{1,0:T(4,128)(4,1)S(1)} %iota_compare_fusion.9, pred[96,96]{0,1:T(8,128)(4,1)S(1)} %iota_compare_fusion.6), kind=kOutput, calls=%fused_computation.31 | convolution fusion | flops 604090176 | bytes 6301444 | tf_op jit(solution)/shard_map/rtd,sud->rtsu/dot_general | solution.py:119
  10.3 0.1 copy.93
  10.4 0.2 convert_reduce_fusion
  10.6 0.5 compare_and_fusion
  11.1 0.1 fusion.59
  11.3 0.1 reshape.359
  11.4 1.5 %multiply_convert_fusion.1 = bf16[96,2,1024]{2,1,0:T(2,128)(2,1)S(1)} fusion(f32[1024]{0:T(1024)S(1)} %dynamic-slice_convert_fusion, f32[96,2]{1,0:T(8,128)S(1)} %copy.93, bf16[96,2,8192]{2,1,0:T(2,128)(2,1)} %param.10, s32[]{:T(128)S(6)} %select_n.46), kind=kLoop, calls=%fused_computation.37 | loop fusion | flops 786432 | bytes 791300 | tf_op jit(solution)/shard_map/convert_element_type | solution.py:153
  13.0 0.3 convolution_convert_fusion
  13.4 0.4 reshape.327
  13.7 1.1 fusion.47
  14.9 11.7 %all-to-all-start = ((bf16[32,13,1024]{2,1,0:T(8,128)(2,1)}), bf16[32,13,1024]{2,1,0:T(8,128)(2,1)S(1)}, u32[]{:S(2)}, u32[]{:S(2)}) async-start(bf16[32,13,1024]{2,1,0:T(8,128)(2,1)} %fusion.47), calls=%async_computation | async-start | bytes 2097152 | tf_op jit(solution)/shard_map/all_to_all | solution.py:168
  26.6 10.0 %fusion = bf16[96,2,8192,1]{2,1,0,3:T(2,128)(2,1)} fusion(bf16[96,2,8192]{2,1,0:T(2,128)(2,1)} %param.10, f32[8192]{0:T(1024)S(1)} %convert_element_type.124, f32[96,2]{1,0:T(8,128)S(1)} %copy.93), kind=kLoop, calls=%fused_computation.3 | loop fusion | flops 6291456 | bytes 6324992 | tf_op jit(solution)/shard_map/convert_element_type | solution.py:129
  36.6 2.5 %copy.152 = bf16[1024,8,2,128]{3,1,2,0:T(8,128)(2,1)} copy(bf16[1024,8,2,128]{3,2,1,0:T(2,128)(2,1)S(1)} %bitcast.152) | data formatting | bytes 8388608
  39.1 6.4 %copy.94 = bf16[256,8192]{1,0:T(8,128)(2,1)} copy(bf16[256,8192]{0,1:T(8,128)(2,1)} %bitcast.150) | data formatting | bytes 8388608 | tf_op jit(solution)/shard_map/dot_general | solution.py:130
  45.5 7.7 %fusion.1 = f32[96,2,2,128]{3,0,2,1:T(8,128)} fusion(bf16[2,128,8192,1]{2,1,0,3:T(8,128)(2,1)} %bitcast.153, bf16[96,2,8192,1]{2,1,0,3:T(2,128)(2,1)} %fusion), kind=kOutput, calls=%fused_computation.4 | convolution fusion | flops 805306368 | bytes 7536640 | tf_op jit(solution)/shard_map/dot_general | solution.py:130
  53.2 1.2 all-to-all-done
  54.5 0.1 reshape.334
  54.6 0.6 reshape.329
  55.3 2.5 %fusion.27 = f32[192,2,128]{2,0,1:T(8,128)} fusion(bf16[4,1024,128]{2,1,0:T(8,128)(2,1)} %param.13, bf16[192,2,1024,1]{2,1,0,3:T(2,128)(2,1)S(1)} %bitcast.157, f32[192,4]{0,1:T(4,128)S(1)} %get-tuple-element.22), kind=kOutput, calls=%fused_computation.24 | convolution fusion | flops 402997248 | bytes 2034688 | tf_op jit(solution)/shard_map/euz,nzs->euns/dot_general | solution.py:176
  57.8 23.7 %all-reduce.2 = bf16[192,2,128]{2,0,1:T(8,128)(2,1)S(1)} all-reduce(f32[192,2,128]{2,0,1:T(8,128)} %fusion.27), channel_id=1, replica_groups=mesh['adapter'=32,'tensor'=8] {'tensor'}, use_global_device_ids=true, to_apply=%region_3.4 | all-reduce | flops 49152 | bytes 294912 | tf_op jit(solution)/shard_map/psum | solution.py:180
  81.5 0.1 copy.99
  81.6 0.2 convolution_bitcast_fusion
  81.9 0.2 convolution_bitcast_fusion.1
  82.2 1.1 copy.102
  83.2 9.7 %all-to-all-start.1 = ((f32[32,24,128]{2,1,0:T(8,128)}), f32[32,24,128]{2,1,0:T(8,128)}, u32[]{:S(2)}, u32[]{:S(2)}) async-start(f32[32,24,128]{2,1,0:T(8,128)} %bitcast.20), calls=%async_computation.1 | async-start | bytes 786432 | tf_op jit(solution)/shard_map/all_to_all | solution.py:198
  92.9 0.8 copy.104
  93.8 0.3 reshape.332
  94.2 3.1 %fusion.89 = (f32[96,2,8]{2,1,0:T(2,128)}, f32[96,2,1,8,64]{4,3,1,0,2:T(8,128)S(1)}) fusion(bf16[96,2,8,128]{3,2,1,0:T(8,128)(2,1)S(1)} %reshape.332, bf16[96,64,128]{2,1,0:T(8,128)(2,1)} %param.17, pred[96,64]{1,0:T(8,128)(4,1)S(1)} %iota_compare_fusion.4), kind=kOutput, calls=%fused_computation.110 | convolution fusion | flops 25459200 | bytes 2371584 | tf_op jit(solution)/shard_map/rthgd,rjhd->rthgj/dot_general | solution.py:57
  97.3 11.6 %all-to-all-done.1 = f32[32,24,128]{2,1,0:T(8,128)} async-done(((f32[32,24,128]{2,1,0:T(8,128)}), f32[32,24,128]{2,1,0:T(8,128)}, u32[]{:S(2)}, u32[]{:S(2)}) %all-to-all-start.1) | async-done | bytes 393248 | tf_op jit(solution)/shard_map/all_to_all | solution.py:198
  108.9 1.1 reshape.331
  110.0 1.4 %gather_fusion = f32[96,512]{1,0:T(8,128)} fusion(f32[192,512]{1,0:T(8,128)S(1)} %reshape.331, s32[1024]{0:T(1024)S(1)} %pad_clamp_fusion), kind=kCustom, calls=%fused_computation | custom fusion | bytes 393600 | tf_op jit(solution)/shard_map/jit(_take)/gather | solution.py:200
  111.4 1.8 %gather.7 = f32[96,2,2,128]{3,2,1,0:T(2,128)} reshape(f32[96,512]{1,0:T(8,128)} %gather_fusion) | data formatting | bytes 393216 | tf_op jit(solution)/shard_map/jit(_take)/gather | solution.py:200
  113.1 1.0 copy.103
  114.2 1.0 select_add_fusion
  115.1 0.3 fusion.96
  115.5 0.3 fusion.65
  115.8 0.3 fusion.95
  116.2 0.3 fusion.94
  116.5 0.7 copy.111
  117.2 0.7 copy.112
  118.0 0.7 copy.120
  118.8 0.6 multiply_reduce_fusion
  119.5 0.4 fusion.80
  120.0 0.5 fusion.55
  120.5 0.6 fusion.50
  121.2 0.5 fusion.56
  121.7 0.6 fusion.34
  122.3 0.8 convert_element_type.149
  (45 shorter events, 0.8 us)
Async XLA Ops:
  0.6 121.1 %copy-start = (bf16[96,64,128]{2,1,0:T(8,128)(2,1)S(1)}, bf16[96,64,128]{2,1,0:T(8,128)(2,1)}, u32[]{:S(2)}) copy-start(bf16[96,64,128]{2,1,0:T(8,128)(2,1)} %param.18) | copy-start | bytes 4718596
  0.7 9.7 %copy-start.9 = (s32[96]{0:T(128)S(1)}, s32[96]{0:T(128)}, u32[]{:S(2)}) copy-start(s32[96]{0:T(128)} %param.15) | copy-start | bytes 1156
  0.7 10.7 %copy-start.7 = (bf16[8192]{0:T(1024)(128)(2,1)S(1)}, bf16[8192]{0:T(1024)(128)(2,1)}, u32[]{:S(2)}) copy-start(bf16[8192]{0:T(1024)(128)(2,1)} %param.11) | copy-start | bytes 49156
  14.9 39.5 %all-to-all-start = ((bf16[32,13,1024]{2,1,0:T(8,128)(2,1)}), bf16[32,13,1024]{2,1,0:T(8,128)(2,1)S(1)}, u32[]{:S(2)}, u32[]{:S(2)}) async-start(bf16[32,13,1024]{2,1,0:T(8,128)(2,1)} %fusion.47), calls=%async_computation | async-start | bytes 2097152 | tf_op jit(solution)/shard_map/all_to_all | solution.py:168
  26.6 10.0 %copy-start.1 = (bf16[8192,2,128]{2,1,0:T(2,128)(2,1)S(1)}, bf16[8192,2,128]{2,1,0:T(2,128)(2,1)}, u32[]{:S(2)}) copy-start(bf16[8192,2,128]{2,1,0:T(2,128)(2,1)} %param.12) | copy-start | bytes 12582916
  53.2 28.4 %copy-start.5 = (bf16[4,2,64,128]{3,2,1,0:T(8,128)(2,1)S(1)}, bf16[4,2,64,128]{3,2,1,0:T(8,128)(2,1)}, u32[]{:S(2)}) copy-start(bf16[4,2,64,128]{3,2,1,0:T(8,128)(2,1)} %param.14) | copy-start | bytes 393220
  55.2 37.7 %copy-start.4 = (f32[96,2,2,128]{3,0,2,1:T(8,128)S(1)}, f32[96,2,2,128]{3,0,2,1:T(8,128)}, u32[]{:S(2)}) copy-start(f32[96,2,2,128]{3,0,2,1:T(8,128)} %fusion.1) | copy-start | bytes 589828
  57.8 36.0 %copy-start.3 = (bf16[96,2,1024]{2,1,0:T(2,128)(2,1)S(1)}, bf16[96,2,1024]{2,1,0:T(2,128)(2,1)}, u32[]{:S(2)}) copy-start(bf16[96,2,1024]{2,1,0:T(2,128)(2,1)} %param.16) | copy-start | bytes 1179652
  81.6 12.5 %copy-start.8 = (s32[96]{0:T(128)S(1)}, s32[96]{0:T(128)}, u32[]{:S(2)}) copy-start(s32[96]{0:T(128)} %param.19) | copy-start | bytes 1156
  83.2 25.7 %all-to-all-start.1 = ((f32[32,24,128]{2,1,0:T(8,128)}), f32[32,24,128]{2,1,0:T(8,128)}, u32[]{:S(2)}, u32[]{:S(2)}) async-start(f32[32,24,128]{2,1,0:T(8,128)} %bitcast.20), calls=%async_computation.1 | async-start | bytes 786432 | tf_op jit(solution)/shard_map/all_to_all | solution.py:198
  111.3 8.6 %copy-start.2 = (f32[96,2,8]{2,1,0:T(2,128)S(1)}, f32[96,2,8]{2,1,0:T(2,128)}, u32[]{:S(2)}) copy-start(f32[96,2,8]{2,1,0:T(2,128)} %get-tuple-element.24) | copy-start | bytes 18436
  118.8 2.3 %copy-start.6 = (bf16[96,2,128,1]{2,1,3,0:T(2,128)(2,1)S(1)}, bf16[96,2,128,1]{2,1,3,0:T(2,128)(2,1)}, u32[]{:S(2)}) copy-start(bf16[96,2,128,1]{2,1,3,0:T(2,128)(2,1)} %copy.120) | copy-start | bytes 147460

commit v7 on v2

--- a/solution.py
+++ b/solution.py
@@ -161,19 +161,17 @@
 
     rank_selector = selector.astype(jnp.bfloat16)
     masked = rank_hidden[:, :, None, :] * rank_selector[:, None, :, None]
-    key_part = jnp.einsum(
-        "gled,edb->glb",
-        masked[..., :rank_width],
-        adapter_up_weight[:, 0],
-        preferred_element_type=jnp.float32,
-    )
-    value_part = jnp.einsum(
-        "gled,edb->glb",
-        masked[..., rank_width:],
-        adapter_up_weight[:, 1],
-        preferred_element_type=jnp.float32,
-    )
-    delta_slots = jnp.stack([key_part, value_part], axis=2)
+    up_zero = jnp.zeros_like(adapter_up_weight[:, 0])
+    up_blocks = jnp.stack(
+        [
+            jnp.concatenate([adapter_up_weight[:, 0], up_zero], axis=1),
+            jnp.concatenate([up_zero, adapter_up_weight[:, 1]], axis=1),
+        ],
+        axis=2,
+    )
+    delta_slots = jnp.einsum(
+        "gled,edkb->glkb", masked, up_blocks, preferred_element_type=jnp.float32
+    )
     delta_send = delta_slots.reshape(owner_count, cap * token_count * 2, column_count)
     delta_recv = lax.all_to_all(delta_send, "adapter", 0, 0, tiled=True)
     delta_rows = delta_recv.reshape(slot_total, token_count * 2 * column_count)

time: 115 us -> 115 us (level)
    unnamed x24 -> x28, local copies, waits for them, and re-layouts: 4.12 us -> 4.13 us
where the time goes in v7:
time: 115 us
  blocking collectives  23.8 us (21%)
  other arithmetic  23.4 us (20%)
  starting transfers between devices  21.2 us (18%)
  matrix products  17.2 us (15%)
  local copies, waits for them, and re-layouts  16.7 us (15%)
  waiting for transfers between devices  11.6 us (10%)
    psum x1, blocking collectives, body(): rank_hidden = lax.psum(partial_rank, 'tensor').astype(jnp.bfloat16)  23.8 us
    all_to_all x1, starting transfers between devices, body(): recv = lax.all_to_all(send, 'adapter', 0, 0, tiled=True)  11.7 us
    all_to_all x1, waiting for transfers between devices, body(): delta_recv = lax.all_to_all(delta_send, 'adapter', 0, 0, tiled=True)  11.2 us
    convert_element_type x1, other arithmetic, body(): (values * row_scale * input_norm_gain.astype(jnp.float32)).astype(jnp.bfl...  9.97 us
    all_to_all x1, starting transfers between devices, body(): delta_recv = lax.all_to_all(delta_send, 'adapter', 0, 0, tiled=True)  9.54 us
    dot_general x1, matrix products, body(): jnp.dot(normed_input.reshape(row_count * token_count, model_width), key_v...  7.74 us
    dot_general x1, local copies, waits for them, and re-layouts, body(): jnp.dot(normed_input.reshape(row_count * token_count, model_width), key_v...  6.4 us
    reduce_sum x1, other arithmetic, body(): meansq = jnp.mean(values * values, axis=-1, keepdims=True)  5.33 us
  transfers between devices with their start and end apart: 2, of which 2 were waited for; matrix products, arithmetic and copies ran while one was open for 28% of the time, Pallas kernels for 0%

profile of v7, /device:TPU:6, one launch (start us, length us, event | category | flops | bytes accessed | tf_op | source)
XLA Modules:
  0.0 114.9 jit_solution(17234377399833465328)
XLA Ops:
  0.7 5.3 %fusion = f32[96,2]{1,0:T(8,128)S(1)} fusion(bf16[96,2,8192]{2,1,0:T(2,128)(2,1)} %param.10), kind=kLoop, calls=%fused_computation.3 | loop fusion | flops 4718400 | bytes 3146496 | tf_op jit(solution)/shard_map/reduce_sum | solution.py:107
  6.0 0.2 convert_reduce_fusion
  6.2 0.5 compare_and_fusion
  6.8 0.1 fusion.54
  6.9 0.1 reshape.289
  7.1 1.5 %multiply_convert_fusion = bf16[96,2,1024]{2,1,0:T(2,128)(2,1)S(1)} fusion(f32[1024]{0:T(1024)S(1)} %dynamic-slice_convert_fusion, f32[96,2]{1,0:T(8,128)S(1)} %add_rsqrt_fusion, bf16[96,2,8192]{2,1,0:T(2,128)(2,1)} %param.10, s32[]{:T(128)S(6)} %select_n.31), kind=kLoop, calls=%fused_computation.36 | loop fusion | flops 786432 | bytes 791300 | tf_op jit(solution)/shard_map/convert_element_type | solution.py:133
  8.7 0.4 convolution_convert_fusion
  9.0 0.4 reshape.258
  9.4 1.1 fusion.38
  10.5 11.7 %all-to-all-start = ((bf16[32,13,1024]{2,1,0:T(8,128)(2,1)}), bf16[32,13,1024]{2,1,0:T(8,128)(2,1)S(1)}, u32[]{:S(2)}, u32[]{:S(2)}) async-start(bf16[32,13,1024]{2,1,0:T(8,128)(2,1)} %fusion.38), calls=%async_computation | async-start | bytes 2097152 | tf_op jit(solution)/shard_map/all_to_all | solution.py:148
  22.2 10.0 %fusion.3 = bf16[96,2,8192,1]{2,1,0,3:T(2,128)(2,1)} fusion(bf16[96,2,8192]{2,1,0:T(2,128)(2,1)} %param.10, f32[8192]{0:T(1024)S(1)} %convert_element_type.100, f32[96,2]{1,0:T(8,128)S(1)} %add_rsqrt_fusion), kind=kLoop, calls=%fused_computation.7 | loop fusion | flops 6291456 | bytes 6324992 | tf_op jit(solution)/shard_map/convert_element_type | solution.py:109
  32.2 2.5 %copy.103 = bf16[1024,8,2,128]{3,1,2,0:T(8,128)(2,1)} copy(bf16[1024,8,2,128]{3,2,1,0:T(2,128)(2,1)S(1)} %bitcast.160) | data formatting | bytes 8388608
  34.7 6.4 %copy.61 = bf16[256,8192]{1,0:T(8,128)(2,1)} copy(bf16[256,8192]{0,1:T(8,128)(2,1)} %bitcast.158) | data formatting | bytes 8388608 | tf_op jit(solution)/shard_map/dot_general | solution.py:110
  41.2 0.7 pad_bitcast_fusion
  41.9 7.7 %fusion.4 = f32[96,2,2,128]{3,0,2,1:T(8,128)} fusion(bf16[2,128,8192,1]{2,1,0,3:T(8,128)(2,1)} %bitcast.161, bf16[96,2,8192,1]{2,1,0,3:T(2,128)(2,1)} %fusion.3), kind=kOutput, calls=%fused_computation.8 | convolution fusion | flops 805306368 | bytes 7536640 | tf_op jit(solution)/shard_map/dot_general | solution.py:110
  49.6 0.5 all-to-all-done
  50.1 0.1 reshape.266
  50.3 0.6 fusion.71
  50.8 0.6 reshape.260
  51.5 1.9 %fusion.26 = f32[192,2,128]{2,0,1:T(8,128)S(1)} fusion(bf16[4,1024,128]{2,1,0:T(8,128)(2,1)} %param.13, bf16[192,2,1024,1]{2,1,0,3:T(2,128)(2,1)S(1)} %bitcast.164, f32[192,4]{0,1:T(4,128)S(1)} %get-tuple-element.21), kind=kOutput, calls=%fused_computation.23 | convolution fusion | flops 402997248 | bytes 2034688 | tf_op jit(solution)/shard_map/euz,nzs->euns/dot_general | solution.py:156
  53.4 23.8 %all-reduce.4 = bf16[192,2,128]{2,0,1:T(8,128)(2,1)S(1)} all-reduce(f32[192,2,128]{2,0,1:T(8,128)S(1)} %fusion.26), channel_id=1, replica_groups=mesh['adapter'=32,'tensor'=8] {'tensor'}, use_global_device_ids=true, to_apply=%region_3.4 | all-reduce | flops 49152 | bytes 294912 | tf_op jit(solution)/shard_map/psum | solution.py:160
  77.2 0.3 convolution_bitcast_fusion
  77.6 1.1 copy.67
  78.6 9.5 %all-to-all-start.1 = ((f32[32,24,128]{2,1,0:T(8,128)}), f32[32,24,128]{2,1,0:T(8,128)S(1)}, u32[]{:S(2)}, u32[]{:S(2)}) async-start(f32[32,24,128]{2,1,0:T(8,128)} %bitcast.17), calls=%async_computation.1 | async-start | bytes 786432 | tf_op jit(solution)/shard_map/all_to_all | solution.py:176
  88.2 0.5 iota_compare_fusion.7
  88.7 0.8 copy.69
  89.6 0.3 reshape.263
  89.8 0.1 iota_compare_fusion.4
  89.9 3.1 %fusion.78 = (f32[96,2,8]{2,1,0:T(2,128)}, f32[96,2,1,8,64]{4,3,1,0,2:T(8,128)S(1)}) fusion(bf16[96,2,8,128]{3,2,1,0:T(8,128)(2,1)S(1)} %reshape.263, bf16[96,64,128]{2,1,0:T(8,128)(2,1)} %param.17, pred[96,64]{1,0:T(8,128)(4,1)S(1)} %iota_compare_fusion.4), kind=kOutput, calls=%fused_computation.107 | convolution fusion | flops 25459200 | bytes 2371584 | tf_op jit(solution)/shard_map/rthgd,rjhd->rthgj/dot_general | solution.py:49
  93.0 11.2 %all-to-all-done.1 = f32[32,24,128]{2,1,0:T(8,128)S(1)} async-done(((f32[32,24,128]{2,1,0:T(8,128)}), f32[32,24,128]{2,1,0:T(8,128)S(1)}, u32[]{:S(2)}, u32[]{:S(2)}) %all-to-all-start.1) | async-done | bytes 393248 | tf_op jit(solution)/shard_map/all_to_all | solution.py:176
  104.3 0.7 gather_fusion
  105.0 0.1 gather.7
  105.1 0.1 copy.68
  105.3 1.0 select_add_fusion
  106.2 0.3 fusion.88
  106.6 0.3 fusion.60
  106.9 0.3 fusion.87
  107.2 0.3 fusion.86
  107.6 0.7 copy.76
  108.3 0.7 copy.77
  109.1 0.1 copy.85
  109.2 0.1 copy.83
  109.3 2.5 %fusion.79 = (f32[96,2,8]{2,1,0:T(2,128)S(1)}, f32[96,2,1,8,2]{3,4,1,0,2:T(2,128)S(1)}) fusion(bf16[96,2,128,1]{2,1,3,0:T(2,128)(2,1)S(1)} %copy.83, bf16[96,2,8,128]{3,2,1,0:T(8,128)(2,1)S(1)} %reshape.263, pred[2,2]{1,0:T(4,128)(4,1)} %iota_compare_fusion.7), kind=kOutput, calls=%fused_computation.108 | convolution fusion | flops 794112 | bytes 460804 | tf_op jit(solution)/shard_map/rthgd,rshd->rthgs/dot_general | solution.py:55
  111.9 0.6 fusion.41
  112.6 0.4 fusion.50
  113.0 0.4 fusion.51
  113.4 0.6 fusion.33
  114.1 0.8 convert_element_type.123
  (42 shorter events, 0.5 us)
Async XLA Ops:
  0.6 112.8 %copy-start = (bf16[96,64,128]{2,1,0:T(8,128)(2,1)S(1)}, bf16[96,64,128]{2,1,0:T(8,128)(2,1)}, u32[]{:S(2)}) copy-start(bf16[96,64,128]{2,1,0:T(8,128)(2,1)} %param.18) | copy-start | bytes 4718596
  0.6 5.4 %copy-start.11 = (s32[96]{0:T(128)S(1)}, s32[96]{0:T(128)}, u32[]{:S(2)}) copy-start(s32[96]{0:T(128)} %param.15) | copy-start | bytes 1156
  0.7 6.4 %copy-start.7 = (bf16[8192]{0:T(1024)(128)(2,1)S(1)}, bf16[8192]{0:T(1024)(128)(2,1)}, u32[]{:S(2)}) copy-start(bf16[8192]{0:T(1024)(128)(2,1)} %param.11) | copy-start | bytes 49156
  10.5 39.5 %all-to-all-start = ((bf16[32,13,1024]{2,1,0:T(8,128)(2,1)}), bf16[32,13,1024]{2,1,0:T(8,128)(2,1)S(1)}, u32[]{:S(2)}, u32[]{:S(2)}) async-start(bf16[32,13,1024]{2,1,0:T(8,128)(2,1)} %fusion.38), calls=%async_computation | async-start | bytes 2097152 | tf_op jit(solution)/shard_map/all_to_all | solution.py:148
  22.2 10.0 %copy-start.1 = (bf16[8192,2,128]{2,1,0:T(2,128)(2,1)S(1)}, bf16[8192,2,128]{2,1,0:T(2,128)(2,1)}, u32[]{:S(2)}) copy-start(bf16[8192,2,128]{2,1,0:T(2,128)(2,1)} %param.12) | copy-start | bytes 12582916
  34.7 6.4 %copy-start.6 = (bf16[4,2,64,128]{3,2,1,0:T(8,128)(2,1)S(1)}, bf16[4,2,64,128]{3,2,1,0:T(8,128)(2,1)}, u32[]{:S(2)}) copy-start(bf16[4,2,64,128]{3,2,1,0:T(8,128)(2,1)} %param.14) | copy-start | bytes 393220
  50.8 26.4 %copy-start.8 = (bf16[192,4]{0,1:T(4,128)(2,1)S(1)}, bf16[192,4]{0,1:T(4,128)(2,1)}, u32[]{:S(2)}) copy-start(bf16[192,4]{0,1:T(4,128)(2,1)} %get-tuple-element.22) | copy-start | bytes 4612
  51.5 25.8 %copy-start.5 = (bf16[4,128,1,128]{3,1,0,2:T(8,128)(2,1)S(1)}, bf16[4,128,1,128]{3,1,0,2:T(8,128)(2,1)}, u32[]{:S(2)}) copy-start(bf16[4,128,1,128]{3,1,0,2:T(8,128)(2,1)} %get-tuple-element.28) | copy-start | bytes 393220
  51.5 37.2 %copy-start.4 = (f32[96,2,2,128]{3,0,2,1:T(8,128)S(1)}, f32[96,2,2,128]{3,0,2,1:T(8,128)}, u32[]{:S(2)}) copy-start(f32[96,2,2,128]{3,0,2,1:T(8,128)} %fusion.4) | copy-start | bytes 589828
  51.5 38.1 %copy-start.3 = (bf16[96,2,1024]{2,1,0:T(2,128)(2,1)S(1)}, bf16[96,2,1024]{2,1,0:T(2,128)(2,1)}, u32[]{:S(2)}) copy-start(bf16[96,2,1024]{2,1,0:T(2,128)(2,1)} %param.16) | copy-start | bytes 1179652
  51.5 38.3 %copy-start.10 = (s32[96]{0:T(128)S(1)}, s32[96]{0:T(128)}, u32[]{:S(2)}) copy-start(s32[96]{0:T(128)} %param.19) | copy-start | bytes 1156
  78.6 25.6 %all-to-all-start.1 = ((f32[32,24,128]{2,1,0:T(8,128)}), f32[32,24,128]{2,1,0:T(8,128)S(1)}, u32[]{:S(2)}, u32[]{:S(2)}) async-start(f32[32,24,128]{2,1,0:T(8,128)} %bitcast.17), calls=%async_computation.1 | async-start | bytes 786432 | tf_op jit(solution)/shard_map/all_to_all | solution.py:176
  89.8 15.4 %copy-start.9 = (pred[96]{0:T(512)(128)(4,1)S(1)}, pred[96]{0:T(512)(128)(4,1)}, u32[]{:S(2)}) copy-start(pred[96]{0:T(512)(128)(4,1)} %get-tuple-element.15) | copy-start | bytes 292
  105.0 6.9 %copy-start.2 = (f32[96,2,8]{2,1,0:T(2,128)S(1)}, f32[96,2,8]{2,1,0:T(2,128)}, u32[]{:S(2)}) copy-start(f32[96,2,8]{2,1,0:T(2,128)} %get-tuple-element.23) | copy-start | bytes 18436

commit v8 on v5

--- a/solution.py
+++ b/solution.py
@@ -79,6 +79,15 @@
         "rthgs,rshd->rthgd", fresh_probs, fresh_vals, preferred_element_type=jnp.float32
     )
     return mixed_out.reshape(row_total, token_total, query_width).astype(jnp.bfloat16)
+
+
+def exchange(blocks):
+    z_count = lax.axis_size("az")
+    y_count = lax.axis_size("ay")
+    grid = blocks.reshape((z_count, y_count) + blocks.shape[1:])
+    grid = lax.all_to_all(grid, "ay", 1, 1, tiled=True)
+    grid = lax.all_to_all(grid, "az", 0, 0, tiled=True)
+    return grid.reshape(blocks.shape)
 
 
 def body(
@@ -99,7 +108,7 @@
     rank_total = adapter_down_weight.shape[2]
     rank_width = adapter_up_weight.shape[2]
     column_count = key_value_weight.shape[2]
-    owner_count = lax.axis_size("adapter")
+    owner_count = lax.axis_size("az") * lax.axis_size("ay")
     cap = SLOT_CAPACITY
     slot_total = owner_count * cap
 
@@ -145,7 +154,7 @@
         id_row, slot_adapter.reshape(owner_count, 1, cap), (0, 0, 0)
     )
     send = jnp.concatenate([packed, id_row], axis=1)
-    recv = lax.all_to_all(send, "adapter", 0, 0, tiled=True)
+    recv = exchange(send)
 
     got_rows = recv[:, : cap * token_count].reshape(slot_total, token_count, feature_total)
     got_adapter = recv[:, cap * token_count, :cap].reshape(slot_total).astype(jnp.int32)
@@ -157,7 +166,7 @@
         "euz,nzs->euns", got_rows, adapter_down_weight, preferred_element_type=jnp.float32
     )
     partial_rank = jnp.sum(down_all * selector[:, None, :, None], axis=2)
-    rank_hidden = lax.psum(lax.psum(partial_rank, "tc"), "tx").astype(jnp.bfloat16)
+    rank_hidden = lax.psum(partial_rank, ("tx", "tc")).astype(jnp.bfloat16)
 
     rank_selector = selector.astype(jnp.bfloat16)
     masked = rank_hidden[:, :, None, :] * rank_selector[:, None, :, None]
@@ -175,7 +184,7 @@
     )
     delta_slots = jnp.stack([key_part, value_part], axis=2)
     delta_send = delta_slots.reshape(owner_count, cap * token_count * 2, column_count)
-    delta_recv = lax.all_to_all(delta_send, "adapter", 0, 0, tiled=True)
+    delta_recv = exchange(delta_send)
     delta_rows = delta_recv.reshape(slot_total, token_count * 2 * column_count)
     adapter_update = jnp.take(delta_rows, slot_of, axis=0).reshape(
         row_count, token_count, 2, column_count
@@ -199,29 +208,34 @@
 
 
 def solution(mesh):
+    owner_devices = mesh.devices.shape[0]
     tensor_devices = mesh.devices.shape[1]
+    y_count = 4 if owner_devices % 4 == 0 else 1
     core_count = 2 if tensor_devices % 2 == 0 else 1
     split_mesh = Mesh(
-        mesh.devices.reshape(mesh.devices.shape[0], tensor_devices // core_count, core_count),
-        ("adapter", "tx", "tc"),
-    )
+        mesh.devices.reshape(
+            owner_devices // y_count, y_count, tensor_devices // core_count, core_count
+        ),
+        ("az", "ay", "tx", "tc"),
+    )
+    adapter = ("az", "ay")
     tensor = ("tx", "tc")
     in_specs = (
-        P("adapter", None, None),
+        P(adapter, None, None),
         P(),
         P(None, None, tensor),
-        P("adapter", tensor, None),
-        P("adapter", None, None, tensor),
-        P("adapter"),
-        P("adapter", None, tensor),
-        P("adapter", None, tensor),
-        P("adapter", None, tensor),
-        P("adapter"),
+        P(adapter, tensor, None),
+        P(adapter, None, None, tensor),
+        P(adapter),
+        P(adapter, None, tensor),
+        P(adapter, None, tensor),
+        P(adapter, None, tensor),
+        P(adapter),
     )
     out_specs = (
-        P("adapter", None, tensor),
-        P("adapter", None, tensor),
-        P("adapter", None, tensor),
+        P(adapter, None, tensor),
+        P(adapter, None, tensor),
+        P(adapter, None, tensor),
     )
     return jax.shard_map(
         body, mesh=split_mesh, in_specs=in_specs, out_specs=out_specs, check_vma=False

time: 150 us -> 142 us (0.947); the launches traced: 148 us -> 142 us
  between operations: 14.4 us -> 1.18 us
  blocking collectives: 16.7 us -> 23.3 us
  local copies, waits for them, and re-layouts: 16.1 us -> 21.8 us
  waiting for transfers between devices: 37.6 us -> 33.6 us
  starting transfers between devices: 21.6 us -> 23.3 us
  other arithmetic: 23.6 us -> 22 us
    psum x1 -> x0, waiting for transfers between devices: 28.8 us -> none  [body(): lax.psum(partial_rank, 'tc')]
    all_to_all x2 -> x4, waiting for transfers between devices: 8.73 us -> 33.6 us  [the longest x2 22.2 us: exchange(): grid = lax.all_to_all(grid, 'ay', 1, 1, tiled=True)]
    psum x1, blocking collectives: 16.7 us -> 23.3 us  [body(): rank_hidden = lax.psum(partial_rank, ('tx', 'tc')).astype(jnp.bfloat16)]
    all_to_all x0 -> x3, local copies, waits for them, and re-layouts: none -> 2.71 us  [the longest x2 2.33 us: exchange(): grid = lax.all_to_all(grid, 'ay', 1, 1, tiled=True)]
    all_to_all x2 -> x4, starting transfers between devices: 21.3 us -> 23.3 us  [the longest x2 15.4 us: exchange(): grid = lax.all_to_all(grid, 'az', 0, 0, tiled=True)]
    concatenate x0 -> x3, local copies, waits for them, and re-layouts: none -> 1.84 us  [body(): send = jnp.concatenate([packed, id_row], axis=1)]
    another operation x1 -> x3, local copies, waits for them, and re-layouts: 0.25 us -> 1.84 us
    unnamed x22 -> x32, local copies, waits for them, and re-layouts: 4.11 us -> 4.14 us
  transfers between devices with their start and end apart: 3 -> 4, of which waited for: 3 -> 3; matrix products, arithmetic and copies ran while one was open for 22% -> 22% of each run, Pallas kernels for 0% -> 0%
where the time goes in v8:
time: 142 us
  waiting for transfers between devices  33.6 us (24%)
  starting transfers between devices  23.3 us (16%)
  blocking collectives  23.3 us (16%)
  other arithmetic  22 us (15%)
  local copies, waits for them, and re-layouts  21.8 us (15%)
  matrix products  16.6 us (12%)
    psum x1, blocking collectives, body(): rank_hidden = lax.psum(partial_rank, ('tx', 'tc')).astype(jnp.bfloat16)  23.3 us
    all_to_all x2, waiting for transfers between devices, exchange(): grid = lax.all_to_all(grid, 'ay', 1, 1, tiled=True)  22.2 us
    all_to_all x2, starting transfers between devices, exchange(): grid = lax.all_to_all(grid, 'az', 0, 0, tiled=True)  15.4 us
    all_to_all x2, waiting for transfers between devices, exchange(): grid = lax.all_to_all(grid, 'az', 0, 0, tiled=True)  11.5 us
    convert_element_type x1, other arithmetic, body(): (values * row_scale * input_norm_gain.astype(jnp.float32)).astype(jnp.bfl...  9.99 us
    all_to_all x2, starting transfers between devices, exchange(): grid = lax.all_to_all(grid, 'ay', 1, 1, tiled=True)  7.92 us
    dot_general x1, matrix products, body(): jnp.dot(normed_input.reshape(row_count * token_count, model_width), key_v...  7.1 us
    dot_general x1, local copies, waits for them, and re-layouts, body(): jnp.dot(normed_input.reshape(row_count * token_count, model_width), key_v...  6.37 us
  transfers between devices with their start and end apart: 4, of which 3 were waited for; matrix products, arithmetic and copies ran while one was open for 22% of the time, Pallas kernels for 0%

profile of v8, /device:TPU:6, one launch (start us, length us, event | category | flops | bytes accessed | tf_op | source)
XLA Modules:
  0.0 141.8 jit_solution(7021704363049437494)
XLA Ops:
  0.7 5.3 %fusion = f32[96,2]{1,0:T(8,128)S(1)} fusion(bf16[96,2,8192]{2,1,0:T(2,128)(2,1)} %param.10), kind=kLoop, calls=%fused_computation.3 | loop fusion | flops 4718400 | bytes 3146496 | tf_op jit(solution)/shard_map/reduce_sum | solution.py:116
  6.2 0.5 compare_and_fusion
  7.2 1.5 %multiply_convert_fusion = bf16[96,2,1024]{2,1,0:T(2,128)(2,1)S(1)} fusion(f32[1024]{0:T(1024)S(1)} %dynamic-slice_convert_fusion, f32[96,2]{1,0:T(8,128)S(1)} %add_rsqrt_fusion, bf16[96,2,8192]{2,1,0:T(2,128)(2,1)} %param.10, s32[]{:T(128)S(6)} %select_n.31), kind=kLoop, calls=%fused_computation.35 | loop fusion | flops 786432 | bytes 791300 | tf_op jit(solution)/shard_map/convert_element_type | solution.py:142
  8.8 0.4 convolution_convert_fusion
  9.1 0.4 concatenate.20
  9.5 0.3 pad_maximum_fusion
  9.8 1.4 copy.142
  11.2 4.5 %all-to-all-start = ((bf16[8,4,13,1024]{3,0,2,1:T(8,128)(2,1)}), bf16[8,4,13,1024]{3,0,2,1:T(8,128)(2,1)S(1)}, u32[]{:S(2)}, u32[]{:S(2)}) async-start(bf16[8,4,13,1024]{3,0,2,1:T(8,128)(2,1)} %copy.142), calls=%async_computation | async-start | bytes 1703936 | tf_op jit(solution)/shard_map/all_to_all | solution.py:88
  15.7 13.0 %all-to-all-done = bf16[8,4,13,1024]{3,0,2,1:T(8,128)(2,1)S(1)} async-done(((bf16[8,4,13,1024]{3,0,2,1:T(8,128)(2,1)}), bf16[8,4,13,1024]{3,0,2,1:T(8,128)(2,1)S(1)}, u32[]{:S(2)}, u32[]{:S(2)}) %all-to-all-start) | async-done | bytes 852000 | tf_op jit(solution)/shard_map/all_to_all | solution.py:88
  28.7 1.6 %copy.143 = bf16[8,4,13,1024]{3,1,2,0:T(4,128)(2,1)} copy(bf16[8,4,13,1024]{3,0,2,1:T(8,128)(2,1)S(1)} %all-to-all-done) | data formatting | bytes 1703936 | tf_op jit(solution)/shard_map/all_to_all | solution.py:88
  30.2 8.5 %all-to-all-start.1 = ((bf16[8,4,13,1024]{3,1,2,0:T(4,128)(2,1)}), bf16[8,4,13,1024]{3,1,2,0:T(4,128)(2,1)S(1)}, u32[]{:S(2)}, u32[]{:S(2)}) async-start(bf16[8,4,13,1024]{3,1,2,0:T(4,128)(2,1)} %copy.143), calls=%async_computation.1 | async-start | bytes 1703936 | tf_op jit(solution)/shard_map/all_to_all | solution.py:89
  38.7 10.0 %fusion.3 = bf16[96,2,8192,1]{2,1,0,3:T(2,128)(2,1)} fusion(bf16[96,2,8192]{2,1,0:T(2,128)(2,1)} %param.10, f32[8192]{0:T(1024)S(1)} %convert_element_type.100, f32[96,2]{1,0:T(8,128)S(1)} %copy-done.4), kind=kLoop, calls=%fused_computation.7 | loop fusion | flops 6291456 | bytes 6324992 | tf_op jit(solution)/shard_map/convert_element_type | solution.py:118
  48.7 2.5 %copy.188 = bf16[1024,8,2,128]{3,1,2,0:T(8,128)(2,1)} copy(bf16[1024,8,2,128]{3,2,1,0:T(2,128)(2,1)S(1)} %bitcast.163) | data formatting | bytes 8388608
  51.2 6.4 %copy.139 = bf16[256,8192]{1,0:T(8,128)(2,1)} copy(bf16[256,8192]{0,1:T(8,128)(2,1)} %bitcast.162) | data formatting | bytes 8388608 | tf_op jit(solution)/shard_map/dot_general | solution.py:119
  57.6 7.1 %fusion.4 = f32[96,2,2,128]{3,0,2,1:T(8,128)S(1)} fusion(bf16[2,128,8192,1]{2,1,0,3:T(8,128)(2,1)} %bitcast.164, bf16[96,2,8192,1]{2,1,0,3:T(2,128)(2,1)} %fusion.3), kind=kOutput, calls=%fused_computation.8 | convolution fusion | flops 805306368 | bytes 7536640 | tf_op jit(solution)/shard_map/dot_general | solution.py:119
  64.7 0.8 copy.154
  65.5 1.0 reshape.260
  66.5 0.6 iota_compare_fusion.6
  67.1 0.4 copy.144
  67.5 0.2 reshape.258
  67.9 0.4 copy.145
  68.3 0.6 reshape.259
  69.0 1.8 %fusion.25 = f32[192,2,128]{2,0,1:T(8,128)S(1)} fusion(bf16[4,1024,128]{2,1,0:T(8,128)(2,1)} %param.13, bf16[192,2,1024,1]{2,1,0,3:T(2,128)(2,1)S(1)} %bitcast.168, f32[192,4]{0,1:T(4,128)S(1)} %get-tuple-element.28), kind=kOutput, calls=%fused_computation.21 | convolution fusion | flops 402997248 | bytes 2034688 | tf_op jit(solution)/shard_map/euz,nzs->euns/dot_general | solution.py:165
  70.8 23.3 %all-reduce.2 = bf16[192,2,128]{2,0,1:T(8,128)(2,1)S(1)} all-reduce(f32[192,2,128]{2,0,1:T(8,128)S(1)} %fusion.25), channel_id=1, replica_groups=mesh['az'=8,'ay'=4,'tx'=4,'tc'=2] {'tx','tc'}, use_global_device_ids=true, to_apply=%region_3.4 | all-reduce | flops 49152 | bytes 294912 | tf_op jit(solution)/shard_map/psum | solution.py:169
  94.4 0.2 convolution_bitcast_fusion
  94.6 0.2 convolution_bitcast_fusion.1
  94.9 0.3 copy.150
  95.2 0.8 copy.151
  96.0 3.5 %all-to-all-start.2 = ((f32[8,4,24,128]{3,2,0,1:T(8,128)}), f32[8,4,24,128]{3,2,0,1:T(8,128)S(1)}, u32[]{:S(2)}, u32[]{:S(2)}) async-start(f32[8,4,24,128]{3,2,0,1:T(8,128)} %copy.151), calls=%async_computation.2 | async-start | bytes 786432 | tf_op jit(solution)/shard_map/all_to_all | solution.py:88
  99.5 9.2 %all-to-all-done.2 = f32[8,4,24,128]{3,2,0,1:T(8,128)S(1)} async-done(((f32[8,4,24,128]{3,2,0,1:T(8,128)}), f32[8,4,24,128]{3,2,0,1:T(8,128)S(1)}, u32[]{:S(2)}, u32[]{:S(2)}) %all-to-all-start.2) | async-done | bytes 393248 | tf_op jit(solution)/shard_map/all_to_all | solution.py:88
  108.7 0.8 copy.152
  109.5 6.9 %all-to-all-start.3 = ((f32[8,4,24,128]{3,2,1,0:T(8,128)}), f32[8,4,24,128]{3,2,1,0:T(8,128)S(1)}, u32[]{:S(2)}, u32[]{:S(2)}) async-start(f32[8,4,24,128]{3,2,1,0:T(8,128)} %copy.152), calls=%async_computation.3 | async-start | bytes 786432 | tf_op jit(solution)/shard_map/all_to_all | solution.py:89
  116.5 3.1 %fusion.74 = (f32[96,2,8]{2,1,0:T(2,128)}, f32[96,2,1,8,64]{4,3,1,0,2:T(8,128)S(1)}) fusion(bf16[96,2,8,128]{3,2,1,0:T(8,128)(2,1)S(1)} %copy-done.2, bf16[96,64,128]{2,1,0:T(8,128)(2,1)} %param.17, pred[96,64]{1,0:T(8,128)(4,1)S(1)} %iota_compare_fusion.3), kind=kOutput, calls=%fused_computation.101 | convolution fusion | flops 25459200 | bytes 2371584 | tf_op jit(solution)/shard_map/rthgd,rjhd->rthgj/dot_general | solution.py:49
  119.6 11.5 %all-to-all-done.3 = f32[8,4,24,128]{3,2,1,0:T(8,128)S(1)} async-done(((f32[8,4,24,128]{3,2,1,0:T(8,128)}), f32[8,4,24,128]{3,2,1,0:T(8,128)S(1)}, u32[]{:S(2)}, u32[]{:S(2)}) %all-to-all-start.3) | async-done | bytes 393248 | tf_op jit(solution)/shard_map/all_to_all | solution.py:89
  131.2 0.7 gather_fusion
  132.2 1.0 select_add_fusion
  133.2 0.3 fusion.84
  133.5 0.3 fusion.54
  133.8 0.3 fusion.83
  134.2 0.3 fusion.82
  134.5 0.7 copy.161
  135.2 0.7 copy.162
  136.2 2.5 %fusion.75 = (f32[96,2,8]{2,1,0:T(2,128)S(1)}, f32[96,2,1,8,2]{3,4,1,0,2:T(2,128)S(1)}) fusion(bf16[96,2,128,1]{2,1,3,0:T(2,128)(2,1)S(1)} %copy.168, bf16[96,2,8,128]{3,2,1,0:T(8,128)(2,1)S(1)} %copy-done.2, pred[2,2]{1,0:T(4,128)(4,1)} %iota_compare_fusion.6), kind=kOutput, calls=%fused_computation.102 | convolution fusion | flops 794112 | bytes 460804 | tf_op jit(solution)/shard_map/rthgd,rshd->rthgs/dot_general | solution.py:55
  138.9 0.6 fusion.39
  139.5 0.4 fusion.44
  139.9 0.4 fusion.45
  140.4 0.6 fusion.32
  141.0 0.8 convert_element_type.123
  (62 shorter events, 1.9 us)
Async XLA Ops:
  0.6 139.7 %copy-start = (bf16[96,64,128]{2,1,0:T(8,128)(2,1)S(1)}, bf16[96,64,128]{2,1,0:T(8,128)(2,1)}, u32[]{:S(2)}) copy-start(bf16[96,64,128]{2,1,0:T(8,128)(2,1)} %param.18) | copy-start | bytes 4718596
  0.6 5.4 %copy-start.13 = (s32[96]{0:T(128)S(1)}, s32[96]{0:T(128)}, u32[]{:S(2)}) copy-start(s32[96]{0:T(128)} %param.15) | copy-start | bytes 1156
  0.7 6.5 %copy-start.8 = (bf16[8192]{0:T(1024)(128)(2,1)S(1)}, bf16[8192]{0:T(1024)(128)(2,1)}, u32[]{:S(2)}) copy-start(bf16[8192]{0:T(1024)(128)(2,1)} %param.11) | copy-start | bytes 49156
  6.0 2.7 %copy-start.3 = (f32[96,2]{1,0:T(8,128)}, f32[96,2]{1,0:T(8,128)S(1)}, u32[]{:S(2)}) copy-start(f32[96,2]{1,0:T(8,128)S(1)} %add_rsqrt_fusion) | copy-start | bytes 2308
  6.8 2.0 %copy-start.9 = (s32[96]{0:T(128)}, s32[96]{0:T(128)S(1)}, u32[]{:S(2)}) copy-start(s32[96]{0:T(128)S(1)} %get-tuple-element.25) | copy-start | bytes 1156
  9.8 28.9 %copy-start.4 = (f32[96,2]{1,0:T(8,128)S(1)}, f32[96,2]{1,0:T(8,128)}, u32[]{:S(2)}) copy-start(f32[96,2]{1,0:T(8,128)} %copy-done.3) | copy-start | bytes 2308
  11.2 17.5 %all-to-all-start = ((bf16[8,4,13,1024]{3,0,2,1:T(8,128)(2,1)}), bf16[8,4,13,1024]{3,0,2,1:T(8,128)(2,1)S(1)}, u32[]{:S(2)}, u32[]{:S(2)}) async-start(bf16[8,4,13,1024]{3,0,2,1:T(8,128)(2,1)} %copy.142), calls=%async_computation | async-start | bytes 1703936 | tf_op jit(solution)/shard_map/all_to_all | solution.py:88
  30.2 36.9 %all-to-all-start.1 = ((bf16[8,4,13,1024]{3,1,2,0:T(4,128)(2,1)}), bf16[8,4,13,1024]{3,1,2,0:T(4,128)(2,1)S(1)}, u32[]{:S(2)}, u32[]{:S(2)}) async-start(bf16[8,4,13,1024]{3,1,2,0:T(4,128)(2,1)} %copy.143), calls=%async_computation.1 | async-start | bytes 1703936 | tf_op jit(solution)/shard_map/all_to_all | solution.py:89
  38.7 10.0 %copy-start.1 = (bf16[8192,2,128]{2,1,0:T(2,128)(2,1)S(1)}, bf16[8192,2,128]{2,1,0:T(2,128)(2,1)}, u32[]{:S(2)}) copy-start(bf16[8192,2,128]{2,1,0:T(2,128)(2,1)} %param.12) | copy-start | bytes 12582916
  57.6 7.9 %copy-start.6 = (bf16[96,2,1024]{2,1,0:T(2,128)(2,1)S(1)}, bf16[96,2,1024]{2,1,0:T(2,128)(2,1)}, u32[]{:S(2)}) copy-start(bf16[96,2,1024]{2,1,0:T(2,128)(2,1)} %param.16) | copy-start | bytes 1179652
  69.0 25.4 %copy-start.7 = (bf16[4,2,64,128]{3,2,1,0:T(8,128)(2,1)S(1)}, bf16[4,2,64,128]{3,2,1,0:T(8,128)(2,1)}, u32[]{:S(2)}) copy-start(bf16[4,2,64,128]{3,2,1,0:T(8,128)(2,1)} %param.14) | copy-start | bytes 393220
  70.8 28.7 %copy-start.10 = (s32[96]{0:T(128)S(1)}, s32[96]{0:T(128)}, u32[]{:S(2)}) copy-start(s32[96]{0:T(128)} %copy-done.9) | copy-start | bytes 1156
  94.3 22.1 %copy-start.12 = (s32[96]{0:T(128)S(1)}, s32[96]{0:T(128)}, u32[]{:S(2)}) copy-start(s32[96]{0:T(128)} %param.19) | copy-start | bytes 1156
  94.3 22.2 %copy-start.2 = (bf16[96,2,8,128]{3,2,1,0:T(8,128)(2,1)S(1)}, bf16[96,2,8,128]{3,2,1,0:T(8,128)(2,1)}, u32[]{:S(2)}) copy-start(bf16[96,2,8,128]{3,2,1,0:T(8,128)(2,1)} %reshape.260) | copy-start | bytes 1179652
  96.0 12.7 %all-to-all-start.2 = ((f32[8,4,24,128]{3,2,0,1:T(8,128)}), f32[8,4,24,128]{3,2,0,1:T(8,128)S(1)}, u32[]{:S(2)}, u32[]{:S(2)}) async-start(f32[8,4,24,128]{3,2,0,1:T(8,128)} %copy.151), calls=%async_computation.2 | async-start | bytes 786432 | tf_op jit(solution)/shard_map/all_to_all | solution.py:88
  109.5 21.6 %all-to-all-start.3 = ((f32[8,4,24,128]{3,2,1,0:T(8,128)}), f32[8,4,24,128]{3,2,1,0:T(8,128)S(1)}, u32[]{:S(2)}, u32[]{:S(2)}) async-start(f32[8,4,24,128]{3,2,1,0:T(8,128)} %copy.152), calls=%async_computation.3 | async-start | bytes 786432 | tf_op jit(solution)/shard_map/all_to_all | solution.py:89
  116.4 15.8 %copy-start.11 = (pred[96]{0:T(512)(128)(4,1)S(1)}, pred[96]{0:T(512)(128)(4,1)}, u32[]{:S(2)}) copy-start(pred[96]{0:T(512)(128)(4,1)} %get-tuple-element.24) | copy-start | bytes 292
  131.9 6.9 %copy-start.5 = (f32[96,2,8]{2,1,0:T(2,128)S(1)}, f32[96,2,8]{2,1,0:T(2,128)}, u32[]{:S(2)}) copy-start(f32[96,2,8]{2,1,0:T(2,128)} %get-tuple-element.30) | copy-start | bytes 18436

commit v9 on v2

--- a/solution.py
+++ b/solution.py
@@ -79,6 +79,16 @@
         "rthgs,rshd->rthgd", fresh_probs, fresh_vals, preferred_element_type=jnp.float32
     )
     return mixed_out.reshape(row_total, token_total, query_width).astype(jnp.bfloat16)
+
+
+def butterfly_sum(value, axis_name):
+    member_count = lax.axis_size(axis_name)
+    stride = 1
+    while stride < member_count:
+        pairs = [(i, i ^ stride) for i in range(member_count)]
+        value = value + lax.ppermute(value, axis_name, pairs)
+        stride *= 2
+    return value
 
 
 def body(
@@ -157,7 +167,7 @@
         "euz,nzs->euns", got_rows, adapter_down_weight, preferred_element_type=jnp.float32
     )
     partial_rank = jnp.sum(down_all * selector[:, None, :, None], axis=2)
-    rank_hidden = lax.psum(partial_rank, "tensor").astype(jnp.bfloat16)
+    rank_hidden = butterfly_sum(partial_rank, "tensor").astype(jnp.bfloat16)
 
     rank_selector = selector.astype(jnp.bfloat16)
     masked = rank_hidden[:, :, None, :] * rank_selector[:, None, :, None]

time: 115 us -> 107 us (0.930)
  blocking collectives: 23.2 us -> 0 us
  waiting for transfers between devices: 12.6 us -> 29.1 us
  local copies, waits for them, and re-layouts: 16.1 us -> 18.4 us
  matrix products: 17.3 us -> 15.9 us
    psum x1 -> x0, blocking collectives: 23.2 us -> none  [body(): rank_hidden = lax.psum(partial_rank, 'tensor').astype(jnp.bfloat16)]
    ppermute x0 -> x3, waiting for transfers between devices: none -> 12.8 us  [butterfly_sum(): value = value + lax.ppermute(value, axis_name, pairs)]
    all_to_all x1, waiting for transfers between devices: 1.21 us -> 7.05 us  [body(): recv = lax.all_to_all(send, 'adapter', 0, 0, tiled=True)]
    all_to_all x1, starting transfers between devices: 9.32 us -> 5.58 us  [body(): delta_recv = lax.all_to_all(delta_send, 'adapter', 0, 0, tiled=True)]
    ppermute x0 -> x3, starting transfers between devices: none -> 2.72 us  [butterfly_sum(): value = value + lax.ppermute(value, axis_name, pairs)]
    unnamed x24 -> x20, local copies, waits for them, and re-layouts: 4.12 us -> 6.42 us
    all_to_all x1, waiting for transfers between devices: 11.4 us -> 9.26 us  [body(): delta_recv = lax.all_to_all(delta_send, 'adapter', 0, 0, tiled=True)]
    dot_general x1, matrix products: 7.75 us -> 6.26 us  [body(): jnp.dot(normed_input.reshape(row_count * token_count, model_width), key_v...]
  transfers between devices with their start and end apart: 2 -> 5, of which waited for: 2 -> 4; matrix products, arithmetic and copies ran while one was open for 28% -> 30% of each run, Pallas kernels for 0% -> 0%
where the time goes in v9:
time: 107 us
  waiting for transfers between devices  29.1 us (27%)
  other arithmetic  22.3 us (21%)
  starting transfers between devices  20 us (19%)
  local copies, waits for them, and re-layouts  18.4 us (17%)
  matrix products  15.9 us (15%)
  between operations  1.07 us (1%)
    ppermute x3, waiting for transfers between devices, butterfly_sum(): value = value + lax.ppermute(value, axis_name, pairs)  12.8 us
    all_to_all x1, starting transfers between devices, body(): recv = lax.all_to_all(send, 'adapter', 0, 0, tiled=True)  11.7 us
    convert_element_type x1, other arithmetic, body(): (values * row_scale * input_norm_gain.astype(jnp.float32)).astype(jnp.bfl...  9.74 us
    all_to_all x1, waiting for transfers between devices, body(): delta_recv = lax.all_to_all(delta_send, 'adapter', 0, 0, tiled=True)  9.26 us
    all_to_all x1, waiting for transfers between devices, body(): recv = lax.all_to_all(send, 'adapter', 0, 0, tiled=True)  7.05 us
    unnamed x20, local copies, waits for them, and re-layouts  6.42 us
    dot_general x1, local copies, waits for them, and re-layouts, body(): jnp.dot(normed_input.reshape(row_count * token_count, model_width), key_v...  6.37 us
    dot_general x1, matrix products, body(): jnp.dot(normed_input.reshape(row_count * token_count, model_width), key_v...  6.26 us
  transfers between devices with their start and end apart: 5, of which 4 were waited for; matrix products, arithmetic and copies ran while one was open for 30% of the time, Pallas kernels for 0%

profile of v9, /device:TPU:6, one launch (start us, length us, event | category | flops | bytes accessed | tf_op | source)
XLA Modules:
  0.0 106.6 jit_solution(5509006960794124276)
XLA Ops:
  0.7 5.3 %fusion = f32[96,2]{1,0:T(8,128)S(1)} fusion(bf16[96,2,8192]{2,1,0:T(2,128)(2,1)} %param.10), kind=kLoop, calls=%fused_computation.3 | loop fusion | flops 4718400 | bytes 3146496 | tf_op jit(solution)/shard_map/reduce_sum | solution.py:117
  6.0 0.2 convert_reduce_fusion
  6.3 0.1 fusion.50
  6.4 0.1 reshape.290
  6.6 1.5 %multiply_convert_fusion = bf16[96,2,1024]{2,1,0:T(2,128)(2,1)S(1)} fusion(f32[1024]{0:T(1024)S(1)} %dynamic-slice_convert_fusion, f32[96,2]{1,0:T(8,128)S(1)} %add_rsqrt_fusion, bf16[96,2,8192]{2,1,0:T(2,128)(2,1)} %param.10, s32[]{:T(128)S(6)} %select_n.31), kind=kLoop, calls=%fused_computation.37 | loop fusion | flops 786432 | bytes 791300 | tf_op jit(solution)/shard_map/convert_element_type | solution.py:143
  8.1 0.4 convolution_convert_fusion
  8.5 0.4 reshape.258
  8.9 1.2 %fusion.38 = bf16[32,13,1024]{2,1,0:T(8,128)(2,1)} fusion(bf16[32,1,6]{2,1,0:T(2,128)(2,1)S(1)} %reshape.290, bf16[32,12,1024]{2,1,0:T(8,128)(2,1)S(1)} %reshape.258), kind=kLoop, calls=%fused_computation.32 | loop fusion | flops 2555904 | bytes 1638784 | tf_op jit(solution)/shard_map/concatenate | solution.py:157
  10.1 11.7 %all-to-all-start = ((bf16[32,13,1024]{2,1,0:T(8,128)(2,1)}), bf16[32,13,1024]{2,1,0:T(8,128)(2,1)S(1)}, u32[]{:S(2)}, u32[]{:S(2)}) async-start(bf16[32,13,1024]{2,1,0:T(8,128)(2,1)} %fusion.38), calls=%async_computation | async-start | bytes 2097152 | tf_op jit(solution)/shard_map/all_to_all | solution.py:158
  21.8 4.7 %copy.122 = bf16[1024,8,2,128]{3,1,2,0:T(8,128)(2,1)} copy(bf16[1024,8,2,128]{3,2,1,0:T(2,128)(2,1)} %bitcast.157) | data formatting | bytes 8388608
  26.5 6.4 %copy.79 = bf16[256,8192]{1,0:T(8,128)(2,1)} copy(bf16[256,8192]{0,1:T(8,128)(2,1)} %bitcast.155) | data formatting | bytes 8388608 | tf_op jit(solution)/shard_map/dot_general | solution.py:120
  32.9 9.7 %fusion.3 = bf16[96,2,8192,1]{2,1,0,3:T(2,128)(2,1)} fusion(bf16[96,2,8192]{2,1,0:T(2,128)(2,1)} %param.10, f32[8192]{0:T(1024)S(1)} %convert_element_type.100, f32[96,2]{1,0:T(8,128)S(1)} %add_rsqrt_fusion), kind=kLoop, calls=%fused_computation.7 | loop fusion | flops 6291456 | bytes 6324992 | tf_op jit(solution)/shard_map/convert_element_type | solution.py:119
  42.6 7.0 %all-to-all-done = bf16[32,13,1024]{2,1,0:T(8,128)(2,1)S(1)} async-done(((bf16[32,13,1024]{2,1,0:T(8,128)(2,1)}), bf16[32,13,1024]{2,1,0:T(8,128)(2,1)S(1)}, u32[]{:S(2)}, u32[]{:S(2)}) %all-to-all-start) | async-done | bytes 852000 | tf_op jit(solution)/shard_map/all_to_all | solution.py:158
  49.9 0.6 reshape.260
  50.5 2.0 %fusion.26 = f32[192,2,128]{2,0,1:T(8,128)S(1)} fusion(bf16[4,1024,128]{2,1,0:T(8,128)(2,1)} %param.13, bf16[192,2,1024,1]{2,1,0,3:T(2,128)(2,1)S(1)} %bitcast.161, f32[192,4]{0,1:T(4,128)S(1)} %get-tuple-element.22), kind=kOutput, calls=%fused_computation.23 | convolution fusion | flops 402997248 | bytes 2034688 | tf_op jit(solution)/shard_map/euz,nzs->euns/dot_general | solution.py:166
  52.6 0.1 copy-done.1
  52.7 6.3 %fusion.4 = f32[96,2,2,128]{3,0,2,1:T(8,128)S(1)} fusion(bf16[2,128,8192,1]{2,1,0,3:T(8,128)(2,1)} %bitcast.158, bf16[96,2,8192,1]{2,1,0,3:T(2,128)(2,1)S(1)} %copy-done.1), kind=kOutput, calls=%fused_computation.8 | convolution fusion | flops 805306368 | bytes 7536640 | tf_op jit(solution)/shard_map/dot_general | solution.py:120
  59.0 0.9 collective-permute-start.1
  59.9 6.3 %collective-permute-done.1 = f32[192,2,128]{2,0,1:T(8,128)S(1)} collective-permute-done((f32[192,2,128]{2,0,1:T(8,128)S(1)}, f32[192,2,128]{2,0,1:T(8,128)S(1)}, u32[]{:S(2)}, u32[]{:S(2)}) %collective-permute-start.1) | collective-permute-done | bytes 196640 | tf_op jit(solution)/shard_map/ppermute | solution.py:89
  66.3 1.7 %collective-permute-start.2 = (f32[192,2,128]{2,0,1:T(8,128)S(1)}, f32[192,2,128]{2,0,1:T(8,128)S(1)}, u32[]{:S(2)}, u32[]{:S(2)}) collective-permute-start(f32[192,2,128]{2,0,1:T(8,128)S(1)} %add.81), channel_id=1, source_target_pairs={{0,4},{1,5},{2,6},{3,7},{4,0},{5,1},{6,2},{7,3},{8,12},{9,13},{10,... | collective-permute-start | bytes 589832 | tf_op jit(solution)/shard_map/ppermute | solution.py:89
  68.0 6.4 %collective-permute-done.2 = f32[192,2,128]{2,0,1:T(8,128)S(1)} collective-permute-done((f32[192,2,128]{2,0,1:T(8,128)S(1)}, f32[192,2,128]{2,0,1:T(8,128)S(1)}, u32[]{:S(2)}, u32[]{:S(2)}) %collective-permute-start.2) | collective-permute-done | bytes 196640 | tf_op jit(solution)/shard_map/ppermute | solution.py:89
  74.5 0.1 copy.83
  74.7 0.2 convolution_bitcast_fusion
  74.9 0.3 convolution_bitcast_fusion.1
  75.2 1.1 copy.86
  76.2 5.6 %all-to-all-start.1 = ((f32[32,24,128]{2,1,0:T(8,128)}), f32[32,24,128]{2,1,0:T(8,128)S(1)}, u32[]{:S(2)}, u32[]{:S(2)}) async-start(f32[32,24,128]{2,1,0:T(8,128)} %bitcast.18), calls=%async_computation.1 | async-start | bytes 786432 | tf_op jit(solution)/shard_map/all_to_all | solution.py:188
  81.8 0.5 iota_compare_fusion.7
  82.4 0.8 copy.88
  83.2 0.3 reshape.263
  83.6 3.1 %fusion.77 = (f32[96,2,8]{2,1,0:T(2,128)}, f32[96,2,1,8,64]{4,3,1,0,2:T(8,128)S(1)}) fusion(bf16[96,2,8,128]{3,2,1,0:T(8,128)(2,1)S(1)} %reshape.263, bf16[96,64,128]{2,1,0:T(8,128)(2,1)} %param.17, pred[96,64]{1,0:T(8,128)(4,1)S(1)} %iota_compare_fusion.4), kind=kOutput, calls=%fused_computation.105 | convolution fusion | flops 25459200 | bytes 2371584 | tf_op jit(solution)/shard_map/rthgd,rjhd->rthgj/dot_general | solution.py:49
  86.7 9.3 %all-to-all-done.1 = f32[32,24,128]{2,1,0:T(8,128)S(1)} async-done(((f32[32,24,128]{2,1,0:T(8,128)}), f32[32,24,128]{2,1,0:T(8,128)S(1)}, u32[]{:S(2)}, u32[]{:S(2)}) %all-to-all-start.1) | async-done | bytes 393248 | tf_op jit(solution)/shard_map/all_to_all | solution.py:188
  96.0 0.7 gather_fusion
  96.7 0.1 gather.7
  96.9 0.1 copy.87
  97.0 1.0 select_add_fusion
  98.0 0.3 fusion.87
  98.3 0.3 fusion.56
  98.7 0.3 fusion.86
  99.0 0.3 fusion.85
  99.3 0.7 copy.95
  100.1 0.7 copy.96
  101.0 0.1 copy.102
  101.1 2.5 %fusion.78 = (f32[96,2,8]{2,1,0:T(2,128)S(1)}, f32[96,2,1,8,2]{3,4,1,0,2:T(2,128)S(1)}) fusion(bf16[96,2,128,1]{2,1,3,0:T(2,128)(2,1)S(1)} %copy.102, bf16[96,2,8,128]{3,2,1,0:T(8,128)(2,1)S(1)} %reshape.263, pred[2,2]{1,0:T(4,128)(4,1)} %iota_compare_fusion.7), kind=kOutput, calls=%fused_computation.106 | convolution fusion | flops 794112 | bytes 460804 | tf_op jit(solution)/shard_map/rthgd,rshd->rthgs/dot_general | solution.py:55
  103.7 0.6 fusion.41
  104.3 0.4 fusion.46
  104.7 0.4 fusion.47
  105.2 0.6 fusion.33
  105.8 0.8 convert_element_type.123
  (44 shorter events, 1.0 us)
Async XLA Ops:
  0.6 104.5 %copy-start = (bf16[96,64,128]{2,1,0:T(8,128)(2,1)S(1)}, bf16[96,64,128]{2,1,0:T(8,128)(2,1)}, u32[]{:S(2)}) copy-start(bf16[96,64,128]{2,1,0:T(8,128)(2,1)} %param.18) | copy-start | bytes 4718596
  0.6 5.4 %copy-start.7 = (s32[96]{0:T(128)S(1)}, s32[96]{0:T(128)}, u32[]{:S(2)}) copy-start(s32[96]{0:T(128)} %param.15) | copy-start | bytes 1156
  0.7 5.9 %copy-start.5 = (bf16[8192]{0:T(1024)(128)(2,1)S(1)}, bf16[8192]{0:T(1024)(128)(2,1)}, u32[]{:S(2)}) copy-start(bf16[8192]{0:T(1024)(128)(2,1)} %param.11) | copy-start | bytes 49156
  10.1 39.5 %all-to-all-start = ((bf16[32,13,1024]{2,1,0:T(8,128)(2,1)}), bf16[32,13,1024]{2,1,0:T(8,128)(2,1)S(1)}, u32[]{:S(2)}, u32[]{:S(2)}) async-start(bf16[32,13,1024]{2,1,0:T(8,128)(2,1)} %fusion.38), calls=%async_computation | async-start | bytes 2097152 | tf_op jit(solution)/shard_map/all_to_all | solution.py:158
  50.5 2.2 %copy-start.1 = (bf16[96,2,8192,1]{2,1,0,3:T(2,128)(2,1)S(1)}, bf16[96,2,8192,1]{2,1,0,3:T(2,128)(2,1)}, u32[]{:S(2)}) copy-start(bf16[96,2,8192,1]{2,1,0,3:T(2,128)(2,1)} %fusion.3) | copy-start | bytes 9437188
  52.5 6.5 %collective-permute-start = (f32[192,2,128]{2,0,1:T(8,128)S(1)}, f32[192,2,128]{2,0,1:T(8,128)S(1)}, u32[]{:S(2)}, u32[]{:S(2)}) collective-permute-start(f32[192,2,128]{2,0,1:T(8,128)S(1)} %fusion.26), channel_id=1, source_target_pairs={{0,1},{1,0},{2,3},{3,2},{4,5},{5,4},{6,7},{7,6},{8,9},{9,8},{10,11... | collective-permute-start | bytes 589832 | tf_op jit(solution)/shard_map/ppermute | solution.py:89
  52.7 22.0 %copy-start.4 = (bf16[4,2,64,128]{3,2,1,0:T(8,128)(2,1)S(1)}, bf16[4,2,64,128]{3,2,1,0:T(8,128)(2,1)}, u32[]{:S(2)}) copy-start(bf16[4,2,64,128]{3,2,1,0:T(8,128)(2,1)} %param.14) | copy-start | bytes 393220
  59.0 24.2 %copy-start.3 = (bf16[96,2,1024]{2,1,0:T(2,128)(2,1)S(1)}, bf16[96,2,1024]{2,1,0:T(2,128)(2,1)}, u32[]{:S(2)}) copy-start(bf16[96,2,1024]{2,1,0:T(2,128)(2,1)} %param.16) | copy-start | bytes 1179652
  59.0 7.3 %collective-permute-start.1 = (f32[192,2,128]{2,0,1:T(8,128)S(1)}, f32[192,2,128]{2,0,1:T(8,128)S(1)}, u32[]{:S(2)}, u32[]{:S(2)}) collective-permute-start(f32[192,2,128]{2,0,1:T(8,128)S(1)} %add.80), channel_id=1, source_target_pairs={{0,2},{1,3},{2,0},{3,1},{4,6},{5,7},{6,4},{7,5},{8,10},{9,11},{10,... | collective-permute-start | bytes 589832 | tf_op jit(solution)/shard_map/ppermute | solution.py:89
  66.3 17.2 %copy-start.6 = (s32[96]{0:T(128)S(1)}, s32[96]{0:T(128)}, u32[]{:S(2)}) copy-start(s32[96]{0:T(128)} %param.19) | copy-start | bytes 1156
  66.3 8.1 %collective-permute-start.2 = (f32[192,2,128]{2,0,1:T(8,128)S(1)}, f32[192,2,128]{2,0,1:T(8,128)S(1)}, u32[]{:S(2)}, u32[]{:S(2)}) collective-permute-start(f32[192,2,128]{2,0,1:T(8,128)S(1)} %add.81), channel_id=1, source_target_pairs={{0,4},{1,5},{2,6},{3,7},{4,0},{5,1},{6,2},{7,3},{8,12},{9,13},{10,... | collective-permute-start | bytes 589832 | tf_op jit(solution)/shard_map/ppermute | solution.py:89
  76.2 19.7 %all-to-all-start.1 = ((f32[32,24,128]{2,1,0:T(8,128)}), f32[32,24,128]{2,1,0:T(8,128)S(1)}, u32[]{:S(2)}, u32[]{:S(2)}) async-start(f32[32,24,128]{2,1,0:T(8,128)} %bitcast.18), calls=%async_computation.1 | async-start | bytes 786432 | tf_op jit(solution)/shard_map/all_to_all | solution.py:188
  96.7 6.9 %copy-start.2 = (f32[96,2,8]{2,1,0:T(2,128)S(1)}, f32[96,2,8]{2,1,0:T(2,128)}, u32[]{:S(2)}) copy-start(f32[96,2,8]{2,1,0:T(2,128)} %get-tuple-element.24) | copy-start | bytes 18436

commit v10 on v2

--- a/solution.py
+++ b/solution.py
@@ -79,6 +79,16 @@
         "rthgs,rshd->rthgd", fresh_probs, fresh_vals, preferred_element_type=jnp.float32
     )
     return mixed_out.reshape(row_total, token_total, query_width).astype(jnp.bfloat16)
+
+
+def butterfly_sum(value, axis_name):
+    member_count = lax.axis_size(axis_name)
+    value = value + lax.ppermute(value, axis_name, [(i, i ^ 1) for i in range(member_count)])
+    shifted = [
+        lax.ppermute(value, axis_name, [(i, (i + 2 * k) % member_count) for i in range(member_count)])
+        for k in (1, 2, 3)
+    ]
+    return (value + shifted[1]) + (shifted[0] + shifted[2])
 
 
 def body(
@@ -157,7 +167,7 @@
         "euz,nzs->euns", got_rows, adapter_down_weight, preferred_element_type=jnp.float32
     )
     partial_rank = jnp.sum(down_all * selector[:, None, :, None], axis=2)
-    rank_hidden = lax.psum(partial_rank, "tensor").astype(jnp.bfloat16)
+    rank_hidden = butterfly_sum(partial_rank, "tensor").astype(jnp.bfloat16)
 
     rank_selector = selector.astype(jnp.bfloat16)
     masked = rank_hidden[:, :, None, :] * rank_selector[:, None, :, None]

time: 115 us -> 100 us (0.87)
  blocking collectives: 23.2 us -> 0 us
  waiting for transfers between devices: 12.6 us -> 25.8 us
  other arithmetic: 22.9 us -> 18.8 us
  matrix products: 17.3 us -> 14.1 us
  local copies, waits for them, and re-layouts: 16.1 us -> 18.2 us
    psum x1 -> x0, blocking collectives: 23.2 us -> none  [body(): rank_hidden = lax.psum(partial_rank, 'tensor').astype(jnp.bfloat16)]
    ppermute x0 -> x4, waiting for transfers between devices: none -> 10.6 us  [the longest x3 9.22 us: butterfly_sum(): lax.ppermute(value, axis_name, [(i, (i + 2 * k) % member_count) for i in...]
    all_to_all x1, waiting for transfers between devices: 1.21 us -> 5.9 us  [body(): recv = lax.all_to_all(send, 'adapter', 0, 0, tiled=True)]
    all_to_all x1, starting transfers between devices: 9.32 us -> 5.58 us  [body(): delta_recv = lax.all_to_all(delta_send, 'adapter', 0, 0, tiled=True)]
    convert_element_type x1, other arithmetic: 9.97 us -> 6.29 us  [body(): (values * row_scale * input_norm_gain.astype(jnp.float32)).astype(jnp.bfl...]
    ppermute x0 -> x4, starting transfers between devices: none -> 3.6 us  [the longest x3 3.51 us: butterfly_sum(): lax.ppermute(value, axis_name, [(i, (i + 2 * k) % member_count) for i in...]
    dot_general x1, matrix products: 7.75 us -> 4.6 us  [body(): jnp.dot(normed_input.reshape(row_count * token_count, model_width), key_v...]
    all_to_all x1, waiting for transfers between devices: 11.4 us -> 9.24 us  [body(): delta_recv = lax.all_to_all(delta_send, 'adapter', 0, 0, tiled=True)]
  transfers between devices with their start and end apart: 2 -> 6, of which waited for: 2 -> 5; matrix products, arithmetic and copies ran while one was open for 28% -> 27% of each run, Pallas kernels for 0% -> 0%
where the time goes in v10:
time: 100 us; the launch traced here: 98.9 us
  waiting for transfers between devices  25.8 us (26%)
  starting transfers between devices  20.8 us (21%)
  other arithmetic  18.8 us (19%)
  local copies, waits for them, and re-layouts  18.2 us (18%)
  matrix products  14.1 us (14%)
  between operations  1.08 us (1%)
    all_to_all x1, starting transfers between devices, body(): recv = lax.all_to_all(send, 'adapter', 0, 0, tiled=True)  11.7 us
    all_to_all x1, waiting for transfers between devices, body(): delta_recv = lax.all_to_all(delta_send, 'adapter', 0, 0, tiled=True)  9.24 us
    ppermute x3, waiting for transfers between devices, butterfly_sum(): lax.ppermute(value, axis_name, [(i, (i + 2 * k) % member_count) for i in...  9.22 us
    dot_general x1, local copies, waits for them, and re-layouts, body(): jnp.dot(normed_input.reshape(row_count * token_count, model_width), key_v...  6.38 us
    convert_element_type x1, other arithmetic, body(): (values * row_scale * input_norm_gain.astype(jnp.float32)).astype(jnp.bfl...  6.29 us
    unnamed x22, local copies, waits for them, and re-layouts  6.26 us
    all_to_all x1, waiting for transfers between devices, body(): recv = lax.all_to_all(send, 'adapter', 0, 0, tiled=True)  5.9 us
    all_to_all x1, starting transfers between devices, body(): delta_recv = lax.all_to_all(delta_send, 'adapter', 0, 0, tiled=True)  5.58 us
  transfers between devices with their start and end apart: 6, of which 5 were waited for; matrix products, arithmetic and copies ran while one was open for 27% of the time, Pallas kernels for 0%

profile of v10, /device:TPU:6, one launch (start us, length us, event | category | flops | bytes accessed | tf_op | source)
XLA Modules:
  0.0 98.9 jit_solution(5011368038984122567)
XLA Ops:
  0.7 5.3 %fusion = f32[96,2]{1,0:T(8,128)S(1)} fusion(bf16[96,2,8192]{2,1,0:T(2,128)(2,1)} %param.10), kind=kLoop, calls=%fused_computation.3 | loop fusion | flops 4718400 | bytes 3146496 | tf_op jit(solution)/shard_map/reduce_sum | solution.py:117
  6.0 0.2 convert_reduce_fusion
  6.3 0.1 fusion.50
  6.4 0.1 reshape.290
  6.6 1.5 %multiply_convert_fusion = bf16[96,2,1024]{2,1,0:T(2,128)(2,1)S(1)} fusion(f32[1024]{0:T(1024)S(1)} %dynamic-slice_convert_fusion, f32[96,2]{1,0:T(8,128)S(1)} %add_rsqrt_fusion, bf16[96,2,8192]{2,1,0:T(2,128)(2,1)} %param.10, s32[]{:T(128)S(6)} %select_n.31), kind=kLoop, calls=%fused_computation.37 | loop fusion | flops 786432 | bytes 791300 | tf_op jit(solution)/shard_map/convert_element_type | solution.py:143
  8.1 0.4 convolution_convert_fusion
  8.5 0.4 reshape.258
  8.9 1.2 %fusion.38 = bf16[32,13,1024]{2,1,0:T(8,128)(2,1)} fusion(bf16[32,1,6]{2,1,0:T(2,128)(2,1)S(1)} %reshape.290, bf16[32,12,1024]{2,1,0:T(8,128)(2,1)S(1)} %reshape.258), kind=kLoop, calls=%fused_computation.32 | loop fusion | flops 2555904 | bytes 1638784 | tf_op jit(solution)/shard_map/concatenate | solution.py:157
  10.1 11.7 %all-to-all-start = ((bf16[32,13,1024]{2,1,0:T(8,128)(2,1)}), bf16[32,13,1024]{2,1,0:T(8,128)(2,1)S(1)}, u32[]{:S(2)}, u32[]{:S(2)}) async-start(bf16[32,13,1024]{2,1,0:T(8,128)(2,1)} %fusion.38), calls=%async_computation | async-start | bytes 2097152 | tf_op jit(solution)/shard_map/all_to_all | solution.py:158
  21.8 4.7 %copy.122 = bf16[1024,8,2,128]{3,1,2,0:T(8,128)(2,1)} copy(bf16[1024,8,2,128]{3,2,1,0:T(2,128)(2,1)} %bitcast.157) | data formatting | bytes 8388608
  26.5 6.4 %copy.79 = bf16[256,8192]{1,0:T(8,128)(2,1)} copy(bf16[256,8192]{0,1:T(8,128)(2,1)} %bitcast.155) | data formatting | bytes 8388608 | tf_op jit(solution)/shard_map/dot_general | solution.py:120
  32.9 6.3 %fusion.3 = bf16[96,2,8192,1]{2,1,0,3:T(2,128)(2,1)S(1)} fusion(bf16[96,2,8192]{2,1,0:T(2,128)(2,1)} %param.10, f32[8192]{0:T(1024)S(1)} %convert_element_type.100, f32[96,2]{1,0:T(8,128)S(1)} %add_rsqrt_fusion), kind=kLoop, calls=%fused_computation.7 | loop fusion | flops 6291456 | bytes 6324992 | tf_op jit(solution)/shard_map/convert_element_type | solution.py:119
  39.2 4.6 %fusion.4 = f32[96,2,2,128]{3,0,2,1:T(8,128)} fusion(bf16[2,128,8192,1]{2,1,0,3:T(8,128)(2,1)S(1)} %bitcast.158, bf16[96,2,8192,1]{2,1,0,3:T(2,128)(2,1)S(1)} %fusion.3), kind=kOutput, calls=%fused_computation.8 | convolution fusion | flops 805306368 | bytes 7536640 | tf_op jit(solution)/shard_map/dot_general | solution.py:120
  43.8 5.9 %all-to-all-done = bf16[32,13,1024]{2,1,0:T(8,128)(2,1)S(1)} async-done(((bf16[32,13,1024]{2,1,0:T(8,128)(2,1)}), bf16[32,13,1024]{2,1,0:T(8,128)(2,1)S(1)}, u32[]{:S(2)}, u32[]{:S(2)}) %all-to-all-start) | async-done | bytes 852000 | tf_op jit(solution)/shard_map/all_to_all | solution.py:158
  49.9 0.6 reshape.260
  50.5 1.8 %fusion.26 = f32[192,2,128]{2,0,1:T(8,128)S(1)} fusion(bf16[4,1024,128]{2,1,0:T(8,128)(2,1)} %param.13, bf16[192,2,1024,1]{2,1,0,3:T(2,128)(2,1)S(1)} %bitcast.161, f32[192,4]{0,1:T(4,128)S(1)} %get-tuple-element.22), kind=kOutput, calls=%fused_computation.23 | convolution fusion | flops 402997248 | bytes 2034688 | tf_op jit(solution)/shard_map/euz,nzs->euns/dot_general | solution.py:166
  52.5 1.4 %collective-permute-done = f32[192,2,128]{2,0,1:T(8,128)S(1)} collective-permute-done((f32[192,2,128]{2,0,1:T(8,128)S(1)}, f32[192,2,128]{2,0,1:T(8,128)S(1)}, u32[]{:S(2)}, u32[]{:S(2)}) %collective-permute-start) | collective-permute-done | bytes 196640 | tf_op jit(solution)/shard_map/ppermute | solution.py:86
  53.9 0.6 collective-permute-start.2
  54.5 1.5 %collective-permute-start.3 = (f32[192,2,128]{2,0,1:T(8,128)S(1)}, f32[192,2,128]{2,0,1:T(8,128)S(1)}, u32[]{:S(2)}, u32[]{:S(2)}) collective-permute-start(f32[192,2,128]{2,0,1:T(8,128)S(1)} %add.83), channel_id=1, source_target_pairs={{0,6},{1,7},{2,0},{3,1},{4,2},{5,3},{6,4},{7,5},{8,14},{9,15},{10,... | collective-permute-start | bytes 589832 | tf_op jit(solution)/shard_map/ppermute | solution.py:88
  56.0 1.4 %collective-permute-start.1 = (f32[192,2,128]{2,0,1:T(8,128)S(1)}, f32[192,2,128]{2,0,1:T(8,128)S(1)}, u32[]{:S(2)}, u32[]{:S(2)}) collective-permute-start(f32[192,2,128]{2,0,1:T(8,128)S(1)} %add.83), channel_id=1, source_target_pairs={{0,4},{1,5},{2,6},{3,7},{4,0},{5,1},{6,2},{7,3},{8,12},{9,13},{10,... | collective-permute-start | bytes 589832 | tf_op jit(solution)/shard_map/ppermute | solution.py:88
  57.5 4.3 %collective-permute-done.2 = f32[192,2,128]{2,0,1:T(8,128)S(1)} collective-permute-done((f32[192,2,128]{2,0,1:T(8,128)S(1)}, f32[192,2,128]{2,0,1:T(8,128)S(1)}, u32[]{:S(2)}, u32[]{:S(2)}) %collective-permute-start.2) | collective-permute-done | bytes 196640 | tf_op jit(solution)/shard_map/ppermute | solution.py:88
  61.8 4.9 %collective-permute-done.3 = f32[192,2,128]{2,0,1:T(8,128)S(1)} collective-permute-done((f32[192,2,128]{2,0,1:T(8,128)S(1)}, f32[192,2,128]{2,0,1:T(8,128)S(1)}, u32[]{:S(2)}, u32[]{:S(2)}) %collective-permute-start.3) | collective-permute-done | bytes 196640 | tf_op jit(solution)/shard_map/ppermute | solution.py:88
  66.9 0.2 convolution_bitcast_fusion
  67.2 0.3 convolution_bitcast_fusion.1
  67.5 1.1 %copy.86 = f32[192,2,2,128]{3,2,1,0:T(2,128)} copy(f32[192,2,2,128]{3,0,1,2:T(8,128)S(1)} %pad_maximum_fusion) | data formatting | bytes 786432 | tf_op jit(solution)/shard_map/stack | solution.py:186
  68.5 5.6 %all-to-all-start.1 = ((f32[32,24,128]{2,1,0:T(8,128)}), f32[32,24,128]{2,1,0:T(8,128)S(1)}, u32[]{:S(2)}, u32[]{:S(2)}) async-start(f32[32,24,128]{2,1,0:T(8,128)} %bitcast.18), calls=%async_computation.1 | async-start | bytes 786432 | tf_op jit(solution)/shard_map/all_to_all | solution.py:188
  74.1 0.5 iota_compare_fusion.7
  74.6 0.8 copy.88
  75.5 0.3 reshape.263
  75.8 3.1 %fusion.77 = (f32[96,2,8]{2,1,0:T(2,128)}, f32[96,2,1,8,64]{4,3,1,0,2:T(8,128)S(1)}) fusion(bf16[96,2,8,128]{3,2,1,0:T(8,128)(2,1)S(1)} %reshape.263, bf16[96,64,128]{2,1,0:T(8,128)(2,1)} %param.17, pred[96,64]{1,0:T(8,128)(4,1)S(1)} %iota_compare_fusion.4), kind=kOutput, calls=%fused_computation.105 | convolution fusion | flops 25459200 | bytes 2371584 | tf_op jit(solution)/shard_map/rthgd,rjhd->rthgj/dot_general | solution.py:49
  78.9 9.2 %all-to-all-done.1 = f32[32,24,128]{2,1,0:T(8,128)S(1)} async-done(((f32[32,24,128]{2,1,0:T(8,128)}), f32[32,24,128]{2,1,0:T(8,128)S(1)}, u32[]{:S(2)}, u32[]{:S(2)}) %all-to-all-start.1) | async-done | bytes 393248 | tf_op jit(solution)/shard_map/all_to_all | solution.py:188
  88.2 0.7 gather_fusion
  89.0 0.1 gather.7
  89.1 0.1 copy.87
  89.2 1.0 select_add_fusion
  90.2 0.3 fusion.87
  90.5 0.3 fusion.56
  90.9 0.3 fusion.86
  91.2 0.3 fusion.85
  91.6 0.7 copy.95
  92.3 0.7 copy.96
  93.2 0.1 copy.102
  93.3 2.5 %fusion.78 = (f32[96,2,8]{2,1,0:T(2,128)S(1)}, f32[96,2,1,8,2]{3,4,1,0,2:T(2,128)S(1)}) fusion(bf16[96,2,128,1]{2,1,3,0:T(2,128)(2,1)S(1)} %copy.102, bf16[96,2,8,128]{3,2,1,0:T(8,128)(2,1)S(1)} %reshape.263, pred[2,2]{1,0:T(4,128)(4,1)} %iota_compare_fusion.7), kind=kOutput, calls=%fused_computation.106 | convolution fusion | flops 794112 | bytes 460804 | tf_op jit(solution)/shard_map/rthgd,rshd->rthgs/dot_general | solution.py:55
  95.9 0.6 fusion.41
  96.5 0.4 fusion.46
  97.0 0.4 fusion.47
  97.4 0.6 fusion.33
  98.0 0.8 convert_element_type.123
  (47 shorter events, 1.2 us)
Async XLA Ops:
  0.6 96.7 %copy-start = (bf16[96,64,128]{2,1,0:T(8,128)(2,1)S(1)}, bf16[96,64,128]{2,1,0:T(8,128)(2,1)}, u32[]{:S(2)}) copy-start(bf16[96,64,128]{2,1,0:T(8,128)(2,1)} %param.18) | copy-start | bytes 4718596
  0.6 5.4 %copy-start.8 = (s32[96]{0:T(128)S(1)}, s32[96]{0:T(128)}, u32[]{:S(2)}) copy-start(s32[96]{0:T(128)} %param.15) | copy-start | bytes 1156
  0.7 5.9 %copy-start.6 = (bf16[8192]{0:T(1024)(128)(2,1)S(1)}, bf16[8192]{0:T(1024)(128)(2,1)}, u32[]{:S(2)}) copy-start(bf16[8192]{0:T(1024)(128)(2,1)} %param.11) | copy-start | bytes 49156
  10.1 39.5 %all-to-all-start = ((bf16[32,13,1024]{2,1,0:T(8,128)(2,1)}), bf16[32,13,1024]{2,1,0:T(8,128)(2,1)S(1)}, u32[]{:S(2)}, u32[]{:S(2)}) async-start(bf16[32,13,1024]{2,1,0:T(8,128)(2,1)} %fusion.38), calls=%async_computation | async-start | bytes 2097152 | tf_op jit(solution)/shard_map/all_to_all | solution.py:158
  32.8 6.3 %copy-start.1 = (bf16[256,8192]{1,0:T(8,128)(2,1)S(1)}, bf16[256,8192]{1,0:T(8,128)(2,1)}, u32[]{:S(2)}) copy-start(bf16[256,8192]{1,0:T(8,128)(2,1)} %copy.79) | copy-start | bytes 12582916
  50.5 16.4 %copy-start.5 = (bf16[4,2,64,128]{3,2,1,0:T(8,128)(2,1)S(1)}, bf16[4,2,64,128]{3,2,1,0:T(8,128)(2,1)}, u32[]{:S(2)}) copy-start(bf16[4,2,64,128]{3,2,1,0:T(8,128)(2,1)} %param.14) | copy-start | bytes 393220
  52.3 22.3 %copy-start.4 = (f32[96,2,2,128]{3,0,2,1:T(8,128)S(1)}, f32[96,2,2,128]{3,0,2,1:T(8,128)}, u32[]{:S(2)}) copy-start(f32[96,2,2,128]{3,0,2,1:T(8,128)} %fusion.4) | copy-start | bytes 589828
  52.4 23.1 %copy-start.3 = (bf16[96,2,1024]{2,1,0:T(2,128)(2,1)S(1)}, bf16[96,2,1024]{2,1,0:T(2,128)(2,1)}, u32[]{:S(2)}) copy-start(bf16[96,2,1024]{2,1,0:T(2,128)(2,1)} %param.16) | copy-start | bytes 1179652
  52.4 1.5 %collective-permute-start = (f32[192,2,128]{2,0,1:T(8,128)S(1)}, f32[192,2,128]{2,0,1:T(8,128)S(1)}, u32[]{:S(2)}, u32[]{:S(2)}) collective-permute-start(f32[192,2,128]{2,0,1:T(8,128)S(1)} %fusion.26), channel_id=1, source_target_pairs={{0,1},{1,0},{2,3},{3,2},{4,5},{5,4},{6,7},{7,6},{8,9},{9,8},{10,11... | collective-permute-start | bytes 589832 | tf_op jit(solution)/shard_map/ppermute | solution.py:86
  53.9 7.9 %collective-permute-start.2 = (f32[192,2,128]{2,0,1:T(8,128)S(1)}, f32[192,2,128]{2,0,1:T(8,128)S(1)}, u32[]{:S(2)}, u32[]{:S(2)}) collective-permute-start(f32[192,2,128]{2,0,1:T(8,128)S(1)} %add.83), channel_id=1, source_target_pairs={{0,2},{1,3},{2,4},{3,5},{4,6},{5,7},{6,0},{7,1},{8,10},{9,11},{10,... | collective-permute-start | bytes 589832 | tf_op jit(solution)/shard_map/ppermute | solution.py:88
  54.5 12.2 %collective-permute-start.3 = (f32[192,2,128]{2,0,1:T(8,128)S(1)}, f32[192,2,128]{2,0,1:T(8,128)S(1)}, u32[]{:S(2)}, u32[]{:S(2)}) collective-permute-start(f32[192,2,128]{2,0,1:T(8,128)S(1)} %add.83), channel_id=1, source_target_pairs={{0,6},{1,7},{2,0},{3,1},{4,2},{5,3},{6,4},{7,5},{8,14},{9,15},{10,... | collective-permute-start | bytes 589832 | tf_op jit(solution)/shard_map/ppermute | solution.py:88
  56.0 10.7 %collective-permute-start.1 = (f32[192,2,128]{2,0,1:T(8,128)S(1)}, f32[192,2,128]{2,0,1:T(8,128)S(1)}, u32[]{:S(2)}, u32[]{:S(2)}) collective-permute-start(f32[192,2,128]{2,0,1:T(8,128)S(1)} %add.83), channel_id=1, source_target_pairs={{0,4},{1,5},{2,6},{3,7},{4,0},{5,1},{6,2},{7,3},{8,12},{9,13},{10,... | collective-permute-start | bytes 589832 | tf_op jit(solution)/shard_map/ppermute | solution.py:88
  57.4 18.3 %copy-start.7 = (s32[96]{0:T(128)S(1)}, s32[96]{0:T(128)}, u32[]{:S(2)}) copy-start(s32[96]{0:T(128)} %param.19) | copy-start | bytes 1156
  68.5 19.7 %all-to-all-start.1 = ((f32[32,24,128]{2,1,0:T(8,128)}), f32[32,24,128]{2,1,0:T(8,128)S(1)}, u32[]{:S(2)}, u32[]{:S(2)}) async-start(f32[32,24,128]{2,1,0:T(8,128)} %bitcast.18), calls=%async_computation.1 | async-start | bytes 786432 | tf_op jit(solution)/shard_map/all_to_all | solution.py:188
  88.9 6.9 %copy-start.2 = (f32[96,2,8]{2,1,0:T(2,128)S(1)}, f32[96,2,8]{2,1,0:T(2,128)}, u32[]{:S(2)}) copy-start(f32[96,2,8]{2,1,0:T(2,128)} %get-tuple-element.24) | copy-start | bytes 18436

commit v11 on v10

--- a/solution.py
+++ b/solution.py
@@ -187,9 +187,12 @@
     delta_send = delta_slots.reshape(owner_count, cap * token_count * 2, column_count)
     delta_recv = lax.all_to_all(delta_send, "adapter", 0, 0, tiled=True)
     delta_rows = delta_recv.reshape(slot_total, token_count * 2 * column_count)
-    adapter_update = jnp.take(delta_rows, slot_of, axis=0).reshape(
-        row_count, token_count, 2, column_count
-    )
+    adapter_update = jnp.dot(
+        pick.astype(jnp.float32).T,
+        delta_rows,
+        precision=lax.Precision.HIGHEST,
+        preferred_element_type=jnp.float32,
+    ).reshape(row_count, token_count, 2, column_count)
 
     projected_output = base_proj + adapter_update
     positions = (cached_length[:, None] + jnp.arange(token_count, dtype=jnp.int32)[None, :]).astype(

time: 100 us -> 114 us (1.14)
  waiting for transfers between devices: 25.8 us -> 40 us
  matrix products: 14.1 us -> 17.9 us
  local copies, waits for them, and re-layouts: 18.2 us -> 15.3 us
    all_to_all x1, waiting for transfers between devices: 5.9 us -> 28 us  [body(): recv = lax.all_to_all(send, 'adapter', 0, 0, tiled=True)]
    ppermute x3, waiting for transfers between devices: 9.22 us -> 2.33 us  [butterfly_sum(): lax.ppermute(value, axis_name, [(i, (i + 2 * k) % member_count) for i in...]
    dot_general x1, matrix products: 4.6 us -> 7.08 us  [body(): jnp.dot(normed_input.reshape(row_count * token_count, model_width), key_v...]
    unnamed x22 -> x24, local copies, waits for them, and re-layouts: 6.26 us -> 4.12 us
    dot_general x0 -> x1, matrix products: none -> 1.64 us  [body(): jnp.dot(pick.astype(jnp.float32).T, delta_rows, precision=lax.Precision.H...]
    ppermute x1, waiting for transfers between devices: 1.42 us -> 0.01 us  [butterfly_sum(): lax.ppermute(value, axis_name, [(i, i ^ 1) for i in range(member_count)])]
  transfers between devices with their start and end apart: 6 -> 6, of which waited for: 5 -> 3; matrix products, arithmetic and copies ran while one was open for 27% -> 24% of each run, Pallas kernels for 0% -> 0%
where the time goes in v11:
time: 114 us; the launch traced here: 113 us
  waiting for transfers between devices  40 us (35%)
  starting transfers between devices  21.1 us (19%)
  matrix products  17.9 us (16%)
  other arithmetic  17.7 us (16%)
  local copies, waits for them, and re-layouts  15.3 us (13%)
    all_to_all x1, waiting for transfers between devices, body(): recv = lax.all_to_all(send, 'adapter', 0, 0, tiled=True)  28 us
    all_to_all x1, starting transfers between devices, body(): recv = lax.all_to_all(send, 'adapter', 0, 0, tiled=True)  11.5 us
    all_to_all x1, waiting for transfers between devices, body(): delta_recv = lax.all_to_all(delta_send, 'adapter', 0, 0, tiled=True)  9.6 us
    dot_general x1, matrix products, body(): jnp.dot(normed_input.reshape(row_count * token_count, model_width), key_v...  7.08 us
    dot_general x1, local copies, waits for them, and re-layouts, body(): jnp.dot(normed_input.reshape(row_count * token_count, model_width), key_v...  6.37 us
    convert_element_type x1, other arithmetic, body(): (values * row_scale * input_norm_gain.astype(jnp.float32)).astype(jnp.bfl...  6.23 us
    all_to_all x1, starting transfers between devices, body(): delta_recv = lax.all_to_all(delta_send, 'adapter', 0, 0, tiled=True)  5.84 us
    reduce_sum x1, other arithmetic, body(): meansq = jnp.mean(values * values, axis=-1, keepdims=True)  5.33 us
  transfers between devices with their start and end apart: 6, of which 3 were waited for; matrix products, arithmetic and copies ran while one was open for 24% of the time, Pallas kernels for 0%

profile of v11, /device:TPU:6, one launch (start us, length us, event | category | flops | bytes accessed | tf_op | source)
XLA Modules:
  0.0 113.1 jit_solution(14528064450327107837)
XLA Ops:
  0.7 5.3 %fusion = f32[96,2]{1,0:T(8,128)S(1)} fusion(bf16[96,2,8192]{2,1,0:T(2,128)(2,1)} %param.10), kind=kLoop, calls=%fused_computation.2 | loop fusion | flops 4718400 | bytes 3146496 | tf_op jit(solution)/shard_map/reduce_sum | solution.py:117
  6.0 0.2 convert_reduce_fusion
  6.2 0.2 fusion.52
  6.5 0.1 reshape.272
  6.6 1.5 %multiply_convert_fusion = bf16[96,2,1024]{2,1,0:T(2,128)(2,1)S(1)} fusion(f32[1024]{0:T(1024)S(1)} %dynamic-slice_convert_fusion, f32[96,2]{1,0:T(8,128)S(1)} %add_rsqrt_fusion, bf16[96,2,8192]{2,1,0:T(2,128)(2,1)} %param.10, s32[]{:T(128)S(6)} %select_n.21), kind=kLoop, calls=%fused_computation.37 | loop fusion | flops 786432 | bytes 791300 | tf_op jit(solution)/shard_map/convert_element_type | solution.py:143
  8.2 0.5 convolution_convert_fusion
  8.7 0.4 reshape.248
  9.0 1.2 %fusion.38 = bf16[32,13,1024]{2,1,0:T(8,128)(2,1)} fusion(bf16[32,1,6]{2,1,0:T(2,128)(2,1)S(1)} %reshape.272, bf16[32,12,1024]{2,1,0:T(8,128)(2,1)S(1)} %reshape.248), kind=kLoop, calls=%fused_computation.32 | loop fusion | flops 2555904 | bytes 1638784 | tf_op jit(solution)/shard_map/concatenate | solution.py:157
  10.2 11.5 %all-to-all-start = ((bf16[32,13,1024]{2,1,0:T(8,128)(2,1)}), bf16[32,13,1024]{2,1,0:T(8,128)(2,1)S(1)}, u32[]{:S(2)}, u32[]{:S(2)}) async-start(bf16[32,13,1024]{2,1,0:T(8,128)(2,1)} %fusion.38), calls=%async_computation | async-start | bytes 2097152 | tf_op jit(solution)/shard_map/all_to_all | solution.py:158
  21.7 28.0 %all-to-all-done = bf16[32,13,1024]{2,1,0:T(8,128)(2,1)S(1)} async-done(((bf16[32,13,1024]{2,1,0:T(8,128)(2,1)}), bf16[32,13,1024]{2,1,0:T(8,128)(2,1)S(1)}, u32[]{:S(2)}, u32[]{:S(2)}) %all-to-all-start) | async-done | bytes 852000 | tf_op jit(solution)/shard_map/all_to_all | solution.py:158
  49.8 0.1 reshape.256
  49.9 0.6 reshape.250
  50.6 2.0 %fusion.26 = f32[192,2,128]{2,0,1:T(8,128)S(1)} fusion(bf16[4,1024,128]{2,1,0:T(8,128)(2,1)} %param.13, bf16[192,2,1024,1]{2,1,0,3:T(2,128)(2,1)S(1)} %bitcast.168, f32[192,4]{0,1:T(4,128)S(1)} %get-tuple-element.20), kind=kOutput, calls=%fused_computation.22 | convolution fusion | flops 402997248 | bytes 2034688 | tf_op jit(solution)/shard_map/euz,nzs->euns/dot_general | solution.py:166
  52.5 0.3 collective-permute-start
  52.8 6.2 %fusion.3 = bf16[96,2,8192,1]{2,1,0,3:T(2,128)(2,1)} fusion(bf16[96,2,8192]{2,1,0:T(2,128)(2,1)S(1)} %copy-done.1, f32[8192]{0:T(1024)S(1)} %convert_element_type.101, f32[96,2]{1,0:T(8,128)S(1)} %add_rsqrt_fusion), kind=kLoop, calls=%fused_computation.6 | loop fusion | flops 6291456 | bytes 6324992 | tf_op jit(solution)/shard_map/convert_element_type | solution.py:119
  59.1 2.5 %copy.128 = bf16[1024,8,2,128]{3,1,2,0:T(8,128)(2,1)} copy(bf16[1024,8,2,128]{3,2,1,0:T(2,128)(2,1)S(1)} %bitcast.163) | data formatting | bytes 8388608
  61.6 6.4 %copy.79 = bf16[256,8192]{1,0:T(8,128)(2,1)} copy(bf16[256,8192]{0,1:T(8,128)(2,1)} %bitcast.161) | data formatting | bytes 8388608 | tf_op jit(solution)/shard_map/dot_general | solution.py:120
  68.0 0.6 collective-permute-start.2
  68.5 1.5 %collective-permute-start.3 = (f32[192,2,128]{2,0,1:T(8,128)S(1)}, f32[192,2,128]{2,0,1:T(8,128)S(1)}, u32[]{:S(2)}, u32[]{:S(2)}) collective-permute-start(f32[192,2,128]{2,0,1:T(8,128)S(1)} %add.73), channel_id=1, source_target_pairs={{0,6},{1,7},{2,0},{3,1},{4,2},{5,3},{6,4},{7,5},{8,14},{9,15},{10,... | collective-permute-start | bytes 589832 | tf_op jit(solution)/shard_map/ppermute | solution.py:88
  70.1 1.4 %collective-permute-start.1 = (f32[192,2,128]{2,0,1:T(8,128)S(1)}, f32[192,2,128]{2,0,1:T(8,128)S(1)}, u32[]{:S(2)}, u32[]{:S(2)}) collective-permute-start(f32[192,2,128]{2,0,1:T(8,128)S(1)} %add.73), channel_id=1, source_target_pairs={{0,4},{1,5},{2,6},{3,7},{4,0},{5,1},{6,2},{7,3},{8,12},{9,13},{10,... | collective-permute-start | bytes 589832 | tf_op jit(solution)/shard_map/ppermute | solution.py:88
  71.5 7.1 %fusion.4 = f32[96,2,2,128]{3,0,2,1:T(8,128)S(1)} fusion(bf16[2,128,8192,1]{2,1,0,3:T(8,128)(2,1)} %bitcast.164, bf16[96,2,8192,1]{2,1,0,3:T(2,128)(2,1)} %fusion.3), kind=kOutput, calls=%fused_computation.7 | convolution fusion | flops 805306368 | bytes 7536640 | tf_op jit(solution)/shard_map/dot_general | solution.py:120
  78.6 2.3 %collective-permute-done.3 = f32[192,2,128]{2,0,1:T(8,128)S(1)} collective-permute-done((f32[192,2,128]{2,0,1:T(8,128)S(1)}, f32[192,2,128]{2,0,1:T(8,128)S(1)}, u32[]{:S(2)}, u32[]{:S(2)}) %collective-permute-start.3) | collective-permute-done | bytes 196640 | tf_op jit(solution)/shard_map/ppermute | solution.py:88
  81.0 0.1 copy.83
  81.2 0.2 convolution_bitcast_fusion
  81.5 0.3 convolution_bitcast_fusion.1
  81.7 1.1 copy.86
  82.8 5.8 %all-to-all-start.1 = ((f32[32,24,128]{2,1,0:T(8,128)}), f32[32,24,128]{2,1,0:T(8,128)S(1)}, u32[]{:S(2)}, u32[]{:S(2)}) async-start(f32[32,24,128]{2,1,0:T(8,128)} %bitcast.19), calls=%async_computation.1 | async-start | bytes 786432 | tf_op jit(solution)/shard_map/all_to_all | solution.py:188
  88.7 0.5 iota_compare_fusion.7
  89.2 0.8 copy.88
  90.0 0.3 reshape.253
  90.4 3.1 %fusion.81 = (f32[96,2,8]{2,1,0:T(2,128)}, f32[96,2,1,8,64]{4,3,1,0,2:T(8,128)S(1)}) fusion(bf16[96,2,8,128]{3,2,1,0:T(8,128)(2,1)S(1)} %reshape.253, bf16[96,64,128]{2,1,0:T(8,128)(2,1)} %param.17, pred[96,64]{1,0:T(8,128)(4,1)S(1)} %iota_compare_fusion.4), kind=kOutput, calls=%fused_computation.104 | convolution fusion | flops 25459200 | bytes 2371584 | tf_op jit(solution)/shard_map/rthgd,rjhd->rthgj/dot_general | solution.py:49
  93.5 9.6 %all-to-all-done.1 = f32[32,24,128]{2,1,0:T(8,128)S(1)} async-done(((f32[32,24,128]{2,1,0:T(8,128)}), f32[32,24,128]{2,1,0:T(8,128)S(1)}, u32[]{:S(2)}, u32[]{:S(2)}) %all-to-all-start.1) | async-done | bytes 393248 | tf_op jit(solution)/shard_map/all_to_all | solution.py:188
  103.2 0.3 dot_general.52
  103.4 1.6 %convolution_add_fusion = f32[96,2,2,128]{0,3,1,2:T(8,128)S(1)} fusion(f32[96,2,2,128]{0,3,1,2:T(8,128)} %copy.88, f32[2,2,128,192]{2,1,0,3:T(2,128)S(1)} %dot_general.52, s32[96]{0:T(128)S(1)} %multiply_add_fusion), kind=kOutput, calls=%fused_computation.26 | convolution fusion | flops 113313792 | bytes 786816 | tf_op jit(solution)/shard_map/dot_general | solution.py:190
  105.1 0.3 fusion.91
  105.4 0.3 fusion.59
  105.8 0.3 fusion.90
  106.1 0.3 fusion.89
  106.4 0.7 copy.96
  107.2 0.7 copy.97
  107.9 0.1 copy.107
  108.0 0.1 copy.105
  108.2 1.9 %fusion.82 = (f32[96,2,8]{2,1,0:T(2,128)S(1)}, f32[96,2,1,8,2]{3,4,1,0,2:T(2,128)S(1)}) fusion(bf16[96,2,128,1]{2,1,3,0:T(2,128)(2,1)S(1)} %copy.105, bf16[96,2,8,128]{3,2,1,0:T(8,128)(2,1)S(1)} %reshape.253, pred[2,2]{1,0:T(4,128)(4,1)S(1)} %copy-done.9), kind=kOutput, calls=%fused_computation.105 | convolution fusion | flops 794112 | bytes 460804 | tf_op jit(solution)/shard_map/rthgd,rshd->rthgs/dot_general | solution.py:55
  110.1 0.6 fusion.41
  110.7 0.4 fusion.47
  111.2 0.4 fusion.48
  111.6 0.6 fusion.33
  112.2 0.8 convert_element_type.124
  (45 shorter events, 0.7 us)
Async XLA Ops:
  0.6 111.0 %copy-start = (bf16[96,64,128]{2,1,0:T(8,128)(2,1)S(1)}, bf16[96,64,128]{2,1,0:T(8,128)(2,1)}, u32[]{:S(2)}) copy-start(bf16[96,64,128]{2,1,0:T(8,128)(2,1)} %param.18) | copy-start | bytes 4718596
  0.6 5.4 %copy-start.8 = (s32[96]{0:T(128)S(1)}, s32[96]{0:T(128)}, u32[]{:S(2)}) copy-start(s32[96]{0:T(128)} %param.15) | copy-start | bytes 1156
  0.7 5.9 %copy-start.6 = (bf16[8192]{0:T(1024)(128)(2,1)S(1)}, bf16[8192]{0:T(1024)(128)(2,1)}, u32[]{:S(2)}) copy-start(bf16[8192]{0:T(1024)(128)(2,1)} %param.11) | copy-start | bytes 49156
  10.2 39.5 %all-to-all-start = ((bf16[32,13,1024]{2,1,0:T(8,128)(2,1)}), bf16[32,13,1024]{2,1,0:T(8,128)(2,1)S(1)}, u32[]{:S(2)}, u32[]{:S(2)}) async-start(bf16[32,13,1024]{2,1,0:T(8,128)(2,1)} %fusion.38), calls=%async_computation | async-start | bytes 2097152 | tf_op jit(solution)/shard_map/all_to_all | solution.py:158
  50.5 2.3 %copy-start.1 = (bf16[96,2,8192]{2,1,0:T(2,128)(2,1)S(1)}, bf16[96,2,8192]{2,1,0:T(2,128)(2,1)}, u32[]{:S(2)}) copy-start(bf16[96,2,8192]{2,1,0:T(2,128)(2,1)} %param.10) | copy-start | bytes 9437188
  52.5 6.5 %copy-start.2 = (bf16[8192,2,128]{2,1,0:T(2,128)(2,1)S(1)}, bf16[8192,2,128]{2,1,0:T(2,128)(2,1)}, u32[]{:S(2)}) copy-start(bf16[8192,2,128]{2,1,0:T(2,128)(2,1)} %param.12) | copy-start | bytes 12582916
  52.5 15.4 %collective-permute-start = (f32[192,2,128]{2,0,1:T(8,128)S(1)}, f32[192,2,128]{2,0,1:T(8,128)S(1)}, u32[]{:S(2)}, u32[]{:S(2)}) collective-permute-start(f32[192,2,128]{2,0,1:T(8,128)S(1)} %fusion.26), channel_id=1, source_target_pairs={{0,1},{1,0},{2,3},{3,2},{4,5},{5,4},{6,7},{7,6},{8,9},{9,8},{10,11... | collective-permute-start | bytes 589832 | tf_op jit(solution)/shard_map/ppermute | solution.py:86
  68.0 10.7 %collective-permute-start.2 = (f32[192,2,128]{2,0,1:T(8,128)S(1)}, f32[192,2,128]{2,0,1:T(8,128)S(1)}, u32[]{:S(2)}, u32[]{:S(2)}) collective-permute-start(f32[192,2,128]{2,0,1:T(8,128)S(1)} %add.73), channel_id=1, source_target_pairs={{0,2},{1,3},{2,4},{3,5},{4,6},{5,7},{6,0},{7,1},{8,10},{9,11},{10,... | collective-permute-start | bytes 589832 | tf_op jit(solution)/shard_map/ppermute | solution.py:88
  68.5 12.4 %collective-permute-start.3 = (f32[192,2,128]{2,0,1:T(8,128)S(1)}, f32[192,2,128]{2,0,1:T(8,128)S(1)}, u32[]{:S(2)}, u32[]{:S(2)}) collective-permute-start(f32[192,2,128]{2,0,1:T(8,128)S(1)} %add.73), channel_id=1, source_target_pairs={{0,6},{1,7},{2,0},{3,1},{4,2},{5,3},{6,4},{7,5},{8,14},{9,15},{10,... | collective-permute-start | bytes 589832 | tf_op jit(solution)/shard_map/ppermute | solution.py:88
  70.1 10.9 %collective-permute-start.1 = (f32[192,2,128]{2,0,1:T(8,128)S(1)}, f32[192,2,128]{2,0,1:T(8,128)S(1)}, u32[]{:S(2)}, u32[]{:S(2)}) collective-permute-start(f32[192,2,128]{2,0,1:T(8,128)S(1)} %add.73), channel_id=1, source_target_pairs={{0,4},{1,5},{2,6},{3,7},{4,0},{5,1},{6,2},{7,3},{8,12},{9,13},{10,... | collective-permute-start | bytes 589832 | tf_op jit(solution)/shard_map/ppermute | solution.py:88
  71.5 9.7 %copy-start.5 = (bf16[4,2,64,128]{3,2,1,0:T(8,128)(2,1)S(1)}, bf16[4,2,64,128]{3,2,1,0:T(8,128)(2,1)}, u32[]{:S(2)}) copy-start(bf16[4,2,64,128]{3,2,1,0:T(8,128)(2,1)} %param.14) | copy-start | bytes 393220
  78.6 11.4 %copy-start.4 = (bf16[96,2,1024]{2,1,0:T(2,128)(2,1)S(1)}, bf16[96,2,1024]{2,1,0:T(2,128)(2,1)}, u32[]{:S(2)}) copy-start(bf16[96,2,1024]{2,1,0:T(2,128)(2,1)} %param.16) | copy-start | bytes 1179652
  78.6 11.6 %copy-start.7 = (s32[96]{0:T(128)S(1)}, s32[96]{0:T(128)}, u32[]{:S(2)}) copy-start(s32[96]{0:T(128)} %param.19) | copy-start | bytes 1156
  82.8 20.3 %all-to-all-start.1 = ((f32[32,24,128]{2,1,0:T(8,128)}), f32[32,24,128]{2,1,0:T(8,128)S(1)}, u32[]{:S(2)}, u32[]{:S(2)}) async-start(f32[32,24,128]{2,1,0:T(8,128)} %bitcast.19), calls=%async_computation.1 | async-start | bytes 786432 | tf_op jit(solution)/shard_map/all_to_all | solution.py:188
  90.4 17.8 %copy-start.9 = (pred[2,2]{1,0:T(4,128)(4,1)S(1)}, pred[2,2]{1,0:T(4,128)(4,1)}, u32[]{:S(2)}) copy-start(pred[2,2]{1,0:T(4,128)(4,1)} %iota_compare_fusion.7) | copy-start | bytes 16
  103.4 6.6 %copy-start.3 = (f32[96,2,8]{2,1,0:T(2,128)S(1)}, f32[96,2,8]{2,1,0:T(2,128)}, u32[]{:S(2)}) copy-start(f32[96,2,8]{2,1,0:T(2,128)} %get-tuple-element.22) | copy-start | bytes 18436

commit v12 on v11

--- a/solution.py
+++ b/solution.py
@@ -167,6 +167,7 @@
         "euz,nzs->euns", got_rows, adapter_down_weight, preferred_element_type=jnp.float32
     )
     partial_rank = jnp.sum(down_all * selector[:, None, :, None], axis=2)
+    partial_rank, base_proj = lax.optimization_barrier((partial_rank, base_proj))
     rank_hidden = butterfly_sum(partial_rank, "tensor").astype(jnp.bfloat16)
 
     rank_selector = selector.astype(jnp.bfloat16)

time: 114 us -> 102 us (0.89)
  waiting for transfers between devices: 40 us -> 24.8 us
  local copies, waits for them, and re-layouts: 15.3 us -> 18.4 us
  matrix products: 17.9 us -> 15.9 us
  other arithmetic: 17.7 us -> 19.2 us
    all_to_all x1, waiting for transfers between devices: 28 us -> 5.89 us  [body(): recv = lax.all_to_all(send, 'adapter', 0, 0, tiled=True)]
    ppermute x3, waiting for transfers between devices: 2.33 us -> 9.24 us  [butterfly_sum(): lax.ppermute(value, axis_name, [(i, (i + 2 * k) % member_count) for i in...]
    dot_general x1, matrix products: 7.08 us -> 4.61 us  [body(): jnp.dot(normed_input.reshape(row_count * token_count, model_width), key_v...]
    unnamed x24, local copies, waits for them, and re-layouts: 4.12 us -> 6.26 us
    ppermute x1, waiting for transfers between devices: 0.01 us -> 1.43 us  [butterfly_sum(): lax.ppermute(value, axis_name, [(i, i ^ 1) for i in range(member_count)])]
    all_to_all x1, waiting for transfers between devices: 9.6 us -> 8.27 us  [body(): delta_recv = lax.all_to_all(delta_send, 'adapter', 0, 0, tiled=True)]
  transfers between devices with their start and end apart: 6 -> 6, of which waited for: 3 -> 5; matrix products, arithmetic and copies ran while one was open for 24% -> 28% of each run, Pallas kernels for 0% -> 0%
where the time goes in v12:
time: 102 us; the launch traced here: 100 us
  waiting for transfers between devices  24.8 us (24%)
  starting transfers between devices  21 us (21%)
  other arithmetic  19.2 us (19%)
  local copies, waits for them, and re-layouts  18.4 us (18%)
  matrix products  15.9 us (16%)
  between operations  1.05 us (1%)
    all_to_all x1, starting transfers between devices, body(): recv = lax.all_to_all(send, 'adapter', 0, 0, tiled=True)  11.7 us
    ppermute x3, waiting for transfers between devices, butterfly_sum(): lax.ppermute(value, axis_name, [(i, (i + 2 * k) % member_count) for i in...  9.24 us
    all_to_all x1, waiting for transfers between devices, body(): delta_recv = lax.all_to_all(delta_send, 'adapter', 0, 0, tiled=True)  8.27 us
    dot_general x1, local copies, waits for them, and re-layouts, body(): jnp.dot(normed_input.reshape(row_count * token_count, model_width), key_v...  6.38 us
    convert_element_type x1, other arithmetic, body(): (values * row_scale * input_norm_gain.astype(jnp.float32)).astype(jnp.bfl...  6.29 us
    unnamed x24, local copies, waits for them, and re-layouts  6.26 us
    all_to_all x1, waiting for transfers between devices, body(): recv = lax.all_to_all(send, 'adapter', 0, 0, tiled=True)  5.89 us
    all_to_all x1, starting transfers between devices, body(): delta_recv = lax.all_to_all(delta_send, 'adapter', 0, 0, tiled=True)  5.71 us
  transfers between devices with their start and end apart: 6, of which 5 were waited for; matrix products, arithmetic and copies ran while one was open for 28% of the time, Pallas kernels for 0%

profile of v12, /device:TPU:6, one launch (start us, length us, event | category | flops | bytes accessed | tf_op | source)
XLA Modules:
  0.0 100.4 jit_solution(15196513464758281919)
XLA Ops:
  0.7 0.8 and_select_fusion
  1.4 0.2 convert_reduce_fusion
  1.6 0.7 multiply_add_fusion
  2.3 0.9 fusion.52
  3.2 0.1 reshape.272
  3.3 5.2 %fusion = f32[96,2]{1,0:T(8,128)S(1)} fusion(bf16[96,2,8192]{2,1,0:T(2,128)(2,1)} %param.10), kind=kLoop, calls=%fused_computation.2 | loop fusion | flops 4718400 | bytes 3146496 | tf_op jit(solution)/shard_map/reduce_sum | solution.py:117
  8.6 1.5 %multiply_convert_fusion = bf16[96,2,1024]{2,1,0:T(2,128)(2,1)S(1)} fusion(f32[1024]{0:T(1024)S(1)} %dynamic-slice_convert_fusion, f32[96,2]{1,0:T(8,128)S(1)} %add_rsqrt_fusion, bf16[96,2,8192]{2,1,0:T(2,128)(2,1)} %param.10, s32[]{:T(128)S(6)} %select_n.21), kind=kLoop, calls=%fused_computation.37 | loop fusion | flops 786432 | bytes 791300 | tf_op jit(solution)/shard_map/convert_element_type | solution.py:143
  10.1 0.5 convolution_convert_fusion
  10.6 0.4 reshape.247
  11.0 1.2 %fusion.38 = bf16[32,13,1024]{2,1,0:T(8,128)(2,1)} fusion(bf16[32,1,6]{2,1,0:T(2,128)(2,1)S(1)} %reshape.272, bf16[32,12,1024]{2,1,0:T(8,128)(2,1)S(1)} %reshape.247), kind=kLoop, calls=%fused_computation.32 | loop fusion | flops 2555904 | bytes 1638784 | tf_op jit(solution)/shard_map/concatenate | solution.py:157
  12.2 11.7 %all-to-all-start = ((bf16[32,13,1024]{2,1,0:T(8,128)(2,1)}), bf16[32,13,1024]{2,1,0:T(8,128)(2,1)S(1)}, u32[]{:S(2)}, u32[]{:S(2)}) async-start(bf16[32,13,1024]{2,1,0:T(8,128)(2,1)} %fusion.38), calls=%async_computation | async-start | bytes 2097152 | tf_op jit(solution)/shard_map/all_to_all | solution.py:158
  23.9 4.7 %copy.128 = bf16[1024,8,2,128]{3,1,2,0:T(8,128)(2,1)} copy(bf16[1024,8,2,128]{3,2,1,0:T(2,128)(2,1)} %bitcast.163) | data formatting | bytes 8388608
  28.6 6.4 %copy.81 = bf16[256,8192]{1,0:T(8,128)(2,1)} copy(bf16[256,8192]{0,1:T(8,128)(2,1)} %bitcast.161) | data formatting | bytes 8388608 | tf_op jit(solution)/shard_map/dot_general | solution.py:120
  35.0 6.3 %fusion.3 = bf16[96,2,8192,1]{2,1,0,3:T(2,128)(2,1)S(1)} fusion(bf16[96,2,8192]{2,1,0:T(2,128)(2,1)} %param.10, f32[8192]{0:T(1024)S(1)} %convert_element_type.111, f32[96,2]{1,0:T(8,128)S(1)} %add_rsqrt_fusion), kind=kLoop, calls=%fused_computation.6 | loop fusion | flops 6291456 | bytes 6324992 | tf_op jit(solution)/shard_map/convert_element_type | solution.py:119
  41.3 4.6 %fusion.4 = f32[96,2,2,128]{3,0,2,1:T(8,128)} fusion(bf16[2,128,8192,1]{2,1,0,3:T(8,128)(2,1)S(1)} %bitcast.164, bf16[96,2,8192,1]{2,1,0,3:T(2,128)(2,1)S(1)} %fusion.3), kind=kOutput, calls=%fused_computation.7 | convolution fusion | flops 805306368 | bytes 7536640 | tf_op jit(solution)/shard_map/dot_general | solution.py:120
  45.9 5.9 %all-to-all-done = bf16[32,13,1024]{2,1,0:T(8,128)(2,1)S(1)} async-done(((bf16[32,13,1024]{2,1,0:T(8,128)(2,1)}), bf16[32,13,1024]{2,1,0:T(8,128)(2,1)S(1)}, u32[]{:S(2)}, u32[]{:S(2)}) %all-to-all-start) | async-done | bytes 852000 | tf_op jit(solution)/shard_map/all_to_all | solution.py:158
  51.8 0.6 reshape.249
  52.6 1.8 %fusion.26 = f32[192,2,128]{2,0,1:T(8,128)S(1)} fusion(bf16[4,1024,128]{2,1,0:T(8,128)(2,1)} %param.13, bf16[192,2,1024,1]{2,1,0,3:T(2,128)(2,1)S(1)} %bitcast.168, f32[192,4]{0,1:T(4,128)S(1)} %get-tuple-element.25), kind=kOutput, calls=%fused_computation.22 | convolution fusion | flops 402997248 | bytes 2034688 | tf_op jit(solution)/shard_map/euz,nzs->euns/dot_general | solution.py:166
  54.5 1.4 %collective-permute-done = f32[192,2,128]{2,0,1:T(8,128)S(1)} collective-permute-done((f32[192,2,128]{2,0,1:T(8,128)S(1)}, f32[192,2,128]{2,0,1:T(8,128)S(1)}, u32[]{:S(2)}, u32[]{:S(2)}) %collective-permute-start) | collective-permute-done | bytes 196640 | tf_op jit(solution)/shard_map/ppermute | solution.py:86
  56.0 0.6 collective-permute-start.2
  56.6 1.5 %collective-permute-start.3 = (f32[192,2,128]{2,0,1:T(8,128)S(1)}, f32[192,2,128]{2,0,1:T(8,128)S(1)}, u32[]{:S(2)}, u32[]{:S(2)}) collective-permute-start(f32[192,2,128]{2,0,1:T(8,128)S(1)} %add.73), channel_id=1, source_target_pairs={{0,6},{1,7},{2,0},{3,1},{4,2},{5,3},{6,4},{7,5},{8,14},{9,15},{10,... | collective-permute-start | bytes 589832 | tf_op jit(solution)/shard_map/ppermute | solution.py:88
  58.1 1.4 %collective-permute-start.1 = (f32[192,2,128]{2,0,1:T(8,128)S(1)}, f32[192,2,128]{2,0,1:T(8,128)S(1)}, u32[]{:S(2)}, u32[]{:S(2)}) collective-permute-start(f32[192,2,128]{2,0,1:T(8,128)S(1)} %add.73), channel_id=1, source_target_pairs={{0,4},{1,5},{2,6},{3,7},{4,0},{5,1},{6,2},{7,3},{8,12},{9,13},{10,... | collective-permute-start | bytes 589832 | tf_op jit(solution)/shard_map/ppermute | solution.py:88
  59.5 4.3 %collective-permute-done.2 = f32[192,2,128]{2,0,1:T(8,128)S(1)} collective-permute-done((f32[192,2,128]{2,0,1:T(8,128)S(1)}, f32[192,2,128]{2,0,1:T(8,128)S(1)}, u32[]{:S(2)}, u32[]{:S(2)}) %collective-permute-start.2) | collective-permute-done | bytes 196640 | tf_op jit(solution)/shard_map/ppermute | solution.py:88
  63.8 4.9 %collective-permute-done.3 = f32[192,2,128]{2,0,1:T(8,128)S(1)} collective-permute-done((f32[192,2,128]{2,0,1:T(8,128)S(1)}, f32[192,2,128]{2,0,1:T(8,128)S(1)}, u32[]{:S(2)}, u32[]{:S(2)}) %collective-permute-start.3) | collective-permute-done | bytes 196640 | tf_op jit(solution)/shard_map/ppermute | solution.py:88
  69.0 0.2 convolution_bitcast_fusion
  69.2 0.3 convolution_bitcast_fusion.1
  69.5 1.1 %copy.86 = f32[192,2,2,128]{3,2,1,0:T(2,128)} copy(f32[192,2,2,128]{3,0,1,2:T(8,128)S(1)} %pad_maximum_fusion) | data formatting | bytes 786432 | tf_op jit(solution)/shard_map/stack | solution.py:187
  70.6 5.7 %all-to-all-start.1 = ((f32[32,24,128]{2,1,0:T(8,128)}), f32[32,24,128]{2,1,0:T(8,128)S(1)}, u32[]{:S(2)}, u32[]{:S(2)}) async-start(f32[32,24,128]{2,1,0:T(8,128)} %bitcast.19), calls=%async_computation.1 | async-start | bytes 786432 | tf_op jit(solution)/shard_map/all_to_all | solution.py:189
  76.3 0.6 iota_compare_fusion.7
  76.9 0.3 reshape.253
  77.3 3.1 %fusion.81 = (f32[96,2,8]{2,1,0:T(2,128)}, f32[96,2,1,8,64]{4,3,1,0,2:T(8,128)S(1)}) fusion(bf16[96,2,8,128]{3,2,1,0:T(8,128)(2,1)S(1)} %reshape.253, bf16[96,64,128]{2,1,0:T(8,128)(2,1)} %param.17, pred[96,64]{1,0:T(8,128)(4,1)S(1)} %iota_compare_fusion.4), kind=kOutput, calls=%fused_computation.104 | convolution fusion | flops 25459200 | bytes 2371584 | tf_op jit(solution)/shard_map/rthgd,rjhd->rthgj/dot_general | solution.py:49
  80.4 1.8 %copy.88 = f32[96,2,2,128]{0,3,1,2:T(8,128)} copy(f32[96,2,2,128]{3,0,2,1:T(8,128)} %fusion.4) | data formatting | bytes 393216 | tf_op jit(solution)/shard_map/optimization_barrier | solution.py:170
  82.1 8.3 %all-to-all-done.1 = f32[32,24,128]{2,1,0:T(8,128)S(1)} async-done(((f32[32,24,128]{2,1,0:T(8,128)}), f32[32,24,128]{2,1,0:T(8,128)S(1)}, u32[]{:S(2)}, u32[]{:S(2)}) %all-to-all-start.1) | async-done | bytes 393248 | tf_op jit(solution)/shard_map/all_to_all | solution.py:189
  90.5 0.3 dot_general.52
  90.7 1.6 %convolution_add_fusion = f32[96,2,2,128]{0,3,1,2:T(8,128)S(1)} fusion(f32[96,2,2,128]{0,3,1,2:T(8,128)} %copy.88, f32[2,2,128,192]{2,1,0,3:T(2,128)S(1)} %dot_general.52, s32[96]{0:T(128)S(1)} %copy-done.7), kind=kOutput, calls=%fused_computation.26 | convolution fusion | flops 113313792 | bytes 786816 | tf_op jit(solution)/shard_map/dot_general | solution.py:191
  92.4 0.3 fusion.91
  92.7 0.3 fusion.59
  93.1 0.3 fusion.90
  93.4 0.3 fusion.89
  93.7 0.7 copy.96
  94.5 0.7 copy.97
  95.3 0.1 copy.105
  95.5 1.9 %fusion.82 = (f32[96,2,8]{2,1,0:T(2,128)S(1)}, f32[96,2,1,8,2]{3,4,1,0,2:T(2,128)S(1)}) fusion(bf16[96,2,128,1]{2,1,3,0:T(2,128)(2,1)S(1)} %copy.105, bf16[96,2,8,128]{3,2,1,0:T(8,128)(2,1)S(1)} %reshape.253, pred[2,2]{1,0:T(4,128)(4,1)S(1)} %copy-done.9), kind=kOutput, calls=%fused_computation.105 | convolution fusion | flops 794112 | bytes 460804 | tf_op jit(solution)/shard_map/rthgd,rshd->rthgs/dot_general | solution.py:55
  97.4 0.6 fusion.41
  98.0 0.4 fusion.47
  98.5 0.4 fusion.48
  98.9 0.6 fusion.33
  99.5 0.8 convert_element_type.124
  (45 shorter events, 1.1 us)
Async XLA Ops:
  0.6 98.3 %copy-start = (bf16[96,64,128]{2,1,0:T(8,128)(2,1)S(1)}, bf16[96,64,128]{2,1,0:T(8,128)(2,1)}, u32[]{:S(2)}) copy-start(bf16[96,64,128]{2,1,0:T(8,128)(2,1)} %param.18) | copy-start | bytes 4718596
  0.6 7.9 %copy-start.5 = (bf16[8192]{0:T(1024)(128)(2,1)S(1)}, bf16[8192]{0:T(1024)(128)(2,1)}, u32[]{:S(2)}) copy-start(bf16[8192]{0:T(1024)(128)(2,1)} %param.11) | copy-start | bytes 49156
  2.3 7.8 %copy-start.6 = (s32[96]{0:T(128)}, s32[96]{0:T(128)S(1)}, u32[]{:S(2)}) copy-start(s32[96]{0:T(128)S(1)} %multiply_add_fusion) | copy-start | bytes 1156
  12.2 39.5 %all-to-all-start = ((bf16[32,13,1024]{2,1,0:T(8,128)(2,1)}), bf16[32,13,1024]{2,1,0:T(8,128)(2,1)S(1)}, u32[]{:S(2)}, u32[]{:S(2)}) async-start(bf16[32,13,1024]{2,1,0:T(8,128)(2,1)} %fusion.38), calls=%async_computation | async-start | bytes 2097152 | tf_op jit(solution)/shard_map/all_to_all | solution.py:158
  35.0 6.3 %copy-start.1 = (bf16[256,8192]{1,0:T(8,128)(2,1)S(1)}, bf16[256,8192]{1,0:T(8,128)(2,1)}, u32[]{:S(2)}) copy-start(bf16[256,8192]{1,0:T(8,128)(2,1)} %copy.81) | copy-start | bytes 12582916
  52.4 16.6 %copy-start.4 = (bf16[4,2,64,128]{3,2,1,0:T(8,128)(2,1)S(1)}, bf16[4,2,64,128]{3,2,1,0:T(8,128)(2,1)}, u32[]{:S(2)}) copy-start(bf16[4,2,64,128]{3,2,1,0:T(8,128)(2,1)} %param.14) | copy-start | bytes 393220
  54.4 22.5 %copy-start.3 = (bf16[96,2,1024]{2,1,0:T(2,128)(2,1)S(1)}, bf16[96,2,1024]{2,1,0:T(2,128)(2,1)}, u32[]{:S(2)}) copy-start(bf16[96,2,1024]{2,1,0:T(2,128)(2,1)} %param.16) | copy-start | bytes 1179652
  54.4 22.7 %copy-start.8 = (s32[96]{0:T(128)S(1)}, s32[96]{0:T(128)}, u32[]{:S(2)}) copy-start(s32[96]{0:T(128)} %param.19) | copy-start | bytes 1156
  54.4 1.5 %collective-permute-start = (f32[192,2,128]{2,0,1:T(8,128)S(1)}, f32[192,2,128]{2,0,1:T(8,128)S(1)}, u32[]{:S(2)}, u32[]{:S(2)}) collective-permute-start(f32[192,2,128]{2,0,1:T(8,128)S(1)} %fusion.26), channel_id=1, source_target_pairs={{0,1},{1,0},{2,3},{3,2},{4,5},{5,4},{6,7},{7,6},{8,9},{9,8},{10,11... | collective-permute-start | bytes 589832 | tf_op jit(solution)/shard_map/ppermute | solution.py:86
  56.0 7.9 %collective-permute-start.2 = (f32[192,2,128]{2,0,1:T(8,128)S(1)}, f32[192,2,128]{2,0,1:T(8,128)S(1)}, u32[]{:S(2)}, u32[]{:S(2)}) collective-permute-start(f32[192,2,128]{2,0,1:T(8,128)S(1)} %add.73), channel_id=1, source_target_pairs={{0,2},{1,3},{2,4},{3,5},{4,6},{5,7},{6,0},{7,1},{8,10},{9,11},{10,... | collective-permute-start | bytes 589832 | tf_op jit(solution)/shard_map/ppermute | solution.py:88
  56.6 12.2 %collective-permute-start.3 = (f32[192,2,128]{2,0,1:T(8,128)S(1)}, f32[192,2,128]{2,0,1:T(8,128)S(1)}, u32[]{:S(2)}, u32[]{:S(2)}) collective-permute-start(f32[192,2,128]{2,0,1:T(8,128)S(1)} %add.73), channel_id=1, source_target_pairs={{0,6},{1,7},{2,0},{3,1},{4,2},{5,3},{6,4},{7,5},{8,14},{9,15},{10,... | collective-permute-start | bytes 589832 | tf_op jit(solution)/shard_map/ppermute | solution.py:88
  58.1 10.7 %collective-permute-start.1 = (f32[192,2,128]{2,0,1:T(8,128)S(1)}, f32[192,2,128]{2,0,1:T(8,128)S(1)}, u32[]{:S(2)}, u32[]{:S(2)}) collective-permute-start(f32[192,2,128]{2,0,1:T(8,128)S(1)} %add.73), channel_id=1, source_target_pairs={{0,4},{1,5},{2,6},{3,7},{4,0},{5,1},{6,2},{7,3},{8,12},{9,13},{10,... | collective-permute-start | bytes 589832 | tf_op jit(solution)/shard_map/ppermute | solution.py:88
  70.6 20.1 %copy-start.7 = (s32[96]{0:T(128)S(1)}, s32[96]{0:T(128)}, u32[]{:S(2)}) copy-start(s32[96]{0:T(128)} %copy-done.6) | copy-start | bytes 1156
  70.6 19.8 %all-to-all-start.1 = ((f32[32,24,128]{2,1,0:T(8,128)}), f32[32,24,128]{2,1,0:T(8,128)S(1)}, u32[]{:S(2)}, u32[]{:S(2)}) async-start(f32[32,24,128]{2,1,0:T(8,128)} %bitcast.19), calls=%async_computation.1 | async-start | bytes 786432 | tf_op jit(solution)/shard_map/all_to_all | solution.py:189
  77.3 18.2 %copy-start.9 = (pred[2,2]{1,0:T(4,128)(4,1)S(1)}, pred[2,2]{1,0:T(4,128)(4,1)}, u32[]{:S(2)}) copy-start(pred[2,2]{1,0:T(4,128)(4,1)} %iota_compare_fusion.7) | copy-start | bytes 16
  90.7 6.6 %copy-start.2 = (f32[96,2,8]{2,1,0:T(2,128)S(1)}, f32[96,2,8]{2,1,0:T(2,128)}, u32[]{:S(2)}) copy-start(f32[96,2,8]{2,1,0:T(2,128)} %get-tuple-element.26) | copy-start | bytes 18436

commit v13 on v10

--- a/solution.py
+++ b/solution.py
@@ -51,8 +51,17 @@
     )
     slot_live = jnp.arange(context, dtype=jnp.int32)[None, :] < cached_length[:, None]
     cache_scores = jnp.where(slot_live[:, None, None, None, :], cache_scores, -1e30)
+    every_fresh = jnp.einsum(
+        "rthgd,ushd->rthgus", query_vecs, fresh_vecs, preferred_element_type=jnp.float32
+    )
+    own_request = (
+        jnp.arange(row_total, dtype=jnp.int32)[:, None]
+        == jnp.arange(row_total, dtype=jnp.int32)[None, :]
+    )
     fresh_scores = (
-        jnp.einsum("rthgd,rshd->rthgs", query_vecs, fresh_vecs, preferred_element_type=jnp.float32)
+        jnp.sum(
+            jnp.where(own_request[:, None, None, None, :, None], every_fresh, 0.0), axis=4
+        )
         * score_scale
     )
     causal = (

time: 100 us -> 104 us (1.040)
  other arithmetic: 18.8 us -> 22.1 us
  matrix products: 14.1 us -> 11.9 us
  local copies, waits for them, and re-layouts: 18.2 us -> 19.7 us
  waiting for transfers between devices: 25.8 us -> 27.2 us
    all_to_all x1, waiting for transfers between devices: 9.24 us -> 12.4 us  [body(): delta_recv = lax.all_to_all(delta_send, 'adapter', 0, 0, tiled=True)]
    dot_general x1, matrix products: 3.11 us -> 1.08 us  [attend(): jnp.einsum('rthgd,rjhd->rthgj', query_vecs, cache_vecs, preferred_element...]
    ppermute x3, waiting for transfers between devices: 9.22 us -> 7.24 us  [butterfly_sum(): lax.ppermute(value, axis_name, [(i, (i + 2 * k) % member_count) for i in...]
    dot_general x1, matrix products: 2.52 us -> 1.19 us  [attend(): jnp.einsum('rthgd,ushd->rthgus', query_vecs, fresh_vecs, preferred_elemen...]
    unnamed x22 -> x30, local copies, waits for them, and re-layouts: 6.26 us -> 6.27 us
  transfers between devices with their start and end apart: 6 -> 6, of which waited for: 5 -> 5; matrix products, arithmetic and copies ran while one was open for 27% -> 25% of each run, Pallas kernels for 0% -> 0%
where the time goes in v13:
time: 104 us; the launch traced here: 103 us
  waiting for transfers between devices  27.2 us (26%)
  other arithmetic  22.1 us (21%)
  starting transfers between devices  21.1 us (20%)
  local copies, waits for them, and re-layouts  19.7 us (19%)
  matrix products  11.9 us (11%)
  between operations  1.1 us (1%)
    all_to_all x1, waiting for transfers between devices, body(): delta_recv = lax.all_to_all(delta_send, 'adapter', 0, 0, tiled=True)  12.4 us
    all_to_all x1, starting transfers between devices, body(): recv = lax.all_to_all(send, 'adapter', 0, 0, tiled=True)  11.7 us
    ppermute x3, waiting for transfers between devices, butterfly_sum(): lax.ppermute(value, axis_name, [(i, (i + 2 * k) % member_count) for i in...  7.24 us
    dot_general x1, local copies, waits for them, and re-layouts, body(): jnp.dot(normed_input.reshape(row_count * token_count, model_width), key_v...  6.43 us
    convert_element_type x1, other arithmetic, body(): (values * row_scale * input_norm_gain.astype(jnp.float32)).astype(jnp.bfl...  6.3 us
    unnamed x30, local copies, waits for them, and re-layouts  6.27 us
    all_to_all x1, waiting for transfers between devices, body(): recv = lax.all_to_all(send, 'adapter', 0, 0, tiled=True)  6.24 us
    all_to_all x1, starting transfers between devices, body(): delta_recv = lax.all_to_all(delta_send, 'adapter', 0, 0, tiled=True)  5.58 us
  transfers between devices with their start and end apart: 6, of which 5 were waited for; matrix products, arithmetic and copies ran while one was open for 25% of the time, Pallas kernels for 0%

profile of v13, /device:TPU:6, one launch (start us, length us, event | category | flops | bytes accessed | tf_op | source)
XLA Modules:
  0.0 103.1 jit_solution(12869896382140885900)
XLA Ops:
  0.7 5.3 %fusion = f32[96,2]{1,0:T(8,128)S(1)} fusion(bf16[96,2,8192]{2,1,0:T(2,128)(2,1)} %param.10), kind=kLoop, calls=%fused_computation.3 | loop fusion | flops 4718400 | bytes 3146496 | tf_op jit(solution)/shard_map/reduce_sum | solution.py:126
  6.1 0.2 convert_reduce_fusion
  6.2 0.6 compare_and_fusion
  6.8 0.1 fusion.47
  7.2 1.5 %multiply_convert_fusion = bf16[96,2,1024]{2,1,0:T(2,128)(2,1)S(1)} fusion(f32[1024]{0:T(1024)S(1)} %dynamic-slice_convert_fusion, f32[96,2]{1,0:T(8,128)S(1)} %add_rsqrt_fusion, bf16[96,2,8192]{2,1,0:T(2,128)(2,1)} %param.10, s32[]{:T(128)S(6)} %select_n.45), kind=kLoop, calls=%fused_computation.36 | loop fusion | flops 786432 | bytes 791300 | tf_op jit(solution)/shard_map/convert_element_type | solution.py:152
  8.7 0.4 convolution_convert_fusion
  9.1 0.4 reshape.284
  9.5 1.2 %fusion.37 = bf16[32,13,1024]{2,1,0:T(8,128)(2,1)} fusion(bf16[32,1,6]{2,1,0:T(2,128)(2,1)S(1)} %reshape.316, bf16[32,12,1024]{2,1,0:T(8,128)(2,1)S(1)} %reshape.284), kind=kLoop, calls=%fused_computation.31 | loop fusion | flops 2555904 | bytes 1638784 | tf_op jit(solution)/shard_map/concatenate | solution.py:166
  10.7 11.7 %all-to-all-start = ((bf16[32,13,1024]{2,1,0:T(8,128)(2,1)}), bf16[32,13,1024]{2,1,0:T(8,128)(2,1)S(1)}, u32[]{:S(2)}, u32[]{:S(2)}) async-start(bf16[32,13,1024]{2,1,0:T(8,128)(2,1)} %fusion.37), calls=%async_computation | async-start | bytes 2097152 | tf_op jit(solution)/shard_map/all_to_all | solution.py:167
  22.4 4.7 %copy.184 = bf16[1024,8,2,128]{3,1,2,0:T(8,128)(2,1)} copy(bf16[1024,8,2,128]{3,2,1,0:T(2,128)(2,1)} %bitcast.159) | data formatting | bytes 8388608
  27.1 6.4 %copy.131 = bf16[256,8192]{1,0:T(8,128)(2,1)} copy(bf16[256,8192]{0,1:T(8,128)(2,1)} %bitcast.157) | data formatting | bytes 8388608 | tf_op jit(solution)/shard_map/dot_general | solution.py:129
  33.5 0.3 reshape.289
  33.8 6.3 %fusion.3 = bf16[96,2,8192,1]{2,1,0,3:T(2,128)(2,1)S(1)} fusion(bf16[96,2,8192]{2,1,0:T(2,128)(2,1)} %param.10, f32[8192]{0:T(1024)S(1)} %convert_element_type.103, f32[96,2]{1,0:T(8,128)S(1)} %copy-done.4), kind=kLoop, calls=%fused_computation.7 | loop fusion | flops 6291456 | bytes 6324992 | tf_op jit(solution)/shard_map/convert_element_type | solution.py:128
  40.1 3.9 %fusion.4 = f32[96,2,2,128]{3,0,2,1:T(8,128)S(1)} fusion(bf16[2,128,8192,1]{2,1,0,3:T(8,128)(2,1)S(1)} %bitcast.160, bf16[96,2,8192,1]{2,1,0,3:T(2,128)(2,1)S(1)} %fusion.3), kind=kOutput, calls=%fused_computation.8 | convolution fusion | flops 805306368 | bytes 7536640 | tf_op jit(solution)/shard_map/dot_general | solution.py:129
  44.0 6.2 %all-to-all-done = bf16[32,13,1024]{2,1,0:T(8,128)(2,1)S(1)} async-done(((bf16[32,13,1024]{2,1,0:T(8,128)(2,1)}), bf16[32,13,1024]{2,1,0:T(8,128)(2,1)S(1)}, u32[]{:S(2)}, u32[]{:S(2)}) %all-to-all-start) | async-done | bytes 852000 | tf_op jit(solution)/shard_map/all_to_all | solution.py:167
  50.4 1.5 %reshape.286 = bf16[192,2,1024]{2,1,0:T(2,128)(2,1)} reshape(bf16[32,12,1024]{2,1,0:T(8,128)(2,1)S(1)} %bitcast.158) | data formatting | bytes 1572864 | tf_op jit(solution)/shard_map/reshape | solution.py:169
  51.9 2.2 %fusion.27 = f32[192,2,128]{2,0,1:T(8,128)S(1)} fusion(bf16[4,1024,128]{2,1,0:T(8,128)(2,1)} %param.13, bf16[192,2,1024,1]{2,1,0,3:T(2,128)(2,1)} %bitcast.163, f32[192,4]{0,1:T(4,128)S(1)} %get-tuple-element.28), kind=kOutput, calls=%fused_computation.25 | convolution fusion | flops 402997248 | bytes 2034688 | tf_op jit(solution)/shard_map/euz,nzs->euns/dot_general | solution.py:175
  54.3 1.3 %collective-permute-done = f32[192,2,128]{2,0,1:T(8,128)S(1)} collective-permute-done((f32[192,2,128]{2,0,1:T(8,128)S(1)}, f32[192,2,128]{2,0,1:T(8,128)S(1)}, u32[]{:S(2)}, u32[]{:S(2)}) %collective-permute-start) | collective-permute-done | bytes 196640 | tf_op jit(solution)/shard_map/ppermute | solution.py:95
  55.7 0.8 collective-permute-start.2
  56.4 1.5 %collective-permute-start.3 = (f32[192,2,128]{2,0,1:T(8,128)S(1)}, f32[192,2,128]{2,0,1:T(8,128)}, u32[]{:S(2)}, u32[]{:S(2)}) collective-permute-start(f32[192,2,128]{2,0,1:T(8,128)S(1)} %add.83), channel_id=1, source_target_pairs={{0,6},{1,7},{2,0},{3,1},{4,2},{5,3},{6,4},{7,5},{8,14},{9,15},{10,... | collective-permute-start | bytes 589832 | tf_op jit(solution)/shard_map/ppermute | solution.py:97
  58.0 1.4 %collective-permute-start.1 = (f32[192,2,128]{2,0,1:T(8,128)S(1)}, f32[192,2,128]{2,0,1:T(8,128)}, u32[]{:S(2)}, u32[]{:S(2)}) collective-permute-start(f32[192,2,128]{2,0,1:T(8,128)S(1)} %add.83), channel_id=1, source_target_pairs={{0,4},{1,5},{2,6},{3,7},{4,0},{5,1},{6,2},{7,3},{8,12},{9,13},{10,... | collective-permute-start | bytes 589832 | tf_op jit(solution)/shard_map/ppermute | solution.py:97
  59.4 1.1 %fusion.79 = (f32[96,2,8]{2,1,0:T(2,128)S(1)}, f32[96,2,1,8,64]{4,3,1,0,2:T(8,128)S(1)}) fusion(bf16[96,2,8,128]{3,2,1,0:T(8,128)(2,1)S(1)} %reshape.289, bf16[96,64,128]{2,1,0:T(8,128)(2,1)S(1)} %copy-done.2, pred[96,64]{1,0:T(8,128)(4,1)S(1)} %iota_compare_fusion.5), kind=kOutput, calls=%fused_computation.109 | convolution fusion | flops 25459200 | bytes 2371584 | tf_op jit(solution)/shard_map/rthgd,rjhd->rthgj/dot_general | solution.py:49
  60.5 0.8 copy.140
  61.4 2.3 %collective-permute-done.2 = f32[192,2,128]{2,0,1:T(8,128)S(1)} collective-permute-done((f32[192,2,128]{2,0,1:T(8,128)S(1)}, f32[192,2,128]{2,0,1:T(8,128)S(1)}, u32[]{:S(2)}, u32[]{:S(2)}) %collective-permute-start.2) | collective-permute-done | bytes 196640 | tf_op jit(solution)/shard_map/ppermute | solution.py:97
  63.7 4.9 %collective-permute-done.3 = f32[192,2,128]{2,0,1:T(8,128)} collective-permute-done((f32[192,2,128]{2,0,1:T(8,128)S(1)}, f32[192,2,128]{2,0,1:T(8,128)}, u32[]{:S(2)}, u32[]{:S(2)}) %collective-permute-start.3) | collective-permute-done | bytes 196640 | tf_op jit(solution)/shard_map/ppermute | solution.py:97
  68.6 1.1 %add_convert_fusion = bf16[192,2,128]{2,0,1:T(8,128)(2,1)S(1)} fusion(f32[192,2,128]{2,0,1:T(8,128)S(1)} %collective-permute-done.2, f32[192,2,128]{2,0,1:T(8,128)} %collective-permute-done.3, f32[192,2,128]{2,0,1:T(8,128)S(1)} %add.83, f32[192,2,128]{2,0,1:T(8,128)} %collective-permute-done.1), kind=kLoop, calls=%fused_computation.47 | loop fusion | flops 196608 | bytes 884736 | tf_op jit(solution)/shard_map/convert_element_type | solution.py:179
  69.9 1.1 %convolution_bitcast_fusion = f32[192,2,1,128]{3,0,1,2:T(8,128)S(1)} fusion(bf16[192,2,4,128]{0,3,2,1:T(8,128)(2,1)S(1)} %broadcast_multiply_fusion, bf16[4,2,64,128]{3,2,1,0:T(8,128)(2,1)} %param.14), kind=kOutput, calls=%fused_computation.29 | convolution fusion | flops 25165824 | bytes 524288 | tf_op jit(solution)/shard_map/gled,edb->glb/dot_general | solution.py:189
  71.0 1.1 %convolution_bitcast_fusion.1 = f32[192,2,1,128]{3,0,1,2:T(8,128)S(1)} fusion(bf16[192,2,4,128]{0,3,2,1:T(8,128)(2,1)S(1)} %broadcast_multiply_fusion, bf16[4,2,64,128]{3,2,1,0:T(8,128)(2,1)} %param.14), kind=kOutput, calls=%fused_computation.30 | convolution fusion | flops 25165824 | bytes 524288 | tf_op jit(solution)/shard_map/gled,edb->glb/dot_general | solution.py:183
  72.1 1.1 %copy.138 = f32[192,2,2,128]{3,2,1,0:T(2,128)} copy(f32[192,2,2,128]{3,0,1,2:T(8,128)S(1)} %pad_maximum_fusion) | data formatting | bytes 786432 | tf_op jit(solution)/shard_map/stack | solution.py:195
  73.2 5.6 %all-to-all-start.1 = ((f32[32,24,128]{2,1,0:T(8,128)}), f32[32,24,128]{2,1,0:T(8,128)S(1)}, u32[]{:S(2)}, u32[]{:S(2)}) async-start(f32[32,24,128]{2,1,0:T(8,128)} %bitcast.18), calls=%async_computation.1 | async-start | bytes 786432 | tf_op jit(solution)/shard_map/all_to_all | solution.py:197
  78.7 0.6 iota_compare_fusion.8
  79.3 0.6 pad_clamp_fusion
  79.9 0.6 iota_compare_fusion.4
  80.5 12.4 %all-to-all-done.1 = f32[32,24,128]{2,1,0:T(8,128)S(1)} async-done(((f32[32,24,128]{2,1,0:T(8,128)}), f32[32,24,128]{2,1,0:T(8,128)S(1)}, u32[]{:S(2)}, u32[]{:S(2)}) %all-to-all-start.1) | async-done | bytes 393248 | tf_op jit(solution)/shard_map/all_to_all | solution.py:197
  93.0 0.8 gather_fusion
  94.1 1.0 select_add_fusion
  95.1 0.3 fusion.88
  95.4 0.3 fusion.53
  95.8 0.3 fusion.87
  96.1 0.3 fusion.86
  96.4 1.2 %fusion.9 = f32[96,2,8,2]{0,2,1,3:T(8,128)S(1)} fusion(pred[96,96]{0,1:T(8,128)(4,1)} %iota_compare_fusion.4, bf16[96,2,8,128]{3,2,1,0:T(8,128)(2,1)S(1)} %reshape.289, bf16[96,2,64]{0,2,1:T(8,128)(2,1)S(1)} %fusion.87, bf16[96,2,64]{0,2,1:T(8,128)(2,1)S(1)} %fusion.86), kind=kOutput, calls=%fused_computation.16 | convolution fusion | flops 76182528 | bytes 463872 | tf_op jit(solution)/shard_map/rthgd,ushd->rthgus/dot_general | solution.py:54
  97.6 0.7 fusion.70
  98.6 0.6 fusion.40
  99.6 0.7 copy.153
  100.3 0.7 copy.154
  101.3 0.3 fusion.80
  101.6 0.6 fusion.34
  102.2 0.8 convert_element_type.126
  (61 shorter events, 2.1 us)
Async XLA Ops:
  0.6 101.0 %copy-start = (bf16[96,64,128]{2,1,0:T(8,128)(2,1)S(1)}, bf16[96,64,128]{2,1,0:T(8,128)(2,1)}, u32[]{:S(2)}) copy-start(bf16[96,64,128]{2,1,0:T(8,128)(2,1)} %param.18) | copy-start | bytes 4718596
  0.6 5.4 %copy-start.12 = (s32[96]{0:T(128)S(1)}, s32[96]{0:T(128)}, u32[]{:S(2)}) copy-start(s32[96]{0:T(128)} %param.15) | copy-start | bytes 1156
  0.7 6.5 %copy-start.6 = (bf16[8192]{0:T(1024)(128)(2,1)S(1)}, bf16[8192]{0:T(1024)(128)(2,1)}, u32[]{:S(2)}) copy-start(bf16[8192]{0:T(1024)(128)(2,1)} %param.11) | copy-start | bytes 49156
  6.0 2.7 %copy-start.3 = (f32[96,2]{1,0:T(8,128)}, f32[96,2]{1,0:T(8,128)S(1)}, u32[]{:S(2)}) copy-start(f32[96,2]{1,0:T(8,128)S(1)} %add_rsqrt_fusion) | copy-start | bytes 2308
  6.8 1.9 %copy-start.8 = (s32[96]{0:T(128)}, s32[96]{0:T(128)S(1)}, u32[]{:S(2)}) copy-start(s32[96]{0:T(128)S(1)} %get-tuple-element.25) | copy-start | bytes 1156
  10.7 39.5 %all-to-all-start = ((bf16[32,13,1024]{2,1,0:T(8,128)(2,1)}), bf16[32,13,1024]{2,1,0:T(8,128)(2,1)S(1)}, u32[]{:S(2)}, u32[]{:S(2)}) async-start(bf16[32,13,1024]{2,1,0:T(8,128)(2,1)} %fusion.37), calls=%async_computation | async-start | bytes 2097152 | tf_op jit(solution)/shard_map/all_to_all | solution.py:167
  27.1 6.4 %copy-start.5 = (bf16[96,2,1024]{2,1,0:T(2,128)(2,1)S(1)}, bf16[96,2,1024]{2,1,0:T(2,128)(2,1)}, u32[]{:S(2)}) copy-start(bf16[96,2,1024]{2,1,0:T(2,128)(2,1)} %param.16) | copy-start | bytes 1179652
  27.1 6.7 %copy-start.4 = (f32[96,2]{1,0:T(8,128)S(1)}, f32[96,2]{1,0:T(8,128)}, u32[]{:S(2)}) copy-start(f32[96,2]{1,0:T(8,128)} %copy-done.3) | copy-start | bytes 2308
  33.8 6.3 %copy-start.1 = (bf16[256,8192]{1,0:T(8,128)(2,1)S(1)}, bf16[256,8192]{1,0:T(8,128)(2,1)}, u32[]{:S(2)}) copy-start(bf16[256,8192]{1,0:T(8,128)(2,1)} %copy.131) | copy-start | bytes 12582916
  44.0 10.2 %copy-start.10 = (s32[96]{0:T(128)S(1)}, s32[96]{0:T(128)}, u32[]{:S(2)}) copy-start(s32[96]{0:T(128)} %param.19) | copy-start | bytes 1156
  51.9 7.5 %copy-start.2 = (bf16[96,64,128]{2,1,0:T(8,128)(2,1)S(1)}, bf16[96,64,128]{2,1,0:T(8,128)(2,1)}, u32[]{:S(2)}) copy-start(bf16[96,64,128]{2,1,0:T(8,128)(2,1)} %param.17) | copy-start | bytes 4718596
  54.1 1.5 %collective-permute-start = (f32[192,2,128]{2,0,1:T(8,128)S(1)}, f32[192,2,128]{2,0,1:T(8,128)S(1)}, u32[]{:S(2)}, u32[]{:S(2)}) collective-permute-start(f32[192,2,128]{2,0,1:T(8,128)S(1)} %fusion.27), channel_id=1, source_target_pairs={{0,1},{1,0},{2,3},{3,2},{4,5},{5,4},{6,7},{7,6},{8,9},{9,8},{10,11... | collective-permute-start | bytes 589832 | tf_op jit(solution)/shard_map/ppermute | solution.py:95
  55.7 8.1 %collective-permute-start.2 = (f32[192,2,128]{2,0,1:T(8,128)S(1)}, f32[192,2,128]{2,0,1:T(8,128)S(1)}, u32[]{:S(2)}, u32[]{:S(2)}) collective-permute-start(f32[192,2,128]{2,0,1:T(8,128)S(1)} %add.83), channel_id=1, source_target_pairs={{0,2},{1,3},{2,4},{3,5},{4,6},{5,7},{6,0},{7,1},{8,10},{9,11},{10,... | collective-permute-start | bytes 589832 | tf_op jit(solution)/shard_map/ppermute | solution.py:97
  56.4 12.2 %collective-permute-start.3 = (f32[192,2,128]{2,0,1:T(8,128)S(1)}, f32[192,2,128]{2,0,1:T(8,128)}, u32[]{:S(2)}, u32[]{:S(2)}) collective-permute-start(f32[192,2,128]{2,0,1:T(8,128)S(1)} %add.83), channel_id=1, source_target_pairs={{0,6},{1,7},{2,0},{3,1},{4,2},{5,3},{6,4},{7,5},{8,14},{9,15},{10,... | collective-permute-start | bytes 589832 | tf_op jit(solution)/shard_map/ppermute | solution.py:97
  58.0 10.6 %collective-permute-start.1 = (f32[192,2,128]{2,0,1:T(8,128)S(1)}, f32[192,2,128]{2,0,1:T(8,128)}, u32[]{:S(2)}, u32[]{:S(2)}) collective-permute-start(f32[192,2,128]{2,0,1:T(8,128)S(1)} %add.83), channel_id=1, source_target_pairs={{0,4},{1,5},{2,6},{3,7},{4,0},{5,1},{6,2},{7,3},{8,12},{9,13},{10,... | collective-permute-start | bytes 589832 | tf_op jit(solution)/shard_map/ppermute | solution.py:97
  60.5 18.8 %copy-start.9 = (s32[96]{0:T(128)S(1)}, s32[96]{0:T(128)}, u32[]{:S(2)}) copy-start(s32[96]{0:T(128)} %copy-done.8) | copy-start | bytes 1156
  60.5 20.0 %copy-start.11 = (s32[96]{0:T(128)S(1)}, s32[96]{0:T(128)}, u32[]{:S(2)}) copy-start(s32[96]{0:T(128)} %param.19) | copy-start | bytes 1156
  73.2 19.8 %all-to-all-start.1 = ((f32[32,24,128]{2,1,0:T(8,128)}), f32[32,24,128]{2,1,0:T(8,128)S(1)}, u32[]{:S(2)}, u32[]{:S(2)}) async-start(f32[32,24,128]{2,1,0:T(8,128)} %bitcast.18), calls=%async_computation.1 | async-start | bytes 786432 | tf_op jit(solution)/shard_map/all_to_all | solution.py:197
  93.8 4.7 %copy-start.7 = (pred[2,2]{0,1:T(4,128)(4,1)S(1)}, pred[2,2]{0,1:T(4,128)(4,1)}, u32[]{:S(2)}) copy-start(pred[2,2]{0,1:T(4,128)(4,1)} %iota_compare_fusion.8) | copy-start | bytes 16

commit v14 on v10

--- a/solution.py
+++ b/solution.py
@@ -157,28 +157,30 @@
     send = jnp.concatenate([packed, id_row], axis=1)
     recv = lax.all_to_all(send, "adapter", 0, 0, tiled=True)
 
-    got_rows = recv[:, : cap * token_count].reshape(slot_total, token_count, feature_total)
+    got_rows = recv[:, : cap * token_count]
     got_adapter = recv[:, cap * token_count, :cap].reshape(slot_total).astype(jnp.int32)
     selector = (
         got_adapter[:, None] == jnp.arange(adapter_number, dtype=jnp.int32)[None, :]
     ).astype(jnp.float32)
+    row_selector = jnp.repeat(
+        selector.reshape(owner_count, cap, adapter_number), token_count, axis=1
+    )
 
     down_all = jnp.einsum(
-        "euz,nzs->euns", got_rows, adapter_down_weight, preferred_element_type=jnp.float32
-    )
-    partial_rank = jnp.sum(down_all * selector[:, None, :, None], axis=2)
+        "qjz,nzs->qjns", got_rows, adapter_down_weight, preferred_element_type=jnp.float32
+    )
+    partial_rank = jnp.sum(down_all * row_selector[..., None], axis=2)
     rank_hidden = butterfly_sum(partial_rank, "tensor").astype(jnp.bfloat16)
 
-    rank_selector = selector.astype(jnp.bfloat16)
-    masked = rank_hidden[:, :, None, :] * rank_selector[:, None, :, None]
+    masked = rank_hidden[:, :, None, :] * row_selector.astype(jnp.bfloat16)[..., None]
     key_part = jnp.einsum(
-        "gled,edb->glb",
+        "qjed,edb->qjb",
         masked[..., :rank_width],
         adapter_up_weight[:, 0],
         preferred_element_type=jnp.float32,
     )
     value_part = jnp.einsum(
-        "gled,edb->glb",
+        "qjed,edb->qjb",
         masked[..., rank_width:],
         adapter_up_weight[:, 1],
         preferred_element_type=jnp.float32,

time: 100 us -> 99.7 us (level)
    another operation x1, local copies, waits for them, and re-layouts: 1.05 us -> 0.03 us  [body(): delta_slots = jnp.stack([key_part, value_part], axis=2)]
    unnamed x22 -> x20, local copies, waits for them, and re-layouts: 6.26 us -> 6.25 us
  transfers between devices with their start and end apart: 6 -> 6, of which waited for: 5 -> 5; matrix products, arithmetic and copies ran while one was open for 27% -> 26% of each run, Pallas kernels for 0% -> 0%
where the time goes in v14:
time: 99.7 us; the launch traced here: 98.5 us
  waiting for transfers between devices  26.4 us (26%)
  starting transfers between devices  20.8 us (21%)
  other arithmetic  19.1 us (19%)
  local copies, waits for them, and re-layouts  17.4 us (17%)
  matrix products  13.6 us (14%)
  between operations  1.07 us (1%)
    all_to_all x1, starting transfers between devices, body(): recv = lax.all_to_all(send, 'adapter', 0, 0, tiled=True)  11.7 us
    all_to_all x1, waiting for transfers between devices, body(): delta_recv = lax.all_to_all(delta_send, 'adapter', 0, 0, tiled=True)  9.24 us
    ppermute x3, waiting for transfers between devices, butterfly_sum(): lax.ppermute(value, axis_name, [(i, (i + 2 * k) % member_count) for i in...  9.21 us
    all_to_all x1, waiting for transfers between devices, body(): recv = lax.all_to_all(send, 'adapter', 0, 0, tiled=True)  6.57 us
    dot_general x1, local copies, waits for them, and re-layouts, body(): jnp.dot(normed_input.reshape(row_count * token_count, model_width), key_v...  6.38 us
    convert_element_type x1, other arithmetic, body(): (values * row_scale * input_norm_gain.astype(jnp.float32)).astype(jnp.bfl...  6.29 us
    unnamed x20, local copies, waits for them, and re-layouts  6.25 us
    all_to_all x1, starting transfers between devices, body(): delta_recv = lax.all_to_all(delta_send, 'adapter', 0, 0, tiled=True)  5.58 us
  transfers between devices with their start and end apart: 6, of which 5 were waited for; matrix products, arithmetic and copies ran while one was open for 26% of the time, Pallas kernels for 0%

profile of v14, /device:TPU:6, one launch (start us, length us, event | category | flops | bytes accessed | tf_op | source)
XLA Modules:
  0.0 98.5 jit_solution(556889673257279599)
XLA Ops:
  0.7 5.3 %fusion = f32[96,2]{1,0:T(8,128)S(1)} fusion(bf16[96,2,8192]{2,1,0:T(2,128)(2,1)} %param.10), kind=kLoop, calls=%fused_computation.3 | loop fusion | flops 4718400 | bytes 3146496 | tf_op jit(solution)/shard_map/reduce_sum | solution.py:117
  6.0 0.2 convert_reduce_fusion
  6.3 0.1 fusion.49
  6.4 0.1 reshape.262
  6.6 1.5 %multiply_convert_fusion = bf16[96,2,1024]{2,1,0:T(2,128)(2,1)S(1)} fusion(f32[1024]{0:T(1024)S(1)} %dynamic-slice_convert_fusion, f32[96,2]{1,0:T(8,128)S(1)} %add_rsqrt_fusion, bf16[96,2,8192]{2,1,0:T(2,128)(2,1)} %param.10, s32[]{:T(128)S(6)} %select_n.31), kind=kLoop, calls=%fused_computation.37 | loop fusion | flops 786432 | bytes 791300 | tf_op jit(solution)/shard_map/convert_element_type | solution.py:143
  8.1 0.4 convolution_convert_fusion
  8.5 0.4 reshape.231
  8.9 1.2 %fusion.38 = bf16[32,13,1024]{2,1,0:T(8,128)(2,1)} fusion(bf16[32,1,6]{2,1,0:T(2,128)(2,1)S(1)} %reshape.262, bf16[32,12,1024]{2,1,0:T(8,128)(2,1)S(1)} %reshape.231), kind=kLoop, calls=%fused_computation.32 | loop fusion | flops 2555904 | bytes 1638784 | tf_op jit(solution)/shard_map/concatenate | solution.py:157
  10.1 11.7 %all-to-all-start = ((bf16[32,13,1024]{2,1,0:T(8,128)(2,1)}), bf16[32,13,1024]{2,1,0:T(8,128)(2,1)S(1)}, u32[]{:S(2)}, u32[]{:S(2)}) async-start(bf16[32,13,1024]{2,1,0:T(8,128)(2,1)} %fusion.38), calls=%async_computation | async-start | bytes 2097152 | tf_op jit(solution)/shard_map/all_to_all | solution.py:158
  21.8 4.7 %copy.127 = bf16[1024,8,2,128]{3,1,2,0:T(8,128)(2,1)} copy(bf16[1024,8,2,128]{3,2,1,0:T(2,128)(2,1)} %bitcast.163) | data formatting | bytes 8388608
  26.5 6.4 %copy.84 = bf16[256,8192]{1,0:T(8,128)(2,1)} copy(bf16[256,8192]{0,1:T(8,128)(2,1)} %bitcast.162) | data formatting | bytes 8388608 | tf_op jit(solution)/shard_map/dot_general | solution.py:120
  32.9 6.3 %fusion.3 = bf16[96,2,8192,1]{2,1,0,3:T(2,128)(2,1)S(1)} fusion(bf16[96,2,8192]{2,1,0:T(2,128)(2,1)} %param.10, f32[8192]{0:T(1024)S(1)} %convert_element_type.94, f32[96,2]{1,0:T(8,128)S(1)} %add_rsqrt_fusion), kind=kLoop, calls=%fused_computation.7 | loop fusion | flops 6291456 | bytes 6324992 | tf_op jit(solution)/shard_map/convert_element_type | solution.py:119
  39.2 3.9 %fusion.4 = f32[96,2,2,128]{3,0,2,1:T(8,128)S(1)} fusion(bf16[2,128,8192,1]{2,1,0,3:T(8,128)(2,1)S(1)} %bitcast.164, bf16[96,2,8192,1]{2,1,0,3:T(2,128)(2,1)S(1)} %fusion.3), kind=kOutput, calls=%fused_computation.8 | convolution fusion | flops 805306368 | bytes 7536640 | tf_op jit(solution)/shard_map/dot_general | solution.py:120
  43.1 6.6 %all-to-all-done = bf16[32,13,1024]{2,1,0:T(8,128)(2,1)S(1)} async-done(((bf16[32,13,1024]{2,1,0:T(8,128)(2,1)}), bf16[32,13,1024]{2,1,0:T(8,128)(2,1)S(1)}, u32[]{:S(2)}, u32[]{:S(2)}) %all-to-all-start) | async-done | bytes 852000 | tf_op jit(solution)/shard_map/all_to_all | solution.py:158
  49.8 1.9 %fusion.26 = f32[32,12,128]{2,0,1:T(8,128)S(1)} fusion(bf16[4,1024,128]{2,1,0:T(8,128)(2,1)} %param.13, bf16[32,12,1024]{2,1,0:T(8,128)(2,1)S(1)} %bitcast.168, f32[32,12,4]{0,2,1:T(4,128)S(1)} %bitcast.170), kind=kOutput, calls=%fused_computation.23 | convolution fusion | flops 402997248 | bytes 2037760 | tf_op jit(solution)/shard_map/qjz,nzs->qjns/dot_general | solution.py:169
  51.9 1.4 %collective-permute-done = f32[32,12,128]{2,0,1:T(8,128)S(1)} collective-permute-done((f32[32,12,128]{2,0,1:T(8,128)S(1)}, f32[32,12,128]{2,0,1:T(8,128)S(1)}, u32[]{:S(2)}, u32[]{:S(2)}) %collective-permute-start) | collective-permute-done | bytes 196640 | tf_op jit(solution)/shard_map/ppermute | solution.py:86
  53.3 0.6 collective-permute-start.2
  53.9 1.6 %collective-permute-start.3 = (f32[32,12,128]{2,0,1:T(8,128)S(1)}, f32[32,12,128]{2,0,1:T(8,128)S(1)}, u32[]{:S(2)}, u32[]{:S(2)}) collective-permute-start(f32[32,12,128]{2,0,1:T(8,128)S(1)} %add.83), channel_id=1, source_target_pairs={{0,6},{1,7},{2,0},{3,1},{4,2},{5,3},{6,4},{7,5},{8,14},{9,15},{10,... | collective-permute-start | bytes 589832 | tf_op jit(solution)/shard_map/ppermute | solution.py:88
  55.4 1.4 %collective-permute-start.1 = (f32[32,12,128]{2,0,1:T(8,128)S(1)}, f32[32,12,128]{2,0,1:T(8,128)S(1)}, u32[]{:S(2)}, u32[]{:S(2)}) collective-permute-start(f32[32,12,128]{2,0,1:T(8,128)S(1)} %add.83), channel_id=1, source_target_pairs={{0,4},{1,5},{2,6},{3,7},{4,0},{5,1},{6,2},{7,3},{8,12},{9,13},{10,... | collective-permute-start | bytes 589832 | tf_op jit(solution)/shard_map/ppermute | solution.py:88
  56.9 4.3 %collective-permute-done.2 = f32[32,12,128]{2,0,1:T(8,128)S(1)} collective-permute-done((f32[32,12,128]{2,0,1:T(8,128)S(1)}, f32[32,12,128]{2,0,1:T(8,128)S(1)}, u32[]{:S(2)}, u32[]{:S(2)}) %collective-permute-start.2) | collective-permute-done | bytes 196640 | tf_op jit(solution)/shard_map/ppermute | solution.py:88
  61.2 4.9 %collective-permute-done.3 = f32[32,12,128]{2,0,1:T(8,128)S(1)} collective-permute-done((f32[32,12,128]{2,0,1:T(8,128)S(1)}, f32[32,12,128]{2,0,1:T(8,128)S(1)}, u32[]{:S(2)}, u32[]{:S(2)}) %collective-permute-start.3) | collective-permute-done | bytes 196640 | tf_op jit(solution)/shard_map/ppermute | solution.py:88
  66.2 0.3 broadcast_multiply_fusion
  66.4 0.4 convolution_bitcast_fusion
  66.8 0.3 convolution_bitcast_fusion.1
  67.1 1.0 copy.92
  68.1 5.6 %all-to-all-start.1 = ((f32[32,24,128]{2,1,0:T(8,128)}), f32[32,24,128]{2,1,0:T(8,128)S(1)}, u32[]{:S(2)}, u32[]{:S(2)}) async-start(f32[32,24,128]{2,1,0:T(8,128)} %copy.92), calls=%async_computation.1 | async-start | bytes 786432 | tf_op jit(solution)/shard_map/all_to_all | solution.py:190
  73.7 0.5 iota_compare_fusion.7
  74.2 0.8 copy.94
  75.1 0.3 reshape.235
  75.4 3.1 %fusion.74 = (f32[96,2,8]{2,1,0:T(2,128)}, f32[96,2,1,8,64]{4,3,1,0,2:T(8,128)S(1)}) fusion(bf16[96,2,8,128]{3,2,1,0:T(8,128)(2,1)S(1)} %reshape.235, bf16[96,64,128]{2,1,0:T(8,128)(2,1)} %param.17, pred[96,64]{1,0:T(8,128)(4,1)S(1)} %iota_compare_fusion.4), kind=kOutput, calls=%fused_computation.104 | convolution fusion | flops 25459200 | bytes 2371584 | tf_op jit(solution)/shard_map/rthgd,rjhd->rthgj/dot_general | solution.py:49
  78.5 9.2 %all-to-all-done.1 = f32[32,24,128]{2,1,0:T(8,128)S(1)} async-done(((f32[32,24,128]{2,1,0:T(8,128)}), f32[32,24,128]{2,1,0:T(8,128)S(1)}, u32[]{:S(2)}, u32[]{:S(2)}) %all-to-all-start.1) | async-done | bytes 393248 | tf_op jit(solution)/shard_map/all_to_all | solution.py:190
  87.8 0.7 gather_fusion
  88.6 0.1 gather.7
  88.7 0.1 copy.93
  88.8 1.0 %select_add_fusion = f32[96,2,2,128]{0,3,1,2:T(8,128)S(1)} fusion(f32[96,2,2,128]{0,3,1,2:T(8,128)} %copy.94, f32[96,2,2,128]{0,3,1,2:T(8,128)S(1)} %copy.93, pred[96]{0:T(512)(128)(4,1)S(1)} %get-tuple-element.18), kind=kLoop, calls=%fused_computation.44 | loop fusion | flops 98304 | bytes 589920 | tf_op jit(solution)/shard_map/add | solution.py:196
  89.8 0.3 fusion.84
  90.2 0.3 fusion.55
  90.5 0.3 fusion.83
  90.8 0.3 fusion.82
  91.2 0.7 copy.101
  91.9 0.7 copy.102
  92.8 0.1 copy.108
  92.9 2.5 %fusion.75 = (f32[96,2,8]{2,1,0:T(2,128)S(1)}, f32[96,2,1,8,2]{3,4,1,0,2:T(2,128)S(1)}) fusion(bf16[96,2,128,1]{2,1,3,0:T(2,128)(2,1)S(1)} %copy.108, bf16[96,2,8,128]{3,2,1,0:T(8,128)(2,1)S(1)} %reshape.235, pred[2,2]{1,0:T(4,128)(4,1)} %iota_compare_fusion.7), kind=kOutput, calls=%fused_computation.105 | convolution fusion | flops 794112 | bytes 460804 | tf_op jit(solution)/shard_map/rthgd,rshd->rthgs/dot_general | solution.py:55
  95.5 0.6 fusion.40
  96.1 0.4 fusion.45
  96.6 0.4 fusion.46
  97.0 0.6 fusion.33
  97.6 0.8 convert_element_type.117
  (46 shorter events, 1.0 us)
Async XLA Ops:
  0.6 96.4 %copy-start = (bf16[96,64,128]{2,1,0:T(8,128)(2,1)S(1)}, bf16[96,64,128]{2,1,0:T(8,128)(2,1)}, u32[]{:S(2)}) copy-start(bf16[96,64,128]{2,1,0:T(8,128)(2,1)} %param.18) | copy-start | bytes 4718596
  0.6 5.4 %copy-start.6 = (s32[96]{0:T(128)S(1)}, s32[96]{0:T(128)}, u32[]{:S(2)}) copy-start(s32[96]{0:T(128)} %param.15) | copy-start | bytes 1156
  0.7 5.9 %copy-start.4 = (bf16[8192]{0:T(1024)(128)(2,1)S(1)}, bf16[8192]{0:T(1024)(128)(2,1)}, u32[]{:S(2)}) copy-start(bf16[8192]{0:T(1024)(128)(2,1)} %param.11) | copy-start | bytes 49156
  10.1 39.5 %all-to-all-start = ((bf16[32,13,1024]{2,1,0:T(8,128)(2,1)}), bf16[32,13,1024]{2,1,0:T(8,128)(2,1)S(1)}, u32[]{:S(2)}, u32[]{:S(2)}) async-start(bf16[32,13,1024]{2,1,0:T(8,128)(2,1)} %fusion.38), calls=%async_computation | async-start | bytes 2097152 | tf_op jit(solution)/shard_map/all_to_all | solution.py:158
  32.8 6.3 %copy-start.1 = (bf16[256,8192]{1,0:T(8,128)(2,1)S(1)}, bf16[256,8192]{1,0:T(8,128)(2,1)}, u32[]{:S(2)}) copy-start(bf16[256,8192]{1,0:T(8,128)(2,1)} %copy.84) | copy-start | bytes 12582916
  43.1 23.3 %copy-start.7 = (bf16[4,2,64,128]{3,2,1,0:T(8,128)(2,1)S(1)}, bf16[4,2,64,128]{3,2,1,0:T(8,128)(2,1)}, u32[]{:S(2)}) copy-start(bf16[4,2,64,128]{3,2,1,0:T(8,128)(2,1)} %param.14) | copy-start | bytes 393220
  51.8 1.5 %collective-permute-start = (f32[32,12,128]{2,0,1:T(8,128)S(1)}, f32[32,12,128]{2,0,1:T(8,128)S(1)}, u32[]{:S(2)}, u32[]{:S(2)}) collective-permute-start(f32[32,12,128]{2,0,1:T(8,128)S(1)} %fusion.26), channel_id=1, source_target_pairs={{0,1},{1,0},{2,3},{3,2},{4,5},{5,4},{6,7},{7,6},{8,9},{9,8},{10,11... | collective-permute-start | bytes 589832 | tf_op jit(solution)/shard_map/ppermute | solution.py:86
  53.3 7.9 %collective-permute-start.2 = (f32[32,12,128]{2,0,1:T(8,128)S(1)}, f32[32,12,128]{2,0,1:T(8,128)S(1)}, u32[]{:S(2)}, u32[]{:S(2)}) collective-permute-start(f32[32,12,128]{2,0,1:T(8,128)S(1)} %add.83), channel_id=1, source_target_pairs={{0,2},{1,3},{2,4},{3,5},{4,6},{5,7},{6,0},{7,1},{8,10},{9,11},{10,... | collective-permute-start | bytes 589832 | tf_op jit(solution)/shard_map/ppermute | solution.py:88
  53.9 12.2 %collective-permute-start.3 = (f32[32,12,128]{2,0,1:T(8,128)S(1)}, f32[32,12,128]{2,0,1:T(8,128)S(1)}, u32[]{:S(2)}, u32[]{:S(2)}) collective-permute-start(f32[32,12,128]{2,0,1:T(8,128)S(1)} %add.83), channel_id=1, source_target_pairs={{0,6},{1,7},{2,0},{3,1},{4,2},{5,3},{6,4},{7,5},{8,14},{9,15},{10,... | collective-permute-start | bytes 589832 | tf_op jit(solution)/shard_map/ppermute | solution.py:88
  55.4 10.7 %collective-permute-start.1 = (f32[32,12,128]{2,0,1:T(8,128)S(1)}, f32[32,12,128]{2,0,1:T(8,128)S(1)}, u32[]{:S(2)}, u32[]{:S(2)}) collective-permute-start(f32[32,12,128]{2,0,1:T(8,128)S(1)} %add.83), channel_id=1, source_target_pairs={{0,4},{1,5},{2,6},{3,7},{4,0},{5,1},{6,2},{7,3},{8,12},{9,13},{10,... | collective-permute-start | bytes 589832 | tf_op jit(solution)/shard_map/ppermute | solution.py:88
  56.8 18.2 %copy-start.3 = (bf16[96,2,1024]{2,1,0:T(2,128)(2,1)S(1)}, bf16[96,2,1024]{2,1,0:T(2,128)(2,1)}, u32[]{:S(2)}) copy-start(bf16[96,2,1024]{2,1,0:T(2,128)(2,1)} %param.16) | copy-start | bytes 1179652
  66.1 9.2 %copy-start.5 = (s32[96]{0:T(128)S(1)}, s32[96]{0:T(128)}, u32[]{:S(2)}) copy-start(s32[96]{0:T(128)} %param.19) | copy-start | bytes 1156
  68.1 19.7 %all-to-all-start.1 = ((f32[32,24,128]{2,1,0:T(8,128)}), f32[32,24,128]{2,1,0:T(8,128)S(1)}, u32[]{:S(2)}, u32[]{:S(2)}) async-start(f32[32,24,128]{2,1,0:T(8,128)} %copy.92), calls=%async_computation.1 | async-start | bytes 786432 | tf_op jit(solution)/shard_map/all_to_all | solution.py:190
  88.6 6.9 %copy-start.2 = (f32[96,2,8]{2,1,0:T(2,128)S(1)}, f32[96,2,8]{2,1,0:T(2,128)}, u32[]{:S(2)}) copy-start(f32[96,2,8]{2,1,0:T(2,128)} %get-tuple-element.22) | copy-start | bytes 18436
